TPU v7x, 32 devices: a whole 2x2x4 slice. The times are simulated.
32 devices in a mesh: groups: 2 (over x), tm: 16 (over z, y, core).
Axes of the slice: x: 2, y: 2, z: 4, core: 2. Of those that a mesh axis runs over, the one named last changes fastest.
Arguments:
- observed: float32 [32, 128], P(('groups', 'tm')), parts along dimension 0, may hold values from -6 to 6
- obs_masks: int32 [32, 128], P(('groups', 'tm')), parts along dimension 0, may hold values 0 or 1
- decay_rates: float32 [256], P('groups'), parts along dimension 0, may hold values from 0.05 to 0.5
- noise_var: float32 [256], P('groups'), parts along dimension 0, may hold values from 0.05 to 0.5
- spatial_cov: float32 [256, 128], P('groups'), parts along dimension 0, may hold values from -1 to 4, as said below
Outputs:
- smooth_mean: float32 [32, 256], P(('groups', 'tm')), parts along dimension 0
- smooth_cov: float32 [32, 256, 256], P(('groups', 'tm')), parts along dimension 0
There are 2 independent parts, one for each index of `groups`. A program takes and returns all parts, laid end to end along the dimension named above; each array names one. Nothing has to cross between parts.
Inputs may be any that keep to these rules, and one draw needn't show every extreme that they name: spatial_cov is symmetric, and each diagonal entry is positive and larger than the sum of the magnitudes of the other entries of its row.
All inputs are finite; a program needn't handle non-finite values. No bound on the sum of `obs_masks` on one device may be relied on, other than what follows from the above.
Results may differ from a plain program's by a relative error of at most 0.0003.
Values sent between devices are 32-bit elements; how exact they have to be, the bound alone decides.
No kernel may reach another device: no remote copies, remote signals or barrier semaphores. Data moves between devices by JAX's collectives and lax.ppermute only.
A program may use at most 128 MiB of HBM per device.

v0:
```python
import jax
import jax.numpy as jnp
from jax import lax
from jax.sharding import PartitionSpec as P

HIGHEST = lax.Precision.HIGHEST
JITTER = 0.001


def shifted_2(array, axis, by):
    devices = lax.axis_size(axis)
    pairs = [(i, i + by) for i in range(devices) if 0 <= i + by < devices]
    return lax.ppermute(array, axis, pairs)


def entering(value, axis, join, neutral):
    count, mine = (lax.axis_size(axis), lax.axis_index(axis))
    pieces = jax.tree.map(lambda part: lax.all_gather(part, axis), value)
    pieces = jax.tree.map(lambda part: part[::-1], pieces)
    mine = count - 1 - mine
    running = jax.tree.map(
        lambda part, zero: jnp.full_like(part, 0) + jnp.asarray(zero, part.dtype), value, neutral
    )

    def lap(position, running):
        longer = join(running, jax.tree.map(lambda part: part[position], pieces))
        return jax.tree.map(lambda new, old: jnp.where(position < mine, new, old), longer, running)

    return lax.fori_loop(0, count - 1, lap, running)


def matmul_hi(left, right):
    return jnp.matmul(left, right, precision=HIGHEST)


def swap_last(matrix):
    return jnp.swapaxes(matrix, -1, -2)


def apply_trans(transit, matrix):
    points = transit.shape[1]
    upper_half = matrix[..., :points, :]
    lower_half = matrix[..., points:, :]
    return jnp.concatenate(
        [
            transit[0][:, None] * upper_half + transit[1][:, None] * lower_half,
            transit[2][:, None] * upper_half + transit[3][:, None] * lower_half,
        ],
        axis=-2,
    )


def apply_trans_t(transit, matrix):
    points = transit.shape[1]
    upper_half = matrix[..., :points, :]
    lower_half = matrix[..., points:, :]
    return jnp.concatenate(
        [
            transit[0][:, None] * upper_half + transit[2][:, None] * lower_half,
            transit[1][:, None] * upper_half + transit[3][:, None] * lower_half,
        ],
        axis=-2,
    )


def spd_inverse(matrix):
    factor = jnp.linalg.cholesky(matrix)
    identity_mat = jnp.broadcast_to(jnp.eye(matrix.shape[-1], dtype=jnp.float32), matrix.shape)
    low_inverse = lax.linalg.triangular_solve(factor, identity_mat, left_side=True, lower=True)
    return matmul_hi(swap_last(low_inverse), low_inverse)


def build_model(decay_rates, spatial_cov):
    decay_one = jnp.exp(-decay_rates)
    transit = jnp.stack(
        [
            decay_one * (1.0 + decay_rates),
            decay_one * decay_rates,
            -decay_one * decay_rates,
            decay_one * (1.0 - decay_rates),
        ]
    )
    decay_two = jnp.exp(-2.0 * decay_rates)
    var_ff = 1.0 - decay_two * (1.0 + 2.0 * decay_rates + 2.0 * decay_rates * decay_rates)
    cov_fg = 2.0 * decay_rates * decay_rates * decay_two
    var_gg = 1.0 - decay_two * (1.0 - 2.0 * decay_rates + 2.0 * decay_rates * decay_rates)
    fac_ff = jnp.sqrt(var_ff)
    fac_gf = cov_fg / fac_ff
    fac_gg = jnp.sqrt(var_gg - fac_gf * fac_gf)

    def scaled(left, right):
        return left[:, None] * spatial_cov * right[None, :]

    zero_block = jnp.zeros_like(spatial_cov)
    process = jnp.block(
        [
            [scaled(fac_ff, fac_ff), scaled(fac_ff, fac_gf)],
            [scaled(fac_gf, fac_ff), scaled(fac_gf, fac_gf) + scaled(fac_gg, fac_gg)],
        ]
    )
    process = process + JITTER * jnp.eye(2 * spatial_cov.shape[0], dtype=jnp.float32)
    prior = jnp.block([[spatial_cov, zero_block], [zero_block, spatial_cov]])
    return (transit, process, prior)


def make_elements(observed, obs_masks, first_flag, model_parts, noise_var):
    transit, process, prior = model_parts
    width = 2 * observed.shape[-1]
    obs_prec = obs_masks.astype(jnp.float32) / noise_var
    prec_root = jnp.sqrt(jnp.concatenate([obs_prec, jnp.zeros_like(obs_prec)], axis=-1))
    obs_full = jnp.concatenate([observed, jnp.zeros_like(observed)], axis=-1)
    identity_mat = jnp.eye(width, dtype=jnp.float32)
    cov_pred = jnp.where(first_flag[:, None, None], prior, process)
    normal = identity_mat + prec_root[:, :, None] * cov_pred * prec_root[:, None, :]
    weight = prec_root[:, :, None] * spd_inverse(normal) * prec_root[:, None, :]
    cov_weight = matmul_hi(cov_pred, weight)
    cov_filt = cov_pred - matmul_hi(cov_weight, cov_pred)
    weight_obs = matmul_hi(weight, obs_full[..., None])
    mean_filt = matmul_hi(cov_pred, weight_obs)[..., 0]
    trans_a = swap_last(apply_trans_t(transit, swap_last(identity_mat - cov_weight)))
    half_info = apply_trans_t(transit, weight)
    info_j = apply_trans_t(transit, swap_last(half_info))
    info_eta = apply_trans_t(transit, weight_obs)[..., 0]
    keep_mask = 1.0 - first_flag.astype(jnp.float32)
    flags = jnp.ones(observed.shape[0], dtype=jnp.float32)
    return (
        trans_a * keep_mask[:, None, None],
        mean_filt,
        cov_filt,
        info_j * keep_mask[:, None, None],
        info_eta * keep_mask[:, None],
        flags,
    )


def cov_gain(cov_early, flag_early, info_later):
    identity_mat = jnp.eye(cov_early.shape[-1], dtype=jnp.float32)
    safe_cov = jnp.where(flag_early > 0, cov_early, identity_mat)
    factor = jnp.linalg.cholesky(safe_cov)
    middle = identity_mat + matmul_hi(swap_last(factor), matmul_hi(info_later, factor))
    return matmul_hi(matmul_hi(factor, spd_inverse(middle)), swap_last(factor))


def combine_full(earlier, later_el):
    trans_e, mean_e, cov_e, info_e, eta_e, flag_e = earlier
    trans_l, mean_l, cov_l, info_l, eta_l, flag_l = later_el
    identity_mat = jnp.eye(cov_e.shape[-1], dtype=jnp.float32)
    gain_cov = cov_gain(cov_e, flag_e, info_l)
    solve_x = identity_mat - matmul_hi(gain_cov, info_l)
    x_trans = matmul_hi(solve_x, trans_e)
    trans_new = matmul_hi(trans_l, x_trans)
    shifted = mean_e + matmul_hi(cov_e, eta_l)
    mean_new = matmul_hi(trans_l, matmul_hi(solve_x, shifted)) + mean_l
    cov_new = matmul_hi(matmul_hi(trans_l, gain_cov), swap_last(trans_l)) + cov_l
    eta_new = matmul_hi(swap_last(x_trans), eta_l - matmul_hi(info_l, mean_e)) + eta_e
    info_new = matmul_hi(swap_last(x_trans), matmul_hi(info_l, trans_e)) + info_e
    joined = (trans_new, mean_new, cov_new, info_new, eta_new, jnp.maximum(flag_e, flag_l))
    return jax.tree.map(
        lambda leaf_e, leaf_l, leaf_j: jnp.where(
            flag_l > 0, jnp.where(flag_e > 0, leaf_j, leaf_l), leaf_e
        ),
        earlier,
        later_el,
        joined,
    )


def combine_state(carry_in, element):
    mean_c, cov_c, flag_c = carry_in
    trans_l, mean_l, cov_l, info_l, eta_l, flag_l = element
    identity_mat = jnp.eye(cov_c.shape[-1], dtype=jnp.float32)
    gain_cov = cov_gain(cov_c, flag_c, info_l)
    solve_x = identity_mat - matmul_hi(gain_cov, info_l)
    shifted = mean_c + matmul_hi(cov_c, eta_l)
    mean_new = matmul_hi(trans_l, matmul_hi(solve_x, shifted)) + mean_l
    cov_new = matmul_hi(matmul_hi(trans_l, gain_cov), swap_last(trans_l)) + cov_l
    return (jnp.where(flag_c > 0, mean_new, mean_l), jnp.where(flag_c > 0, cov_new, cov_l))


def smoother_elements(means, covs, last_flag, transit, process):
    forward_cov = apply_trans(transit, covs)
    predicted = apply_trans(transit, swap_last(forward_cov)) + process
    factor = jnp.linalg.cholesky(predicted)
    half_solve = lax.linalg.triangular_solve(factor, forward_cov, left_side=True, lower=True)
    gain_t = lax.linalg.triangular_solve(
        factor, half_solve, left_side=True, lower=True, transpose_a=True
    )
    gains = swap_last(gain_t) * (1.0 - last_flag.astype(jnp.float32))[:, None, None]
    forward_mean = apply_trans(transit, means[..., None])
    shift_means = means - matmul_hi(gains, forward_mean)[..., 0]
    shift_covs = covs - matmul_hi(gains, forward_cov)
    return (gains, shift_means, shift_covs)


def smooth_join(lower_el, higher_el):
    gain_a, mean_a, cov_a = lower_el
    gain_b, mean_b, cov_b = higher_el
    return (
        matmul_hi(gain_a, gain_b),
        matmul_hi(gain_a, mean_b) + mean_a,
        matmul_hi(matmul_hi(gain_a, cov_b), swap_last(gain_a)) + cov_a,
    )


def reverse_join(earlier, later_el):
    return smooth_join(later_el, earlier)


def shards(observed, obs_masks, decay_rates, noise_var, spatial_cov):
    model_parts = build_model(decay_rates, spatial_cov)
    transit, process, prior = model_parts
    local_steps = observed.shape[0]
    width = 2 * observed.shape[1]
    position = lax.axis_index("tm")
    tm_count = lax.axis_size("tm")
    global_step = position * local_steps + jnp.arange(local_steps)
    elements = make_elements(observed, obs_masks, global_step == 0, model_parts, noise_var)
    first_el = jax.tree.map(lambda leaf: leaf[0], elements)
    rest_els = jax.tree.map(lambda leaf: leaf[1:], elements)

    def forward(running, element):
        joined = combine_full(running, element)
        return (joined, joined)

    _, tail_els = lax.scan(forward, first_el, rest_els)
    prefixes = jax.tree.map(
        lambda head_leaf, tail_leaf: jnp.concatenate([head_leaf[None], tail_leaf], axis=0),
        first_el,
        tail_els,
    )
    dev_total = jax.tree.map(lambda leaf: leaf[-1], prefixes)
    zero_vec = jnp.zeros((width,), jnp.float32)
    zero_mat = jnp.zeros((width, width), jnp.float32)
    one_flag = jnp.float32(1.0)
    start_state = (zero_vec, zero_mat, jnp.float32(0.0), dev_total[1], dev_total[2])

    def handoff_turn(turn_no, loop_state):
        sent_mean, sent_cov = shifted_2((loop_state[3], loop_state[4]), "tm", 1)

        def advance(operand):
            new_mean, new_cov = combine_state((operand[0], operand[1], one_flag), dev_total)
            return (operand[0], operand[1], one_flag, new_mean, new_cov)

        def remain(operand):
            return loop_state

        return lax.cond(position == turn_no, advance, remain, (sent_mean, sent_cov))

    final_state = lax.fori_loop(1, tm_count, handoff_turn, start_state)
    carry_in = (final_state[0], final_state[1], final_state[2])
    means, covs = jax.vmap(combine_state, in_axes=(None, 0))(carry_in, prefixes)
    smooth = smoother_elements(
        means, covs, global_step == tm_count * local_steps - 1, transit, process
    )
    last_el = jax.tree.map(lambda leaf: leaf[-1], smooth)
    front_els = jax.tree.map(lambda leaf: leaf[:-1], smooth)

    def backward(running, element):
        joined = smooth_join(element, running)
        return (joined, joined)

    _, head_els = lax.scan(backward, last_el, front_els, reverse=True)
    suffixes = jax.tree.map(
        lambda head_leaf, last_leaf: jnp.concatenate([head_leaf, last_leaf[None]], axis=0),
        head_els,
        last_el,
    )
    block_total = jax.tree.map(lambda leaf: leaf[0], suffixes)
    identity_smooth = (jnp.eye(width, dtype=jnp.float32), zero_vec, zero_mat)
    outer_gain, outer_mean, outer_cov = entering(block_total, "tm", reverse_join, identity_smooth)
    gains, shift_means, shift_covs = suffixes
    smooth_mean = matmul_hi(gains, outer_mean) + shift_means
    smooth_cov = matmul_hi(matmul_hi(gains, outer_cov), swap_last(gains)) + shift_covs
    return (smooth_mean, smooth_cov)


def solution(mesh):
    placed = (
        P(("groups", "tm"), None),
        P(("groups", "tm"), None),
        P("groups"),
        P("groups"),
        P("groups", None),
    )
    return jax.shard_map(
        shards,
        mesh=mesh,
        in_specs=placed,
        out_specs=(P(("groups", "tm"), None), P(("groups", "tm"), None, None)),
        check_vma=False,
    )
```

profile of v0, /device:TPU:1, one launch (start us, length us, event | category | flops | bytes accessed | tf_op | source)
XLA Modules:
  0.0 2068.3 jit_solution(4631852891109033968)
XLA Ops:
  10.9 11.7 custom-call.52
  22.6 9.8 custom-call.53
  33.2 11.7 custom-call.54
  51.9 19.7 custom-call.55
  75.5 1131.2 %while.46 = (s32[]{:T(128)}, f32[256]{0:T(256)S(1)}, f32[256,256]{0,1:T(8,128)S(1)}, f32[]{:T(128)}, f32[256]{0:T(256)S(1)}, /*index=5*/f32[256,256]{1,0:T(8,128...) while((s32[]{:T(128)}, f32[256]{0:T(256)S(1)}, ...), condition=%wide.region_11.15_spmd, body=%wide.region_4.14_spmd.sunk | while | flops 1867187200 | bytes 16702023 | solution.py:249
  76.0 4.5 collective-permute-start
  83.8 102.8 %conditional.2 = ((f32[256]{0:T(256)S(1)}, f32[256,256]{0,1:T(8,128)S(1)}, f32[]{:T(128)}, f32[256]{0:T(256)S(1)}, f32[256,256]{1,0:T(8,128)S(1)})) conditional(s32[]{:T(128)} %convert_element_type.81, (f32[256]{0:T(256)S(1)}, f32[256,256]{0,1:T(8,128)S(1)}, f32[]{:T(128)}, f32[256]{0:T(256)S(1)}, f32[256,256]{1,0:T(8,128)S(1)}) %tuple.164, ...), branch_computations={%region_5.7_spmd, %region_6.13_spmd} | conditional | flops 1867187200 | bytes 15124748 | solution.py:247
  84.0 11.7 custom-call.46
  95.8 9.8 custom-call.47
  106.3 11.7 custom-call.48
  121.3 11.7 custom-call.49
  133.0 9.8 custom-call.50
  143.6 11.7 custom-call.51
  162.1 19.7 custom-call.27
  192.2 107.2 %collective-permute-start = (f32[256,256]{0,1:T(8,128)S(1)}, f32[256,256]{0,1:T(8,128)S(1)}, u32[]{:S(2)}, u32[]{:S(2)}) collective-permute-start(f32[256,256]{0,1:T(8,128)S(1)} %copy.117), channel_id=1, source_target_pairs={{0,1},{1,2},{2,3},{3,4},{4,5},{5,6},{6,7},{7,8},{8,9},{9,10},{10,1... | collective-permute-start | bytes 786440 | tf_op jit(solution)/shard_map/while/body/eval_jaxpr/ppermute | solution.py:13
  302.9 4.4 collective-permute-start
  307.3 102.0 %collective-permute-start.1 = (f32[256]{0:T(256)S(1)}, f32[256]{0:T(256)S(1)}, u32[]{:S(2)}, u32[]{:S(2)}) collective-permute-start(f32[256]{0:T(256)S(1)} %get-tuple-element.919), channel_id=1, source_target_pairs={{0,1},{1,2},{2,3},{3,4},{4,5},{5,6},{6,7},{7,8},{8,9},{9,10},{10,1... | collective-permute-start | bytes 3080 | tf_op jit(solution)/shard_map/while/body/eval_jaxpr/ppermute | solution.py:13
  417.8 106.0 %collective-permute-start = (f32[256,256]{0,1:T(8,128)S(1)}, f32[256,256]{0,1:T(8,128)S(1)}, u32[]{:S(2)}, u32[]{:S(2)}) collective-permute-start(f32[256,256]{0,1:T(8,128)S(1)} %copy.117), channel_id=1, source_target_pairs={{0,1},{1,2},{2,3},{3,4},{4,5},{5,6},{6,7},{7,8},{8,9},{9,10},{10,1... | collective-permute-start | bytes 786440 | tf_op jit(solution)/shard_map/while/body/eval_jaxpr/ppermute | solution.py:13
  527.2 5.3 collective-permute-start
  532.5 101.0 %collective-permute-start.1 = (f32[256]{0:T(256)S(1)}, f32[256]{0:T(256)S(1)}, u32[]{:S(2)}, u32[]{:S(2)}) collective-permute-start(f32[256]{0:T(256)S(1)} %get-tuple-element.919), channel_id=1, source_target_pairs={{0,1},{1,2},{2,3},{3,4},{4,5},{5,6},{6,7},{7,8},{8,9},{9,10},{10,1... | collective-permute-start | bytes 3080 | tf_op jit(solution)/shard_map/while/body/eval_jaxpr/ppermute | solution.py:13
  634.4 5.2 collective-permute-start
  643.0 104.2 %collective-permute-start = (f32[256,256]{0,1:T(8,128)S(1)}, f32[256,256]{0,1:T(8,128)S(1)}, u32[]{:S(2)}, u32[]{:S(2)}) collective-permute-start(f32[256,256]{0,1:T(8,128)S(1)} %copy.117), channel_id=1, source_target_pairs={{0,1},{1,2},{2,3},{3,4},{4,5},{5,6},{6,7},{7,8},{8,9},{9,10},{10,1... | collective-permute-start | bytes 786440 | tf_op jit(solution)/shard_map/while/body/eval_jaxpr/ppermute | solution.py:13
  750.6 5.3 collective-permute-start
  756.0 100.9 %collective-permute-start.1 = (f32[256]{0:T(256)S(1)}, f32[256]{0:T(256)S(1)}, u32[]{:S(2)}, u32[]{:S(2)}) collective-permute-start(f32[256]{0:T(256)S(1)} %get-tuple-element.919), channel_id=1, source_target_pairs={{0,1},{1,2},{2,3},{3,4},{4,5},{5,6},{6,7},{7,8},{8,9},{9,10},{10,1... | collective-permute-start | bytes 3080 | tf_op jit(solution)/shard_map/while/body/eval_jaxpr/ppermute | solution.py:13
  857.7 5.2 collective-permute-start
  866.3 105.2 %collective-permute-start = (f32[256,256]{0,1:T(8,128)S(1)}, f32[256,256]{0,1:T(8,128)S(1)}, u32[]{:S(2)}, u32[]{:S(2)}) collective-permute-start(f32[256,256]{0,1:T(8,128)S(1)} %copy.117), channel_id=1, source_target_pairs={{0,1},{1,2},{2,3},{3,4},{4,5},{5,6},{6,7},{7,8},{8,9},{9,10},{10,1... | collective-permute-start | bytes 786440 | tf_op jit(solution)/shard_map/while/body/eval_jaxpr/ppermute | solution.py:13
  975.0 5.3 collective-permute-start
  980.3 100.8 %collective-permute-start.1 = (f32[256]{0:T(256)S(1)}, f32[256]{0:T(256)S(1)}, u32[]{:S(2)}, u32[]{:S(2)}) collective-permute-start(f32[256]{0:T(256)S(1)} %get-tuple-element.919), channel_id=1, source_target_pairs={{0,1},{1,2},{2,3},{3,4},{4,5},{5,6},{6,7},{7,8},{8,9},{9,10},{10,1... | collective-permute-start | bytes 3080 | tf_op jit(solution)/shard_map/while/body/eval_jaxpr/ppermute | solution.py:13
  1081.9 5.4 collective-permute-start
  1090.7 104.2 %collective-permute-start = (f32[256,256]{0,1:T(8,128)S(1)}, f32[256,256]{0,1:T(8,128)S(1)}, u32[]{:S(2)}, u32[]{:S(2)}) collective-permute-start(f32[256,256]{0,1:T(8,128)S(1)} %copy.117), channel_id=1, source_target_pairs={{0,1},{1,2},{2,3},{3,4},{4,5},{5,6},{6,7},{7,8},{8,9},{9,10},{10,1... | collective-permute-start | bytes 786440 | tf_op jit(solution)/shard_map/while/body/eval_jaxpr/ppermute | solution.py:13
  1207.1 11.7 custom-call.56
  1218.9 9.8 custom-call.57
  1229.5 11.7 custom-call.58
  1245.1 12.1 custom-call.59
  1257.3 9.8 custom-call.60
  1267.9 11.7 custom-call.61
  1286.4 19.8 custom-call.62
  1310.8 11.7 custom-call.63
  1322.6 9.8 custom-call.64
  1333.1 11.9 custom-call.65
  1351.8 19.7 custom-call.29
  1377.1 528.5 %all-gather.2 = f32[16,1,256]{2,1,0:T(1,128)S(1)} all-gather(f32[1,1,256]{2,1,0:T(1,128)S(1)} %bitcast.494), channel_id=2, replica_groups=mesh['groups'=2,'tm'=16] {'tm'}, dimensions={0}, use_global_device_ids=true | all-gather | bytes 17408 | tf_op jit(solution)/shard_map/all_gather | solution.py:18
  1905.7 34.0 %all-gather.8.cloned.1.call-done = f32[4096,256]{0,1:T(8,128)} async-done(((f32[256,256]{0,1:T(8,128)}), f32[4096,256]{0,1:T(8,128)}) %all-gather.8.cloned.1.call-update) | async-done | bytes 4194320 | tf_op jit(solution)/shard_map/all_gather | solution.py:18
  1939.6 5.6 copy.89
  1945.2 4.6 rev.11
  1949.8 41.4 %all-gather.6.cloned.1.call-done = f32[16,256,256]{2,1,0:T(8,128)} async-done(((f32[1,256,256]{2,1,0:T(8,128)}), f32[16,256,256]{2,1,0:T(8,128)}) %all-gather.6.cloned.1.call-update) | async-done | bytes 4194320 | tf_op jit(solution)/shard_map/all_gather | solution.py:18
  1991.1 4.6 rev.9
  1995.7 62.7 %while.48 = (s32[]{:T(128)}, f32[256]{0:T(256)S(1)}, f32[256,256]{1,0:T(8,128)S(1)}, s32[]{:T(128)}, f32[16,256,256]{2,1,0:T(8,128)}, /*index=5*/f32[16,256]{1,0...) while((s32[]{:T(128)}, f32[256]{0:T(256)S(1)}, f32[256,256]{1,0:T(8,128)S(1)}, ...), condition=%wide.region_13.17_spmd.clone, body=%wide.region_12.16_spmd.clone.sunk | while | flops 403702784 | bytes 2371705 | solution.py:29
  (389 shorter events, 181.5 us)
Async XLA Ops:
  7.2 1932.5 %all-gather.8.cloned.1.call-start = ((), (), s32[]{:S(2)}) async-start(), calls=%async_computation.1 | async-start | bytes 4456448 | tf_op jit(solution)/shard_map/all_gather | solution.py:18
  8.9 64.3 %copy-start.2 = (f32[1,128]{1,0:T(1,128)S(1)}, f32[1,128]{1,0:T(1,128)}, u32[]{:S(2)}) copy-start(f32[1,128]{1,0:T(1,128)} %param.15) | copy-start | bytes 1540
  10.7 63.4 %copy-start.1 = (f32[128]{0:T(128)S(1)}, f32[128]{0:T(128)}, u32[]{:S(2)}) copy-start(f32[128]{0:T(128)} %param.17) | copy-start | bytes 1540
  76.0 7.9 collective-permute-start
  80.5 3.3 collective-permute-start.1
  186.8 5.3 collective-permute-start
  188.7 3.3 collective-permute-start.1
  192.2 110.6 %collective-permute-start = (f32[256,256]{0,1:T(8,128)S(1)}, f32[256,256]{0,1:T(8,128)S(1)}, u32[]{:S(2)}, u32[]{:S(2)}) collective-permute-start(f32[256,256]{0,1:T(8,128)S(1)} %copy.117), channel_id=1, source_target_pairs={{0,1},{1,2},{2,3},{3,4},{4,5},{5,6},{6,7},{7,8},{8,9},{9,10},{10,1... | collective-permute-start | bytes 786440 | tf_op jit(solution)/shard_map/while/body/eval_jaxpr/ppermute | solution.py:13
  299.4 3.3 collective-permute-start.1
  302.9 107.1 %collective-permute-start = (f32[256,256]{0,1:T(8,128)S(1)}, f32[256,256]{0,1:T(8,128)S(1)}, u32[]{:S(2)}, u32[]{:S(2)}) collective-permute-start(f32[256,256]{0,1:T(8,128)S(1)} %copy.117), channel_id=1, source_target_pairs={{0,1},{1,2},{2,3},{3,4},{4,5},{5,6},{6,7},{7,8},{8,9},{9,10},{10,1... | collective-permute-start | bytes 786440 | tf_op jit(solution)/shard_map/while/body/eval_jaxpr/ppermute | solution.py:13
  307.3 102.7 %collective-permute-start.1 = (f32[256]{0:T(256)S(1)}, f32[256]{0:T(256)S(1)}, u32[]{:S(2)}, u32[]{:S(2)}) collective-permute-start(f32[256]{0:T(256)S(1)} %get-tuple-element.919), channel_id=1, source_target_pairs={{0,1},{1,2},{2,3},{3,4},{4,5},{5,6},{6,7},{7,8},{8,9},{9,10},{10,1... | collective-permute-start | bytes 3080 | tf_op jit(solution)/shard_map/while/body/eval_jaxpr/ppermute | solution.py:13
  410.1 7.5 collective-permute-start
  414.3 3.3 collective-permute-start.1
  417.8 109.3 %collective-permute-start = (f32[256,256]{0,1:T(8,128)S(1)}, f32[256,256]{0,1:T(8,128)S(1)}, u32[]{:S(2)}, u32[]{:S(2)}) collective-permute-start(f32[256,256]{0,1:T(8,128)S(1)} %copy.117), channel_id=1, source_target_pairs={{0,1},{1,2},{2,3},{3,4},{4,5},{5,6},{6,7},{7,8},{8,9},{9,10},{10,1... | collective-permute-start | bytes 786440 | tf_op jit(solution)/shard_map/while/body/eval_jaxpr/ppermute | solution.py:13
  523.8 3.3 collective-permute-start.1
  527.2 107.0 %collective-permute-start = (f32[256,256]{0,1:T(8,128)S(1)}, f32[256,256]{0,1:T(8,128)S(1)}, u32[]{:S(2)}, u32[]{:S(2)}) collective-permute-start(f32[256,256]{0,1:T(8,128)S(1)} %copy.117), channel_id=1, source_target_pairs={{0,1},{1,2},{2,3},{3,4},{4,5},{5,6},{6,7},{7,8},{8,9},{9,10},{10,1... | collective-permute-start | bytes 786440 | tf_op jit(solution)/shard_map/while/body/eval_jaxpr/ppermute | solution.py:13
  532.5 101.7 %collective-permute-start.1 = (f32[256]{0:T(256)S(1)}, f32[256]{0:T(256)S(1)}, u32[]{:S(2)}, u32[]{:S(2)}) collective-permute-start(f32[256]{0:T(256)S(1)} %get-tuple-element.919), channel_id=1, source_target_pairs={{0,1},{1,2},{2,3},{3,4},{4,5},{5,6},{6,7},{7,8},{8,9},{9,10},{10,1... | collective-permute-start | bytes 3080 | tf_op jit(solution)/shard_map/while/body/eval_jaxpr/ppermute | solution.py:13
  634.4 8.5 collective-permute-start
  639.5 3.3 collective-permute-start.1
  643.0 107.5 %collective-permute-start = (f32[256,256]{0,1:T(8,128)S(1)}, f32[256,256]{0,1:T(8,128)S(1)}, u32[]{:S(2)}, u32[]{:S(2)}) collective-permute-start(f32[256,256]{0,1:T(8,128)S(1)} %copy.117), channel_id=1, source_target_pairs={{0,1},{1,2},{2,3},{3,4},{4,5},{5,6},{6,7},{7,8},{8,9},{9,10},{10,1... | collective-permute-start | bytes 786440 | tf_op jit(solution)/shard_map/while/body/eval_jaxpr/ppermute | solution.py:13
  747.2 3.3 collective-permute-start.1
  750.6 106.9 %collective-permute-start = (f32[256,256]{0,1:T(8,128)S(1)}, f32[256,256]{0,1:T(8,128)S(1)}, u32[]{:S(2)}, u32[]{:S(2)}) collective-permute-start(f32[256,256]{0,1:T(8,128)S(1)} %copy.117), channel_id=1, source_target_pairs={{0,1},{1,2},{2,3},{3,4},{4,5},{5,6},{6,7},{7,8},{8,9},{9,10},{10,1... | collective-permute-start | bytes 786440 | tf_op jit(solution)/shard_map/while/body/eval_jaxpr/ppermute | solution.py:13
  756.0 101.6 %collective-permute-start.1 = (f32[256]{0:T(256)S(1)}, f32[256]{0:T(256)S(1)}, u32[]{:S(2)}, u32[]{:S(2)}) collective-permute-start(f32[256]{0:T(256)S(1)} %get-tuple-element.919), channel_id=1, source_target_pairs={{0,1},{1,2},{2,3},{3,4},{4,5},{5,6},{6,7},{7,8},{8,9},{9,10},{10,1... | collective-permute-start | bytes 3080 | tf_op jit(solution)/shard_map/while/body/eval_jaxpr/ppermute | solution.py:13
  857.7 8.5 collective-permute-start
  862.9 3.3 collective-permute-start.1
  866.3 108.5 %collective-permute-start = (f32[256,256]{0,1:T(8,128)S(1)}, f32[256,256]{0,1:T(8,128)S(1)}, u32[]{:S(2)}, u32[]{:S(2)}) collective-permute-start(f32[256,256]{0,1:T(8,128)S(1)} %copy.117), channel_id=1, source_target_pairs={{0,1},{1,2},{2,3},{3,4},{4,5},{5,6},{6,7},{7,8},{8,9},{9,10},{10,1... | collective-permute-start | bytes 786440 | tf_op jit(solution)/shard_map/while/body/eval_jaxpr/ppermute | solution.py:13
  971.5 3.3 collective-permute-start.1
  975.0 106.8 %collective-permute-start = (f32[256,256]{0,1:T(8,128)S(1)}, f32[256,256]{0,1:T(8,128)S(1)}, u32[]{:S(2)}, u32[]{:S(2)}) collective-permute-start(f32[256,256]{0,1:T(8,128)S(1)} %copy.117), channel_id=1, source_target_pairs={{0,1},{1,2},{2,3},{3,4},{4,5},{5,6},{6,7},{7,8},{8,9},{9,10},{10,1... | collective-permute-start | bytes 786440 | tf_op jit(solution)/shard_map/while/body/eval_jaxpr/ppermute | solution.py:13
  980.3 101.5 %collective-permute-start.1 = (f32[256]{0:T(256)S(1)}, f32[256]{0:T(256)S(1)}, u32[]{:S(2)}, u32[]{:S(2)}) collective-permute-start(f32[256]{0:T(256)S(1)} %get-tuple-element.919), channel_id=1, source_target_pairs={{0,1},{1,2},{2,3},{3,4},{4,5},{5,6},{6,7},{7,8},{8,9},{9,10},{10,1... | collective-permute-start | bytes 3080 | tf_op jit(solution)/shard_map/while/body/eval_jaxpr/ppermute | solution.py:13
  1081.9 8.7 collective-permute-start
  1087.3 3.3 collective-permute-start.1
  1090.7 107.5 %collective-permute-start = (f32[256,256]{0,1:T(8,128)S(1)}, f32[256,256]{0,1:T(8,128)S(1)}, u32[]{:S(2)}, u32[]{:S(2)}) collective-permute-start(f32[256,256]{0,1:T(8,128)S(1)} %copy.117), channel_id=1, source_target_pairs={{0,1},{1,2},{2,3},{3,4},{4,5},{5,6},{6,7},{7,8},{8,9},{9,10},{10,1... | collective-permute-start | bytes 786440 | tf_op jit(solution)/shard_map/while/body/eval_jaxpr/ppermute | solution.py:13
  1194.9 3.3 collective-permute-start.1
  1374.5 616.6 %all-gather.6.cloned.1.call-start = ((), (), s32[]{:S(2)}) async-start(), calls=%async_computation | async-start | bytes 4456448 | tf_op jit(solution)/shard_map/all_gather | solution.py:18
  1995.7 63.3 %copy-start = (f32[256,256]{0,1:T(8,128)S(1)}, f32[256,256]{0,1:T(8,128)}, u32[]{:S(2)}) copy-start(f32[256,256]{0,1:T(8,128)} %convolution_subtract_fusion.5) | copy-start | bytes 786436
Sparse Core Ops, SparseCore 0:
  1374.6 564.9 all-gather.7
  1942.4 48.7 all-gather.5
where the time goes:
time: 2080 us; the launch traced here: 2070 us
  starting transfers between devices  1000 us (48%)
  blocking collectives  529 us (25%)
  other arithmetic  292 us (14%)
  waiting for transfers between devices  89.2 us (4%)
  matrix products  82.8 us (4%)
  local copies, waits for them, and re-layouts  39 us (2%)
    ppermute x30, starting transfers between devices, shifted_2(): return lax.ppermute(array, axis, pairs)  1000 us
    all_gather x1, blocking collectives, entering(): pieces = jax.tree.map(lambda part: lax.all_gather(part, axis), value)  529 us
    another operation x21, other arithmetic, spd_inverse(): factor = jnp.linalg.cholesky(matrix)  104 us
    all_gather x2, waiting for transfers between devices, entering(): pieces = jax.tree.map(lambda part: lax.all_gather(part, axis), value)  75.3 us
    dot_general x77, matrix products, matmul_hi(): return jnp.matmul(left, right, precision=HIGHEST)  75 us
    another operation x13, other arithmetic, cov_gain(): factor = jnp.linalg.cholesky(safe_cov)  68.7 us
    another operation x8, other arithmetic, spd_inverse(): lax.linalg.triangular_solve(factor, identity_mat, left_side=True, lower=T...  59.3 us
  transfers between devices with their start and end apart: 32, of which 17 were waited for; matrix products, arithmetic and copies ran while one was open for 1% of the time, Pallas kernels for 0%

commit v1 on v0

v1 whole, which is shorter than its diff:
```python
import jax
import jax.numpy as jnp
from jax import lax
from jax.sharding import PartitionSpec as P

HIGHEST = lax.Precision.HIGHEST
JITTER = 0.001


def matmul_hi(left, right):
    return jnp.matmul(left, right, precision=HIGHEST)


def swap_last(matrix):
    return jnp.swapaxes(matrix, -1, -2)


def apply_trans(transit, matrix):
    points = transit.shape[1]
    upper_half = matrix[..., :points, :]
    lower_half = matrix[..., points:, :]
    return jnp.concatenate(
        [
            transit[0][:, None] * upper_half + transit[1][:, None] * lower_half,
            transit[2][:, None] * upper_half + transit[3][:, None] * lower_half,
        ],
        axis=-2,
    )


def build_model(decay_rates, spatial_cov):
    decay_one = jnp.exp(-decay_rates)
    transit = jnp.stack(
        [
            decay_one * (1.0 + decay_rates),
            decay_one * decay_rates,
            -decay_one * decay_rates,
            decay_one * (1.0 - decay_rates),
        ]
    )
    decay_two = jnp.exp(-2.0 * decay_rates)
    var_ff = 1.0 - decay_two * (1.0 + 2.0 * decay_rates + 2.0 * decay_rates * decay_rates)
    cov_fg = 2.0 * decay_rates * decay_rates * decay_two
    var_gg = 1.0 - decay_two * (1.0 - 2.0 * decay_rates + 2.0 * decay_rates * decay_rates)
    fac_ff = jnp.sqrt(var_ff)
    fac_gf = cov_fg / fac_ff
    fac_gg = jnp.sqrt(var_gg - fac_gf * fac_gf)

    def scaled(left, right):
        return left[:, None] * spatial_cov * right[None, :]

    zero_block = jnp.zeros_like(spatial_cov)
    process = jnp.block(
        [
            [scaled(fac_ff, fac_ff), scaled(fac_ff, fac_gf)],
            [scaled(fac_gf, fac_ff), scaled(fac_gf, fac_gf) + scaled(fac_gg, fac_gg)],
        ]
    )
    process = process + JITTER * jnp.eye(2 * spatial_cov.shape[0], dtype=jnp.float32)
    prior = jnp.block([[spatial_cov, zero_block], [zero_block, spatial_cov]])
    return (transit, process, prior)


def predict(transit, process, mean, cov):
    forward_cov = apply_trans(transit, cov)
    cov_pred = apply_trans(transit, swap_last(forward_cov)) + process
    mean_pred = apply_trans(transit, mean[:, None])[:, 0]
    return mean_pred, cov_pred


def kalman_update(mean_pred, cov_pred, obs, root):
    points = obs.shape[-1]
    normal = jnp.eye(points, dtype=jnp.float32) + root[:, None] * cov_pred[:points, :points] * root[None, :]
    factor = jnp.linalg.cholesky(normal)
    innovation = root * (obs - mean_pred[:points])
    rhs = jnp.concatenate([root[:, None] * cov_pred[:points, :], innovation[:, None]], axis=1)
    half = lax.linalg.triangular_solve(factor, rhs, left_side=True, lower=True)
    gain_half = half[:, :-1]
    cov_new = cov_pred - matmul_hi(swap_last(gain_half), gain_half)
    mean_new = mean_pred + matmul_hi(swap_last(gain_half), half[:, -1])
    return mean_new, cov_new


def smoother_elements(means, covs, last_flag, transit, process):
    forward_cov = apply_trans(transit, covs)
    predicted = apply_trans(transit, swap_last(forward_cov)) + process
    factor = jnp.linalg.cholesky(predicted)
    half_solve = lax.linalg.triangular_solve(factor, forward_cov, left_side=True, lower=True)
    gain_t = lax.linalg.triangular_solve(
        factor, half_solve, left_side=True, lower=True, transpose_a=True
    )
    gains = swap_last(gain_t) * (1.0 - last_flag.astype(jnp.float32))[:, None, None]
    forward_mean = apply_trans(transit, means[..., None])
    shift_means = means - matmul_hi(gains, forward_mean)[..., 0]
    shift_covs = covs - matmul_hi(gains, forward_cov)
    return (gains, shift_means, shift_covs)


def smooth_join(lower_el, higher_el):
    gain_a, mean_a, cov_a = lower_el
    gain_b, mean_b, cov_b = higher_el
    return (
        matmul_hi(gain_a, gain_b),
        matmul_hi(gain_a, mean_b[..., None])[..., 0] + mean_a,
        matmul_hi(matmul_hi(gain_a, cov_b), swap_last(gain_a)) + cov_a,
    )


def shards(observed, obs_masks, decay_rates, noise_var, spatial_cov):
    transit, process, prior = build_model(decay_rates, spatial_cov)
    local_steps, points = observed.shape
    width = 2 * points
    position = lax.axis_index("tm")
    tm_count = lax.axis_size("tm")
    total_steps = tm_count * local_steps

    root_local = jnp.sqrt(obs_masks.astype(jnp.float32) / noise_var)
    packed = jnp.stack([observed, root_local], axis=1)
    gathered = lax.all_gather(packed, "tm", tiled=True)
    obs_all = gathered[:, 0]
    root_all = gathered[:, 1]

    mean_first, cov_first = kalman_update(
        jnp.zeros((width,), jnp.float32), prior, obs_all[0], root_all[0]
    )
    last_local = position * local_steps + (local_steps - 1)

    def filter_step(step, mean, cov):
        mean_pred, cov_pred = predict(transit, process, mean, cov)
        obs_now = lax.dynamic_index_in_dim(obs_all, step, keepdims=False)
        root_now = lax.dynamic_index_in_dim(root_all, step, keepdims=False)
        return kalman_update(mean_pred, cov_pred, obs_now, root_now)

    if local_steps == 1:

        def body(step, carry):
            return filter_step(step, carry[0], carry[1])

        mean_last, cov_last = lax.fori_loop(1, last_local + 1, body, (mean_first, cov_first))
        means = mean_last[None]
        covs = cov_last[None]
    else:
        mean_buf = jnp.zeros((local_steps, width), jnp.float32).at[0].set(mean_first)
        cov_buf = jnp.zeros((local_steps, width, width), jnp.float32).at[0].set(cov_first)

        def body(step, carry):
            mean, cov, mean_buf, cov_buf = carry
            mean, cov = filter_step(step, mean, cov)
            slot = step % local_steps
            mean_buf = lax.dynamic_update_index_in_dim(mean_buf, mean, slot, 0)
            cov_buf = lax.dynamic_update_index_in_dim(cov_buf, cov, slot, 0)
            return (mean, cov, mean_buf, cov_buf)

        _, _, means, covs = lax.fori_loop(
            1, last_local + 1, body, (mean_first, cov_first, mean_buf, cov_buf)
        )

    global_step = position * local_steps + jnp.arange(local_steps)
    last_flag = global_step == total_steps - 1
    if local_steps == 1:

        def compute_elements(operand):
            return smoother_elements(operand[0], operand[1], last_flag, transit, process)

        def final_elements(operand):
            return (jnp.zeros_like(operand[1]), operand[0], operand[1])

        smooth = lax.cond(position == tm_count - 1, final_elements, compute_elements, (means, covs))
    else:
        smooth = smoother_elements(means, covs, last_flag, transit, process)

    if local_steps > 1:
        last_el = jax.tree.map(lambda leaf: leaf[-1], smooth)
        front_els = jax.tree.map(lambda leaf: leaf[:-1], smooth)

        def backward(running, element):
            joined = smooth_join(element, running)
            return (joined, joined)

        _, head_els = lax.scan(backward, last_el, front_els, reverse=True)
        suffixes = jax.tree.map(
            lambda head_leaf, last_leaf: jnp.concatenate([head_leaf, last_leaf[None]], axis=0),
            head_els,
            last_el,
        )
        block_total = jax.tree.map(lambda leaf: leaf[0], suffixes)
    else:
        block_total = jax.tree.map(lambda leaf: leaf[0], smooth)

    running = block_total
    shift = 1
    while shift < tm_count:
        pairs = [(source, source - shift) for source in range(shift, tm_count)]
        received = lax.ppermute(running, "tm", pairs)
        running = smooth_join(running, received)
        shift *= 2

    if local_steps == 1:
        return (running[1][None], running[2][None])
    pairs = [(source, source - 1) for source in range(1, tm_count)]
    after_mine = lax.ppermute(running, "tm", pairs)
    gains, shift_means, shift_covs = suffixes
    smooth_mean = matmul_hi(gains, after_mine[1][:, None])[..., 0] + shift_means
    smooth_cov = matmul_hi(matmul_hi(gains, after_mine[2]), swap_last(gains)) + shift_covs
    return (smooth_mean, smooth_cov)


def solution(mesh):
    placed = (
        P(("groups", "tm"), None),
        P(("groups", "tm"), None),
        P("groups"),
        P("groups"),
        P("groups", None),
    )
    return jax.shard_map(
        shards,
        mesh=mesh,
        in_specs=placed,
        out_specs=(P(("groups", "tm"), None), P(("groups", "tm"), None, None)),
        check_vma=False,
    )
```

time: 2080 us -> 505 us (0.24)
  starting transfers between devices: 1000 us -> 16.2 us
  blocking collectives: 529 us -> 23.1 us
  waiting for transfers between devices: 89.2 us -> 336 us
  other arithmetic: 292 us -> 100 us
  matrix products: 82.8 us -> 12.2 us
  local copies, waits for them, and re-layouts: 39 us -> 6.42 us
    ppermute x30 -> x11, starting transfers between devices: 1000 us -> 16.2 us  [shards(): received = lax.ppermute(running, 'tm', pairs)]
    all_gather x1, blocking collectives: 529 us -> 23.1 us  [shards(): gathered = lax.all_gather(packed, 'tm', tiled=True)]
    ppermute x30 -> x11, waiting for transfers between devices: 13.9 us -> 336 us  [shards(): received = lax.ppermute(running, 'tm', pairs)]
    another operation x43 -> x12, other arithmetic: 232 us -> 45.8 us  [the longest x6 24.9 us: kalman_update(): factor = jnp.linalg.cholesky(normal)]
    all_gather x2 -> x0, waiting for transfers between devices: 75.3 us -> none  [entering(): pieces = jax.tree.map(lambda part: lax.all_gather(part, axis), value)]
    dot_general x77 -> x21, matrix products: 75 us -> 9.03 us  [matmul_hi(): return jnp.matmul(left, right, precision=HIGHEST)]
  transfers between devices with their start and end apart: 32 -> 11, of which waited for: 17 -> 9; matrix products, arithmetic and copies ran while one was open for 1% -> 1% of each run, Pallas kernels for 0% -> 0%
where the time goes in v1:
time: 505 us; the launch traced here: 498 us
  waiting for transfers between devices  336 us (67%)
  other arithmetic  100 us (20%)
  blocking collectives  23.1 us (5%)
  starting transfers between devices  16.2 us (3%)
  matrix products  12.2 us (2%)
  local copies, waits for them, and re-layouts  6.42 us (1%)
    ppermute x11, waiting for transfers between devices, shards(): received = lax.ppermute(running, 'tm', pairs)  336 us
    another operation x6, other arithmetic, smoother_elements(): factor = jnp.linalg.cholesky(predicted)  34 us
    another operation x6, other arithmetic, kalman_update(): factor = jnp.linalg.cholesky(normal)  24.9 us
    all_gather x1, blocking collectives, shards(): gathered = lax.all_gather(packed, 'tm', tiled=True)  23.1 us
    another operation x4, other arithmetic, kalman_update(): half = lax.linalg.triangular_solve(factor, rhs, left_side=True, lower=True)  20.9 us
    another operation x3, other arithmetic, smoother_elements(): lax.linalg.triangular_solve(factor, half_solve, left_side=True, lower=Tru...  19.7 us
    ppermute x11, starting transfers between devices, shards(): received = lax.ppermute(running, 'tm', pairs)  16.2 us
  transfers between devices with their start and end apart: 11, of which 9 were waited for; matrix products, arithmetic and copies ran while one was open for 1% of the time, Pallas kernels for 0%

profile of v1, /device:TPU:1, one launch (start us, length us, event | category | flops | bytes accessed | tf_op | source)
XLA Modules:
  0.0 498.3 jit_solution(2744481612989866936)
XLA Ops:
  0.7 0.6 copy-done.3
  1.3 0.7 copy-done.1
  2.0 23.1 %all_gather.3 = f32[16,2,128]{2,1,0:T(2,128)S(1)} all-gather(f32[1,2,128]{2,1,0:T(2,128)S(1)} %pad_maximum_fusion.3), channel_id=1, replica_groups=mesh['groups'=2,'tm'=16] {'tm'}, dimensions={0}, use_global_device_ids=true | all-gather | bytes 17408 | tf_op jit(solution)/shard_map/all_gather | solution.py:119
  25.7 11.7 %custom-call.32 = f32[128,128]{1,0:T(8,128)S(1)} custom-call(f32[128,128]{1,0:T(8,128)S(1)} %fusion.49), custom_call_target="Cholesky" | custom-call | tf_op jit(solution)/shard_map/jit(cholesky)/cholesky/custom-call.1 | solution.py:74
  37.5 0.7 compare_reduce_fusion.3
  38.2 0.6 fusion.47
  38.8 9.8 %custom-call.33 = f32[1,128,128]{1,2,0:T(8,128)S(1)} custom-call(f32[1,128,128]{2,1,0:T(8,128)S(1)} %fusion.47), custom_call_target="InvertDiagBlocksLowerTriangular" | custom-call | tf_op jit(solution)/shard_map/triangular_solve/custom-call.0 | solution.py:77
  49.9 25.2 %while.14 = (s32[]{:T(128)}, f32[256]{0:T(256)S(1)}, f32[256,256]{0,1:T(8,128)S(1)}, s32[]{:T(128)}, f32[128]{0:T(128)S(1)}, /*index=5*/f32[128]{0:T(128)S(1)}, ...) while((s32[]{:T(128)}, f32[256]{0:T(256)S(1)}, ...), condition=%wide.region_3.6_spmd, body=%wide.region_2.5_spmd.sunk | while | flops 152618752 | bytes 5461689 | solution.py:139
  51.2 11.7 %custom-call.37 = f32[128,128]{1,0:T(8,128)S(1)} custom-call(f32[128,128]{1,0:T(8,128)S(1)} %fusion.129), custom_call_target="Cholesky" | custom-call | tf_op jit(solution)/shard_map/while/body/jit(cholesky)/cholesky/custom-call.1 | solution.py:74
  62.9 0.7 compare_reduce_fusion.5
  63.6 0.6 fusion.130
  64.3 9.8 %custom-call.38 = f32[1,128,128]{1,2,0:T(8,128)S(1)} custom-call(f32[1,128,128]{2,1,0:T(8,128)S(1)} %fusion.130), custom_call_target="InvertDiagBlocksLowerTriangular" | custom-call | tf_op jit(solution)/shard_map/while/body/triangular_solve/custom-call.0 | solution.py:77
  75.1 63.4 %conditional.1 = (f32[1,256]{1,0:T(1,128)S(1)}, f32[256,256]{0,1:T(8,128)S(1)}, f32[1,256,256]{2,1,0:T(8,128)S(1)}) conditional(s32[]{:T(128)} %convert_element_type.18, (f32[128]{0:T(128)S(1)}, f32[1,256,256]{1,2,0:T(8,128)S(1)}, f32[128]{0:T(128)S(1)}, f32[128]{0:T(128)S(1)}, f32[128]{0:T(128)S(1)}, /*index=5*/f32[256,256]{0,1:T(8,128)S(1)}, ...), branch_computations={%region_4.11_spmd, %region_9.12_spmd} | conditional | flops 556025344 | bytes 11482373 | solution.py:168
  75.8 11.7 %custom-call.24 = f32[1,128,128]{2,1,0:T(8,128)S(1)} custom-call(f32[1,128,128]{2,1,0:T(8,128)S(1)} %cholesky.48), custom_call_target="Cholesky" | custom-call | tf_op jit(solution)/shard_map/cond/branch_0_fun/jit(cholesky)/cholesky | solution.py:87
  87.6 9.8 %custom-call.25 = f32[1,1,128,128]{2,3,1,0:T(8,128)S(1)} custom-call(f32[1,1,128,128]{3,2,1,0:T(8,128)S(1)} %get-tuple-element.221), custom_call_target="InvertDiagBlocksLowerTriangular" | custom-call | tf_op jit(solution)/shard_map/cond/branch_0_fun/jit(cholesky)/cholesky | solution.py:87
  97.9 11.7 %custom-call.26 = f32[1,128,128]{2,1,0:T(8,128)S(1)} custom-call(f32[1,128,128]{2,1,0:T(8,128)S(1)} %fusion.20), custom_call_target="Cholesky" | custom-call | tf_op jit(solution)/shard_map/cond/branch_0_fun/jit(cholesky)/cholesky | solution.py:87
  109.7 0.7 compare_reduce_fusion.1
  111.6 4.0 while.13
  111.8 0.6 fusion.133
  112.5 1.3 bitcast_dynamic-update-slice_fusion.3
  113.8 0.6 fusion.133
  114.4 1.3 bitcast_dynamic-update-slice_fusion.3
  115.7 19.7 %custom-call.27 = f32[1,2,128,128]{2,3,1,0:T(8,128)S(1)} custom-call(f32[1,2,128,128]{3,2,1,0:T(8,128)S(1)} %bitcast.262), custom_call_target="InvertDiagBlocksLowerTriangular" | custom-call | tf_op jit(solution)/shard_map/cond/branch_0_fun/triangular_solve | solution.py:89
  137.7 0.6 fusion.17
  138.5 1.9 collective-permute-start.7
  140.4 1.9 collective-permute-start.3
  142.4 1.9 collective-permute-start
  144.3 22.4 %collective-permute-done.3 = f32[256]{0:T(256)S(1)} collective-permute-done((f32[256]{0:T(256)S(1)}, f32[256]{0:T(256)S(1)}, u32[]{:S(2)}, u32[]{:S(2)}) %collective-permute-start.3) | collective-permute-done | bytes 1056 | tf_op jit(solution)/shard_map/ppermute | solution.py:194
  167.0 1.3 collective-permute-start.4
  168.3 0.6 fusion.65
  169.3 1.3 collective-permute-start.8
  170.6 0.6 fusion.59
  171.2 1.3 collective-permute-start.1
  172.5 48.7 %collective-permute-done.4 = f32[256]{0:T(256)S(1)} collective-permute-done((f32[256]{0:T(256)S(1)}, f32[256]{0:T(256)S(1)}, u32[]{:S(2)}, u32[]{:S(2)}) %collective-permute-start.4) | collective-permute-done | bytes 1056 | tf_op jit(solution)/shard_map/ppermute | solution.py:194
  221.5 1.3 collective-permute-start.5
  222.9 4.1 collective-permute-done.8
  227.8 1.3 collective-permute-start.9
  229.1 0.7 collective-permute-done.1
  230.2 1.3 collective-permute-start.2
  231.5 89.9 %collective-permute-done.5 = f32[256]{0:T(256)S(1)} collective-permute-done((f32[256]{0:T(256)S(1)}, f32[256]{0:T(256)S(1)}, u32[]{:S(2)}, u32[]{:S(2)}) %collective-permute-start.5) | collective-permute-done | bytes 1056 | tf_op jit(solution)/shard_map/ppermute | solution.py:194
  321.7 1.3 collective-permute-start.6
  323.0 7.4 %collective-permute-done.9 = f32[256,256]{1,0:T(8,128)S(1)} collective-permute-done((f32[256,256]{1,0:T(8,128)S(1)}, f32[256,256]{1,0:T(8,128)S(1)}, u32[]{:S(2)}, u32[]{:S(2)}) %collective-permute-start.9) | collective-permute-done | bytes 262176 | tf_op jit(solution)/shard_map/ppermute | solution.py:194
  331.2 1.3 collective-permute-start.10
  332.5 0.7 collective-permute-done.2
  333.6 145.0 %collective-permute-done.6 = f32[256]{0:T(256)S(1)} collective-permute-done((f32[256]{0:T(256)S(1)}, f32[256]{0:T(256)S(1)}, u32[]{:S(2)}, u32[]{:S(2)}) %collective-permute-start.6) | collective-permute-done | bytes 1056 | tf_op jit(solution)/shard_map/ppermute | solution.py:194
  478.6 0.9 convolution_add_fusion.4
  479.5 17.0 %collective-permute-done.10 = f32[256,256]{1,0:T(8,128)S(1)} collective-permute-done((f32[256,256]{1,0:T(8,128)S(1)}, f32[256,256]{1,0:T(8,128)S(1)}, u32[]{:S(2)}, u32[]{:S(2)}) %collective-permute-start.10) | collective-permute-done | bytes 262176 | tf_op jit(solution)/shard_map/ppermute | solution.py:194
  496.9 1.1 fusion.38
  (91 shorter events, 10.8 us)
Async XLA Ops:
  0.6 0.7 copy-start.3
  0.6 0.7 copy-start.4
  1.3 0.7 copy-start.1
  2.0 23.2 %copy-start.2 = (f32[128]{0:T(128)S(1)}, f32[128]{0:T(128)}, u32[]{:S(2)}) copy-start(f32[128]{0:T(128)} %param.14) | copy-start | bytes 1540
  2.0 23.3 %copy-start = (f32[128,128]{1,0:T(8,128)S(1)}, f32[128,128]{1,0:T(8,128)}, u32[]{:S(2)}) copy-start(f32[128,128]{1,0:T(8,128)} %param.16) | copy-start | bytes 196612
  138.5 29.8 %collective-permute-start.7 = (f32[256,256]{1,0:T(8,128)S(1)}, f32[256,256]{1,0:T(8,128)S(1)}, u32[]{:S(2)}, u32[]{:S(2)}) collective-permute-start(f32[256,256]{1,0:T(8,128)S(1)} %bitcast.242), channel_id=1, source_target_pairs={{1,0},{2,1},{3,2},{4,3},{5,4},{6,5},{7,6},{8,7},{9,8},{10,9},{11,1... | collective-permute-start | bytes 786440 | tf_op jit(solution)/shard_map/ppermute | solution.py:194
  140.4 26.3 %collective-permute-start.3 = (f32[256]{0:T(256)S(1)}, f32[256]{0:T(256)S(1)}, u32[]{:S(2)}, u32[]{:S(2)}) collective-permute-start(f32[256]{0:T(256)S(1)} %bitcast.255), channel_id=1, source_target_pairs={{1,0},{2,1},{3,2},{4,3},{5,4},{6,5},{7,6},{8,7},{9,8},{10,9},{11,1... | collective-permute-start | bytes 3080 | tf_op jit(solution)/shard_map/ppermute | solution.py:194
  142.4 28.2 %collective-permute-start = (f32[256,256]{0,1:T(8,128)S(1)}, f32[256,256]{0,1:T(8,128)S(1)}, u32[]{:S(2)}, u32[]{:S(2)}) collective-permute-start(f32[256,256]{0,1:T(8,128)S(1)} %get-tuple-element.136), channel_id=1, source_target_pairs={{1,0},{2,1},{3,2},{4,3},{5,4},{6,5},{7,6},{8,7},{9,8},{10,9},{11,1... | collective-permute-start | bytes 786440 | tf_op jit(solution)/shard_map/ppermute | solution.py:194
  167.0 54.3 %collective-permute-start.4 = (f32[256]{0:T(256)S(1)}, f32[256]{0:T(256)S(1)}, u32[]{:S(2)}, u32[]{:S(2)}) collective-permute-start(f32[256]{0:T(256)S(1)} %add.183), channel_id=1, source_target_pairs={{2,0},{3,1},{4,2},{5,3},{6,4},{7,5},{8,6},{9,7},{10,8},{11,9},{12,... | collective-permute-start | bytes 3080 | tf_op jit(solution)/shard_map/ppermute | solution.py:194
  169.3 57.7 %collective-permute-start.8 = (f32[256,256]{1,0:T(8,128)S(1)}, f32[256,256]{1,0:T(8,128)S(1)}, u32[]{:S(2)}, u32[]{:S(2)}) collective-permute-start(f32[256,256]{1,0:T(8,128)S(1)} %convolution_add_fusion.3), channel_id=1, source_target_pairs={{2,0},{3,1},{4,2},{5,3},{6,4},{7,5},{8,6},{9,7},{10,8},{11,9},{12,... | collective-permute-start | bytes 786440 | tf_op jit(solution)/shard_map/ppermute | solution.py:194
  171.2 58.6 %collective-permute-start.1 = (f32[256,256]{1,0:T(8,128)S(1)}, f32[256,256]{1,0:T(8,128)S(1)}, u32[]{:S(2)}, u32[]{:S(2)}) collective-permute-start(f32[256,256]{1,0:T(8,128)S(1)} %fusion.59), channel_id=1, source_target_pairs={{2,0},{3,1},{4,2},{5,3},{6,4},{7,5},{8,6},{9,7},{10,8},{11,9},{12,... | collective-permute-start | bytes 786440 | tf_op jit(solution)/shard_map/ppermute | solution.py:194
  221.5 99.9 %collective-permute-start.5 = (f32[256]{0:T(256)S(1)}, f32[256]{0:T(256)S(1)}, u32[]{:S(2)}, u32[]{:S(2)}) collective-permute-start(f32[256]{0:T(256)S(1)} %add.184), channel_id=1, source_target_pairs={{4,0},{5,1},{6,2},{7,3},{8,4},{9,5},{10,6},{11,7},{12,8},{13,9},{1... | collective-permute-start | bytes 3080 | tf_op jit(solution)/shard_map/ppermute | solution.py:194
  227.8 102.6 %collective-permute-start.9 = (f32[256,256]{1,0:T(8,128)S(1)}, f32[256,256]{1,0:T(8,128)S(1)}, u32[]{:S(2)}, u32[]{:S(2)}) collective-permute-start(f32[256,256]{1,0:T(8,128)S(1)} %convolution_add_fusion.2), channel_id=1, source_target_pairs={{4,0},{5,1},{6,2},{7,3},{8,4},{9,5},{10,6},{11,7},{12,8},{13,9},{1... | collective-permute-start | bytes 786440 | tf_op jit(solution)/shard_map/ppermute | solution.py:194
  230.2 103.1 %collective-permute-start.2 = (f32[256,256]{1,0:T(8,128)S(1)}, f32[256,256]{1,0:T(8,128)S(1)}, u32[]{:S(2)}, u32[]{:S(2)}) collective-permute-start(f32[256,256]{1,0:T(8,128)S(1)} %fusion.60), channel_id=1, source_target_pairs={{4,0},{5,1},{6,2},{7,3},{8,4},{9,5},{10,6},{11,7},{12,8},{13,9},{1... | collective-permute-start | bytes 786440 | tf_op jit(solution)/shard_map/ppermute | solution.py:194
  321.7 156.9 %collective-permute-start.6 = (f32[256]{0:T(256)S(1)}, f32[256]{0:T(256)S(1)}, u32[]{:S(2)}, u32[]{:S(2)}) collective-permute-start(f32[256]{0:T(256)S(1)} %add.185), channel_id=1, source_target_pairs={{8,0},{9,1},{10,2},{11,3},{12,4},{13,5},{14,6},{15,7},{24,16},{25,... | collective-permute-start | bytes 3080 | tf_op jit(solution)/shard_map/ppermute | solution.py:194
  331.2 165.2 %collective-permute-start.10 = (f32[256,256]{1,0:T(8,128)S(1)}, f32[256,256]{1,0:T(8,128)S(1)}, u32[]{:S(2)}, u32[]{:S(2)}) collective-permute-start(f32[256,256]{1,0:T(8,128)S(1)} %convolution_add_fusion.1), channel_id=1, source_target_pairs={{8,0},{9,1},{10,2},{11,3},{12,4},{13,5},{14,6},{15,7},{24,16},{25,... | collective-permute-start | bytes 786440 | tf_op jit(solution)/shard_map/ppermute | solution.py:194

commit v2 on v1

--- a/solution.py
+++ b/solution.py
@@ -1,10 +1,57 @@
 import jax
 import jax.numpy as jnp
 from jax import lax
+from jax.experimental import pallas as pl
+from jax.experimental.pallas import tpu as pltpu
 from jax.sharding import PartitionSpec as P
 
 HIGHEST = lax.Precision.HIGHEST
 JITTER = 0.001
+PANEL = 32
+
+
+def _sweep_kernel(a_ref, o_ref):
+    n = a_ref.shape[0]
+    o_ref[...] = a_ref[...]
+    sub = lax.broadcasted_iota(jnp.int32, (PANEL, n), 0)
+    lane = lax.broadcasted_iota(jnp.int32, (PANEL, n), 1)
+    sub_col = lax.broadcasted_iota(jnp.int32, (PANEL, 1), 0)
+    lane_full = lax.broadcasted_iota(jnp.int32, (n, n), 1)
+    for blk in range(n // PANEL):
+        base = blk * PANEL
+        orig = o_ref[base:base + PANEL, :]
+        panel = orig
+        for t in range(PANEL):
+            is_row = sub == t
+            is_col = lane == base + t
+            colv = jnp.sum(jnp.where(is_col, panel, 0.0), axis=1, keepdims=True)
+            rowv = jnp.sum(jnp.where(is_row, panel, 0.0), axis=0, keepdims=True)
+            pivot = jnp.sum(jnp.where(sub_col == t, colv, 0.0), axis=0, keepdims=True)
+            inv = 1.0 / pivot
+            scaled_row = rowv * inv
+            panel = jnp.where(
+                is_row,
+                jnp.where(is_col, -inv, scaled_row),
+                jnp.where(is_col, colv * inv, panel - colv * scaled_row),
+            )
+        full = o_ref[...]
+        update = lax.dot_general(
+            orig, panel, (((0,), (0,)), ((), ())), precision=HIGHEST,
+            preferred_element_type=jnp.float32,
+        )
+        in_block = (lane_full >= base) & (lane_full < base + PANEL)
+        o_ref[...] = jnp.where(in_block, 0.0, full) - update
+        o_ref[base:base + PANEL, :] = panel
+
+
+def neg_inverse(matrix):
+    size = matrix.shape[-1]
+    return pl.pallas_call(
+        _sweep_kernel,
+        out_shape=jax.ShapeDtypeStruct((size, size), jnp.float32),
+        in_specs=[pl.BlockSpec(memory_space=pltpu.VMEM)],
+        out_specs=pl.BlockSpec(memory_space=pltpu.VMEM),
+    )(matrix)
 
 
 def matmul_hi(left, right):
@@ -71,25 +118,23 @@
 def kalman_update(mean_pred, cov_pred, obs, root):
     points = obs.shape[-1]
     normal = jnp.eye(points, dtype=jnp.float32) + root[:, None] * cov_pred[:points, :points] * root[None, :]
-    factor = jnp.linalg.cholesky(normal)
+    neg_inv = neg_inverse(normal)
     innovation = root * (obs - mean_pred[:points])
-    rhs = jnp.concatenate([root[:, None] * cov_pred[:points, :], innovation[:, None]], axis=1)
-    half = lax.linalg.triangular_solve(factor, rhs, left_side=True, lower=True)
-    gain_half = half[:, :-1]
-    cov_new = cov_pred - matmul_hi(swap_last(gain_half), gain_half)
-    mean_new = mean_pred + matmul_hi(swap_last(gain_half), half[:, -1])
+    scaled = root[:, None] * cov_pred[:points, :]
+    rhs = jnp.concatenate([scaled, innovation[:, None]], axis=1)
+    solved = matmul_hi(neg_inv, rhs)
+    correction = matmul_hi(swap_last(scaled), solved)
+    cov_new = cov_pred + correction[:, :-1]
+    mean_new = mean_pred - correction[:, -1]
     return mean_new, cov_new
 
 
 def smoother_elements(means, covs, last_flag, transit, process):
     forward_cov = apply_trans(transit, covs)
     predicted = apply_trans(transit, swap_last(forward_cov)) + process
-    factor = jnp.linalg.cholesky(predicted)
-    half_solve = lax.linalg.triangular_solve(factor, forward_cov, left_side=True, lower=True)
-    gain_t = lax.linalg.triangular_solve(
-        factor, half_solve, left_side=True, lower=True, transpose_a=True
-    )
-    gains = swap_last(gain_t) * (1.0 - last_flag.astype(jnp.float32))[:, None, None]
+    neg_inv = jax.vmap(neg_inverse)(predicted)
+    gains = -matmul_hi(swap_last(forward_cov), neg_inv)
+    gains = gains * (1.0 - last_flag.astype(jnp.float32))[:, None, None]
     forward_mean = apply_trans(transit, means[..., None])
     shift_means = means - matmul_hi(gains, forward_mean)[..., 0]
     shift_covs = covs - matmul_hi(gains, forward_cov)

time: 505 us -> 384 us (0.76); the launches traced: 498 us -> 383 us
  other arithmetic: 100 us -> 3.75 us
  waiting for transfers between devices: 336 us -> 261 us
  Pallas kernels: 0 us -> 62.5 us
    another operation x19 -> x0, other arithmetic: 99.4 us -> none  [the longest x6 34 us: smoother_elements(): factor = jnp.linalg.cholesky(predicted)]
    ppermute x11, waiting for transfers between devices: 336 us -> 261 us  [shards(): received = lax.ppermute(running, 'tm', pairs)]
    pallas_call x0 -> x3, Pallas kernels: none -> 62.5 us  [neg_inverse(): pl.pallas_call(_sweep_kernel, out_shape=jax.ShapeDtypeStruct((size, size)...]
    dot_general x21 -> x22, matrix products: 9.03 us -> 11.3 us  [matmul_hi(): return jnp.matmul(left, right, precision=HIGHEST)]
where the time goes in v2:
time: 384 us; the launch traced here: 383 us
  waiting for transfers between devices  261 us (68%)
  Pallas kernels  62.5 us (16%)
  blocking collectives  23 us (6%)
  starting transfers between devices  16.5 us (4%)
  matrix products  11.3 us (3%)
    ppermute x11, waiting for transfers between devices, shards(): received = lax.ppermute(running, 'tm', pairs)  261 us
    pallas_call x3, Pallas kernels, neg_inverse(): pl.pallas_call(_sweep_kernel, out_shape=jax.ShapeDtypeStruct((size, size)...  62.5 us
    all_gather x1, blocking collectives, shards(): gathered = lax.all_gather(packed, 'tm', tiled=True)  23 us
    ppermute x11, starting transfers between devices, shards(): received = lax.ppermute(running, 'tm', pairs)  16.5 us
    dot_general x22, matrix products, matmul_hi(): return jnp.matmul(left, right, precision=HIGHEST)  11.3 us
  transfers between devices with their start and end apart: 11, of which 9 were waited for; matrix products, arithmetic and copies ran while one was open for 1% of the time, Pallas kernels for 0%

profile of v2, /device:TPU:1, one launch (start us, length us, event | category | flops | bytes accessed | tf_op | source)
XLA Modules:
  0.0 382.6 jit_solution(6030724286483625121)
XLA Ops:
  0.7 0.6 copy-done.3
  1.3 0.7 pad_maximum_fusion.3
  2.0 23.0 %all_gather.3 = f32[16,2,128]{2,1,0:T(2,128)S(1)} all-gather(f32[1,2,128]{2,1,0:T(2,128)S(1)} %pad_maximum_fusion.3), channel_id=1, replica_groups=mesh['groups'=2,'tm'=16] {'tm'}, dimensions={0}, use_global_device_ids=true | all-gather | bytes 17408 | tf_op jit(solution)/shard_map/all_gather | solution.py:164
  25.0 0.6 copy-done.2
  25.8 0.7 multiply_multiply_fusion.1
  26.5 15.5 %shard_map.68 = f32[128,128]{1,0:T(8,128)} custom-call(f32[128,128]{1,0:T(8,128)} %get-tuple-element.204.a_ref), custom_call_target="tpu_custom_call" | custom-call | tf_op jit(solution)/shard_map/pallas_call | solution.py:49
  42.1 1.1 fusion.22
  43.2 0.5 fusion.26
  43.9 18.9 %while.12 = (s32[]{:T(128)}, f32[256]{0:T(256)S(1)}, f32[256,256]{1,0:T(8,128)S(1)}, s32[]{:T(128)}, f32[128]{0:T(128)S(1)}, /*index=5*/f32[128]{0:T(128)S(1)}, ...) while((s32[]{:T(128)}, f32[256]{0:T(256)S(1)}, ...), condition=%wide.region_1.2_spmd, body=%wide.region_0.1_spmd.sunk | while | flops 152389248 | bytes 6769363 | solution.py:184
  44.7 0.7 fusion.98.a_ref
  45.4 15.5 %body.1 = f32[128,128]{1,0:T(8,128)} custom-call(f32[128,128]{1,0:T(8,128)} %fusion.98.a_ref), custom_call_target="tpu_custom_call" | custom-call | tf_op jit(solution)/shard_map/while/body/pallas_call | solution.py:49
  61.0 0.8 copy-done
  62.1 0.5 fusion.101
  62.8 35.1 %conditional.1 = (f32[1,256]{1,0:T(1,128)S(1)}, f32[256,256]{1,0:T(8,128)S(1)}, f32[1,256,256]{2,1,0:T(8,128)S(1)}) conditional(s32[]{:T(128)} %convert_element_type.18, (f32[128]{0:T(128)S(1)}, f32[1,256,256]{2,1,0:T(8,128)S(1)}, f32[128]{0:T(128)S(1)}, f32[128]{0:T(128)S(1)}, f32[128]{0:T(128)S(1)}, /*index=5*/f32[256,256]{1,0:T(8,128)S(1)}, ...), branch_computations={%region_2.3_spmd, %region_3.4_spmd} | conditional | flops 404358400 | bytes 5516342 | solution.py:213
  63.6 0.7 maximum_add_fusion.1.a_ref
  64.3 31.4 %vmap__.2 = f32[256,256]{1,0:T(8,128)} custom-call(f32[256,256]{1,0:T(8,128)} %maximum_add_fusion.1.a_ref), custom_call_target="tpu_custom_call" | custom-call | tf_op jit(solution)/shard_map/cond/branch_0_fun/vmap()/pallas_call | solution.py:49
  95.7 1.5 fusion.9
  97.3 0.4 fusion.10
  98.0 2.0 collective-permute-start.7
  99.9 1.9 collective-permute-start.3
  101.9 1.9 collective-permute-start
  103.8 16.7 %collective-permute-done.3 = f32[256]{0:T(256)S(1)} collective-permute-done((f32[256]{0:T(256)S(1)}, f32[256]{0:T(256)S(1)}, u32[]{:S(2)}, u32[]{:S(2)}) %collective-permute-start.3) | collective-permute-done | bytes 1056 | tf_op jit(solution)/shard_map/ppermute | solution.py:239
  120.8 1.3 collective-permute-start.4
  122.1 0.4 fusion.42
  122.5 0.4 convolution_add_fusion.3
  122.9 1.5 collective-permute-start.8
  124.5 0.4 fusion.36
  124.9 1.3 collective-permute-start.1
  126.2 37.4 %collective-permute-done.4 = f32[256]{0:T(256)S(1)} collective-permute-done((f32[256]{0:T(256)S(1)}, f32[256]{0:T(256)S(1)}, u32[]{:S(2)}, u32[]{:S(2)}) %collective-permute-start.4) | collective-permute-done | bytes 1056 | tf_op jit(solution)/shard_map/ppermute | solution.py:239
  163.8 1.3 collective-permute-start.5
  165.2 3.9 %collective-permute-done.8 = f32[256,256]{1,0:T(8,128)S(1)} collective-permute-done((f32[256,256]{1,0:T(8,128)S(1)}, f32[256,256]{1,0:T(8,128)S(1)}, u32[]{:S(2)}, u32[]{:S(2)}) %collective-permute-start.8) | collective-permute-done | bytes 262176 | tf_op jit(solution)/shard_map/ppermute | solution.py:239
  169.1 0.4 fusion.43
  169.5 0.4 convolution_add_fusion.2
  169.9 1.3 collective-permute-start.9
  171.2 0.7 collective-permute-done.1
  172.3 1.3 collective-permute-start.2
  173.6 67.1 %collective-permute-done.5 = f32[256]{0:T(256)S(1)} collective-permute-done((f32[256]{0:T(256)S(1)}, f32[256]{0:T(256)S(1)}, u32[]{:S(2)}, u32[]{:S(2)}) %collective-permute-start.5) | collective-permute-done | bytes 1056 | tf_op jit(solution)/shard_map/ppermute | solution.py:239
  241.0 1.3 collective-permute-start.6
  242.3 7.2 %collective-permute-done.9 = f32[256,256]{1,0:T(8,128)S(1)} collective-permute-done((f32[256,256]{1,0:T(8,128)S(1)}, f32[256,256]{1,0:T(8,128)S(1)}, u32[]{:S(2)}, u32[]{:S(2)}) %collective-permute-start.9) | collective-permute-done | bytes 262176 | tf_op jit(solution)/shard_map/ppermute | solution.py:239
  249.9 0.4 convolution_add_fusion.1
  250.4 1.3 collective-permute-start.10
  251.7 0.7 collective-permute-done.2
  252.4 0.4 fusion.38
  252.8 110.5 %collective-permute-done.6 = f32[256]{0:T(256)S(1)} collective-permute-done((f32[256]{0:T(256)S(1)}, f32[256]{0:T(256)S(1)}, u32[]{:S(2)}, u32[]{:S(2)}) %collective-permute-start.6) | collective-permute-done | bytes 1056 | tf_op jit(solution)/shard_map/ppermute | solution.py:239
  363.3 0.9 convolution_add_fusion.4
  364.2 17.0 %collective-permute-done.10 = f32[256,256]{1,0:T(8,128)S(1)} collective-permute-done((f32[256,256]{1,0:T(8,128)S(1)}, f32[256,256]{1,0:T(8,128)S(1)}, u32[]{:S(2)}, u32[]{:S(2)}) %collective-permute-start.10) | collective-permute-done | bytes 262176 | tf_op jit(solution)/shard_map/ppermute | solution.py:239
  381.1 0.4 fusion.45
  381.5 1.1 fusion.21
  (51 shorter events, 4.0 us)
Async XLA Ops:
  0.6 0.7 copy-start.3
  0.6 0.7 copy-start.4
  0.7 25.0 %copy-start.1 = (f32[128,128]{1,0:T(8,128)S(1)}, f32[128,128]{1,0:T(8,128)}, u32[]{:S(2)}) copy-start(f32[128,128]{1,0:T(8,128)} %param.13) | copy-start | bytes 196612
  25.0 0.7 copy-start.2
  60.9 0.8 copy-start
  98.0 24.2 %collective-permute-start.7 = (f32[256,256]{1,0:T(8,128)S(1)}, f32[256,256]{1,0:T(8,128)S(1)}, u32[]{:S(2)}, u32[]{:S(2)}) collective-permute-start(f32[256,256]{1,0:T(8,128)S(1)} %bitcast.147), channel_id=1, source_target_pairs={{1,0},{2,1},{3,2},{4,3},{5,4},{6,5},{7,6},{8,7},{9,8},{10,9},{11,1... | collective-permute-start | bytes 786440 | tf_op jit(solution)/shard_map/ppermute | solution.py:239
  99.9 20.6 %collective-permute-start.3 = (f32[256]{0:T(256)S(1)}, f32[256]{0:T(256)S(1)}, u32[]{:S(2)}, u32[]{:S(2)}) collective-permute-start(f32[256]{0:T(256)S(1)} %bitcast.159), channel_id=1, source_target_pairs={{1,0},{2,1},{3,2},{4,3},{5,4},{6,5},{7,6},{8,7},{9,8},{10,9},{11,1... | collective-permute-start | bytes 3080 | tf_op jit(solution)/shard_map/ppermute | solution.py:239
  101.9 22.6 %collective-permute-start = (f32[256,256]{1,0:T(8,128)S(1)}, f32[256,256]{1,0:T(8,128)S(1)}, u32[]{:S(2)}, u32[]{:S(2)}) collective-permute-start(f32[256,256]{1,0:T(8,128)S(1)} %get-tuple-element.134), channel_id=1, source_target_pairs={{1,0},{2,1},{3,2},{4,3},{5,4},{6,5},{7,6},{8,7},{9,8},{10,9},{11,1... | collective-permute-start | bytes 786440 | tf_op jit(solution)/shard_map/ppermute | solution.py:239
  120.8 42.8 %collective-permute-start.4 = (f32[256]{0:T(256)S(1)}, f32[256]{0:T(256)S(1)}, u32[]{:S(2)}, u32[]{:S(2)}) collective-permute-start(f32[256]{0:T(256)S(1)} %add.147), channel_id=1, source_target_pairs={{2,0},{3,1},{4,2},{5,3},{6,4},{7,5},{8,6},{9,7},{10,8},{11,9},{12,... | collective-permute-start | bytes 3080 | tf_op jit(solution)/shard_map/ppermute | solution.py:239
  122.9 46.2 %collective-permute-start.8 = (f32[256,256]{1,0:T(8,128)S(1)}, f32[256,256]{1,0:T(8,128)S(1)}, u32[]{:S(2)}, u32[]{:S(2)}) collective-permute-start(f32[256,256]{1,0:T(8,128)S(1)} %convolution_add_fusion.3), channel_id=1, source_target_pairs={{2,0},{3,1},{4,2},{5,3},{6,4},{7,5},{8,6},{9,7},{10,8},{11,9},{12,... | collective-permute-start | bytes 786440 | tf_op jit(solution)/shard_map/ppermute | solution.py:239
  124.9 47.1 %collective-permute-start.1 = (f32[256,256]{1,0:T(8,128)S(1)}, f32[256,256]{1,0:T(8,128)S(1)}, u32[]{:S(2)}, u32[]{:S(2)}) collective-permute-start(f32[256,256]{1,0:T(8,128)S(1)} %fusion.36), channel_id=1, source_target_pairs={{2,0},{3,1},{4,2},{5,3},{6,4},{7,5},{8,6},{9,7},{10,8},{11,9},{12,... | collective-permute-start | bytes 786440 | tf_op jit(solution)/shard_map/ppermute | solution.py:239
  163.8 76.9 %collective-permute-start.5 = (f32[256]{0:T(256)S(1)}, f32[256]{0:T(256)S(1)}, u32[]{:S(2)}, u32[]{:S(2)}) collective-permute-start(f32[256]{0:T(256)S(1)} %add.148), channel_id=1, source_target_pairs={{4,0},{5,1},{6,2},{7,3},{8,4},{9,5},{10,6},{11,7},{12,8},{13,9},{1... | collective-permute-start | bytes 3080 | tf_op jit(solution)/shard_map/ppermute | solution.py:239
  169.9 79.6 %collective-permute-start.9 = (f32[256,256]{1,0:T(8,128)S(1)}, f32[256,256]{1,0:T(8,128)S(1)}, u32[]{:S(2)}, u32[]{:S(2)}) collective-permute-start(f32[256,256]{1,0:T(8,128)S(1)} %convolution_add_fusion.2), channel_id=1, source_target_pairs={{4,0},{5,1},{6,2},{7,3},{8,4},{9,5},{10,6},{11,7},{12,8},{13,9},{1... | collective-permute-start | bytes 786440 | tf_op jit(solution)/shard_map/ppermute | solution.py:239
  172.3 80.1 %collective-permute-start.2 = (f32[256,256]{1,0:T(8,128)S(1)}, f32[256,256]{1,0:T(8,128)S(1)}, u32[]{:S(2)}, u32[]{:S(2)}) collective-permute-start(f32[256,256]{1,0:T(8,128)S(1)} %fusion.37), channel_id=1, source_target_pairs={{4,0},{5,1},{6,2},{7,3},{8,4},{9,5},{10,6},{11,7},{12,8},{13,9},{1... | collective-permute-start | bytes 786440 | tf_op jit(solution)/shard_map/ppermute | solution.py:239
  241.0 122.3 %collective-permute-start.6 = (f32[256]{0:T(256)S(1)}, f32[256]{0:T(256)S(1)}, u32[]{:S(2)}, u32[]{:S(2)}) collective-permute-start(f32[256]{0:T(256)S(1)} %add.149), channel_id=1, source_target_pairs={{8,0},{9,1},{10,2},{11,3},{12,4},{13,5},{14,6},{15,7},{24,16},{25,... | collective-permute-start | bytes 3080 | tf_op jit(solution)/shard_map/ppermute | solution.py:239
  250.4 130.8 %collective-permute-start.10 = (f32[256,256]{1,0:T(8,128)S(1)}, f32[256,256]{1,0:T(8,128)S(1)}, u32[]{:S(2)}, u32[]{:S(2)}) collective-permute-start(f32[256,256]{1,0:T(8,128)S(1)} %convolution_add_fusion.1), channel_id=1, source_target_pairs={{8,0},{9,1},{10,2},{11,3},{12,4},{13,5},{14,6},{15,7},{24,16},{25,... | collective-permute-start | bytes 786440 | tf_op jit(solution)/shard_map/ppermute | solution.py:239

commit v3 on v2

--- a/solution.py
+++ b/solution.py
@@ -11,8 +11,12 @@
 
 
 def _sweep_kernel(a_ref, o_ref):
-    n = a_ref.shape[0]
     o_ref[...] = a_ref[...]
+    _sweep_in_place(o_ref)
+
+
+def _sweep_in_place(o_ref):
+    n = o_ref.shape[0]
     sub = lax.broadcasted_iota(jnp.int32, (PANEL, n), 0)
     lane = lax.broadcasted_iota(jnp.int32, (PANEL, n), 1)
     sub_col = lax.broadcasted_iota(jnp.int32, (PANEL, 1), 0)
@@ -54,6 +58,83 @@
     )(matrix)
 
 
+def _filter_kernel(
+    count_ref, obs_ref, root_row_ref, root_col_ref, trans_row_ref, trans_col_ref, process_ref,
+    prior_ref, mean_ref, cov_ref, pred_ref, normal_ref,
+):
+    points = obs_ref.shape[1]
+    eye = (
+        lax.broadcasted_iota(jnp.int32, (points, points), 0)
+        == lax.broadcasted_iota(jnp.int32, (points, points), 1)
+    ).astype(jnp.float32)
+    cov_ref[...] = prior_ref[...]
+    a_col, b_col, c_col, d_col = (trans_col_ref[i] for i in range(4))
+    a_row, b_row, c_row, d_row = (trans_row_ref[i:i + 1, :] for i in range(4))
+
+    def step(t, mean):
+        first = t == 0
+        top = cov_ref[:points, :]
+        bottom = cov_ref[points:, :]
+        for rows, left_w, right_w in ((slice(0, points), a_col, b_col), (slice(points, None), c_col, d_col)):
+            forward = left_w * top + right_w * bottom
+            f_left = forward[:, :points]
+            f_right = forward[:, points:]
+            pred_ref[rows, :points] = f_left * a_row + f_right * b_row
+            pred_ref[rows, points:] = f_left * c_row + f_right * d_row
+        cov_pred = jnp.where(first, prior_ref[...], pred_ref[...] + process_ref[...])
+        m_top = mean[:, :points]
+        m_bottom = mean[:, points:]
+        mean_fwd = jnp.concatenate(
+            [a_row * m_top + b_row * m_bottom, c_row * m_top + d_row * m_bottom], axis=1
+        )
+        mean_pred = jnp.where(first, 0.0, mean_fwd)
+        r_col = root_col_ref[t]
+        r_row = root_row_ref[pl.ds(t, 1), :]
+        obs_row = obs_ref[pl.ds(t, 1), :]
+        normal_ref[...] = eye + r_col * cov_pred[:points, :points] * r_row
+        _sweep_in_place(normal_ref)
+        scaled = r_col * cov_pred[:points, :]
+        solved = jnp.dot(normal_ref[...], scaled, precision=HIGHEST, preferred_element_type=jnp.float32)
+        correction = lax.dot_general(
+            scaled, solved, (((0,), (0,)), ((), ())), precision=HIGHEST,
+            preferred_element_type=jnp.float32,
+        )
+        cov_ref[...] = cov_pred + correction
+        innovation = jnp.broadcast_to(r_row * (obs_row - mean_pred[:, :points]), (8, points))
+        mean_shift = jnp.dot(innovation, solved, precision=HIGHEST, preferred_element_type=jnp.float32)
+        return mean_pred - mean_shift[0:1, :]
+
+    mean_ref[...] = lax.fori_loop(0, count_ref[0], step, jnp.zeros((1, 2 * points), jnp.float32))
+
+
+def run_filter(count, obs_all, root_all, transit, process, prior):
+    total, points = obs_all.shape
+    width = 2 * points
+    vmem = pl.BlockSpec(memory_space=pltpu.VMEM)
+    return pl.pallas_call(
+        _filter_kernel,
+        out_shape=(
+            jax.ShapeDtypeStruct((1, width), jnp.float32),
+            jax.ShapeDtypeStruct((width, width), jnp.float32),
+        ),
+        in_specs=[pl.BlockSpec(memory_space=pltpu.SMEM)] + [vmem] * 7,
+        out_specs=(vmem, vmem),
+        scratch_shapes=[
+            pltpu.VMEM((width, width), jnp.float32),
+            pltpu.VMEM((points, points), jnp.float32),
+        ],
+    )(
+        jnp.reshape(count, (1,)).astype(jnp.int32),
+        obs_all,
+        root_all,
+        root_all[:, :, None],
+        transit,
+        transit[:, :, None],
+        process,
+        prior,
+    )
+
+
 def matmul_hi(left, right):
     return jnp.matmul(left, right, precision=HIGHEST)
 
@@ -165,9 +246,6 @@
     obs_all = gathered[:, 0]
     root_all = gathered[:, 1]
 
-    mean_first, cov_first = kalman_update(
-        jnp.zeros((width,), jnp.float32), prior, obs_all[0], root_all[0]
-    )
     last_local = position * local_steps + (local_steps - 1)
 
     def filter_step(step, mean, cov):
@@ -177,14 +255,13 @@
         return kalman_update(mean_pred, cov_pred, obs_now, root_now)
 
     if local_steps == 1:
-
-        def body(step, carry):
-            return filter_step(step, carry[0], carry[1])
-
-        mean_last, cov_last = lax.fori_loop(1, last_local + 1, body, (mean_first, cov_first))
-        means = mean_last[None]
+        mean_last, cov_last = run_filter(position + 1, obs_all, root_all, transit, process, prior)
+        means = mean_last
         covs = cov_last[None]
     else:
+        mean_first, cov_first = kalman_update(
+            jnp.zeros((width,), jnp.float32), prior, obs_all[0], root_all[0]
+        )
         mean_buf = jnp.zeros((local_steps, width), jnp.float32).at[0].set(mean_first)
         cov_buf = jnp.zeros((local_steps, width, width), jnp.float32).at[0].set(cov_first)
 

time: 384 us -> 330 us (0.86)
  waiting for transfers between devices: 261 us -> 210 us
    ppermute x11, waiting for transfers between devices: 261 us -> 210 us  [shards(): received = lax.ppermute(running, 'tm', pairs)]
    pallas_call x0 -> x1, Pallas kernels: none -> 31.3 us  [run_filter(): pl.pallas_call(_filter_kernel, out_shape=(jax.ShapeDtypeStruct((1, width)...]
    pallas_call x3 -> x1, Pallas kernels: 62.5 us -> 31.4 us  [neg_inverse(): pl.pallas_call(_sweep_kernel, out_shape=jax.ShapeDtypeStruct((size, size)...]
    dot_general x22 -> x18, matrix products: 11.3 us -> 8.89 us  [matmul_hi(): return jnp.matmul(left, right, precision=HIGHEST)]
  transfers between devices with their start and end apart: 11 -> 11, of which waited for: 9 -> 9; matrix products, arithmetic and copies ran while one was open for 1% -> 2% of each run, Pallas kernels for 0% -> 0%
where the time goes in v3:
time: 330 us; the launch traced here: 329 us
  waiting for transfers between devices  210 us (64%)
  Pallas kernels  62.7 us (19%)
  blocking collectives  23 us (7%)
  starting transfers between devices  16.5 us (5%)
  matrix products  8.89 us (3%)
  local copies, waits for them, and re-layouts  4.36 us (1%)
    ppermute x11, waiting for transfers between devices, shards(): received = lax.ppermute(running, 'tm', pairs)  210 us
    pallas_call x1, Pallas kernels, neg_inverse(): pl.pallas_call(_sweep_kernel, out_shape=jax.ShapeDtypeStruct((size, size)...  31.4 us
    pallas_call x1, Pallas kernels, run_filter(): pl.pallas_call(_filter_kernel, out_shape=(jax.ShapeDtypeStruct((1, width)...  31.3 us
    all_gather x1, blocking collectives, shards(): gathered = lax.all_gather(packed, 'tm', tiled=True)  23 us
    ppermute x11, starting transfers between devices, shards(): received = lax.ppermute(running, 'tm', pairs)  16.5 us
    dot_general x18, matrix products, matmul_hi(): return jnp.matmul(left, right, precision=HIGHEST)  8.89 us
  transfers between devices with their start and end apart: 11, of which 9 were waited for; matrix products, arithmetic and copies ran while one was open for 2% of the time, Pallas kernels for 0%

profile of v3, /device:TPU:1, one launch (start us, length us, event | category | flops | bytes accessed | tf_op | source)
XLA Modules:
  0.0 329.1 jit_solution(3219991922980315080)
XLA Ops:
  0.6 0.6 copy-done.2
  1.3 0.6 fusion.15
  1.9 0.9 copy.22.trans_col_ref
  2.8 0.7 copy-done.3
  3.5 23.0 %all_gather.3 = f32[16,2,128]{2,1,0:T(2,128)S(1)} all-gather(f32[1,2,128]{2,1,0:T(2,128)S(1)} %pad_maximum_fusion.4), channel_id=1, replica_groups=mesh['groups'=2,'tm'=16] {'tm'}, dimensions={0}, use_global_device_ids=true | all-gather | bytes 17408 | tf_op jit(solution)/shard_map/all_gather | solution.py:245
  26.4 0.6 fusion.17
  27.0 1.4 copy.21.root_col_ref
  28.5 0.7 select_maximum_fusion
  29.3 31.3 %shard_map.68 = (f32[1,256]{1,0:T(1,128)S(1)}, f32[256,256]{1,0:T(8,128)S(1)}) custom-call(s32[1]{0:T(128)} %bitcast.14.count_ref, f32[16,128]{1,0:T(8,128)} %bitcast.115, f32[16,128]{1,0:T(8,128)} %bitcast.114, f32[16,128,1]{2,1,0:T(8,128)} %copy.21.root_col_ref, f32[4,128]{1,0:T(4,128)} %get-tuple-element.92.trans_row_ref, ...), custom_call_target="tpu_custom_call" | custom-call | tf_op jit(solution)/shard_map/pallas_call | solution.py:114
  60.6 35.1 %conditional.1 = (f32[1,256]{1,0:T(1,128)S(1)}, f32[256,256]{1,0:T(8,128)S(1)}, f32[1,256,256]{2,1,0:T(8,128)S(1)}) conditional(s32[]{:T(128)} %convert_element_type.12, (f32[128]{0:T(128)S(1)}, f32[1,256,256]{2,1,0:T(8,128)S(1)}, f32[128]{0:T(128)S(1)}, f32[128]{0:T(128)S(1)}, f32[128]{0:T(128)S(1)}, /*index=5*/f32[256,256]{1,0:T(8,128)S(1)}, ...), branch_computations={%region_0.1_spmd, %region_1.2_spmd} | conditional | flops 404358400 | bytes 5516342 | solution.py:290
  61.3 0.7 maximum_add_fusion.a_ref
  62.0 31.4 %vmap__.2 = f32[256,256]{1,0:T(8,128)} custom-call(f32[256,256]{1,0:T(8,128)} %maximum_add_fusion.a_ref), custom_call_target="tpu_custom_call" | custom-call | tf_op jit(solution)/shard_map/cond/branch_0_fun/vmap()/pallas_call | solution.py:53
  93.5 1.5 fusion
  95.0 0.4 fusion.1
  95.4 0.3 convolution_subtract_fusion
  95.7 2.0 collective-permute-start.7
  97.7 1.9 collective-permute-start.3
  99.6 1.9 collective-permute-start
  101.5 12.7 %collective-permute-done.3 = f32[256]{0:T(256)S(1)} collective-permute-done((f32[256]{0:T(256)S(1)}, f32[256]{0:T(256)S(1)}, u32[]{:S(2)}, u32[]{:S(2)}) %collective-permute-start.3) | collective-permute-done | bytes 1056 | tf_op jit(solution)/shard_map/ppermute | solution.py:316
  114.3 0.3 fusion.21
  114.6 1.3 collective-permute-start.4
  115.9 0.4 fusion.24
  116.3 0.4 convolution_add_fusion.3
  116.7 1.5 collective-permute-start.8
  118.3 0.4 fusion.18
  118.6 1.3 collective-permute-start.1
  119.9 29.5 %collective-permute-done.4 = f32[256]{0:T(256)S(1)} collective-permute-done((f32[256]{0:T(256)S(1)}, f32[256]{0:T(256)S(1)}, u32[]{:S(2)}, u32[]{:S(2)}) %collective-permute-start.4) | collective-permute-done | bytes 1056 | tf_op jit(solution)/shard_map/ppermute | solution.py:316
  149.7 1.3 collective-permute-start.5
  151.1 3.9 %collective-permute-done.8 = f32[256,256]{1,0:T(8,128)S(1)} collective-permute-done((f32[256,256]{1,0:T(8,128)S(1)}, f32[256,256]{1,0:T(8,128)S(1)}, u32[]{:S(2)}, u32[]{:S(2)}) %collective-permute-start.8) | collective-permute-done | bytes 262176 | tf_op jit(solution)/shard_map/ppermute | solution.py:316
  155.0 0.4 fusion.25
  155.4 0.4 convolution_add_fusion.2
  155.8 1.3 collective-permute-start.9
  157.1 0.7 collective-permute-done.1
  157.8 0.4 fusion.19
  158.2 1.3 collective-permute-start.2
  159.5 51.3 %collective-permute-done.5 = f32[256]{0:T(256)S(1)} collective-permute-done((f32[256]{0:T(256)S(1)}, f32[256]{0:T(256)S(1)}, u32[]{:S(2)}, u32[]{:S(2)}) %collective-permute-start.5) | collective-permute-done | bytes 1056 | tf_op jit(solution)/shard_map/ppermute | solution.py:316
  211.1 1.3 collective-permute-start.6
  212.5 7.2 %collective-permute-done.9 = f32[256,256]{1,0:T(8,128)S(1)} collective-permute-done((f32[256,256]{1,0:T(8,128)S(1)}, f32[256,256]{1,0:T(8,128)S(1)}, u32[]{:S(2)}, u32[]{:S(2)}) %collective-permute-start.9) | collective-permute-done | bytes 262176 | tf_op jit(solution)/shard_map/ppermute | solution.py:316
  219.7 0.4 fusion.26
  220.1 0.4 convolution_add_fusion.1
  220.5 1.3 collective-permute-start.10
  221.8 0.7 collective-permute-done.2
  222.5 0.4 fusion.20
  222.9 86.8 %collective-permute-done.6 = f32[256]{0:T(256)S(1)} collective-permute-done((f32[256]{0:T(256)S(1)}, f32[256]{0:T(256)S(1)}, u32[]{:S(2)}, u32[]{:S(2)}) %collective-permute-start.6) | collective-permute-done | bytes 1056 | tf_op jit(solution)/shard_map/ppermute | solution.py:316
  309.7 0.9 convolution_add_fusion.4
  310.6 17.0 %collective-permute-done.10 = f32[256,256]{1,0:T(8,128)S(1)} collective-permute-done((f32[256,256]{1,0:T(8,128)S(1)}, f32[256,256]{1,0:T(8,128)S(1)}, u32[]{:S(2)}, u32[]{:S(2)}) %collective-permute-start.10) | collective-permute-done | bytes 262176 | tf_op jit(solution)/shard_map/ppermute | solution.py:316
  327.6 0.4 fusion.27
  328.0 1.1 fusion.12
  (28 shorter events, 1.2 us)
Async XLA Ops:
  0.6 0.7 copy-start.2
  1.9 0.9 copy-start.4
  1.9 0.9 copy-start.5
  2.8 0.7 copy-start.3
  27.0 1.4 copy-start.1
  27.0 1.4 copy-start
  95.7 20.2 %collective-permute-start.7 = (f32[256,256]{1,0:T(8,128)S(1)}, f32[256,256]{1,0:T(8,128)S(1)}, u32[]{:S(2)}, u32[]{:S(2)}) collective-permute-start(f32[256,256]{1,0:T(8,128)S(1)} %bitcast.112), channel_id=1, source_target_pairs={{1,0},{2,1},{3,2},{4,3},{5,4},{6,5},{7,6},{8,7},{9,8},{10,9},{11,1... | collective-permute-start | bytes 786440 | tf_op jit(solution)/shard_map/ppermute | solution.py:316
  97.7 16.6 %collective-permute-start.3 = (f32[256]{0:T(256)S(1)}, f32[256]{0:T(256)S(1)}, u32[]{:S(2)}, u32[]{:S(2)}) collective-permute-start(f32[256]{0:T(256)S(1)} %bitcast.122), channel_id=1, source_target_pairs={{1,0},{2,1},{3,2},{4,3},{5,4},{6,5},{7,6},{8,7},{9,8},{10,9},{11,1... | collective-permute-start | bytes 3080 | tf_op jit(solution)/shard_map/ppermute | solution.py:316
  99.6 18.6 %collective-permute-start = (f32[256,256]{1,0:T(8,128)S(1)}, f32[256,256]{1,0:T(8,128)S(1)}, u32[]{:S(2)}, u32[]{:S(2)}) collective-permute-start(f32[256,256]{1,0:T(8,128)S(1)} %get-tuple-element.72), channel_id=1, source_target_pairs={{1,0},{2,1},{3,2},{4,3},{5,4},{6,5},{7,6},{8,7},{9,8},{10,9},{11,1... | collective-permute-start | bytes 786440 | tf_op jit(solution)/shard_map/ppermute | solution.py:316
  114.6 34.9 %collective-permute-start.4 = (f32[256]{0:T(256)S(1)}, f32[256]{0:T(256)S(1)}, u32[]{:S(2)}, u32[]{:S(2)}) collective-permute-start(f32[256]{0:T(256)S(1)} %add.98), channel_id=1, source_target_pairs={{2,0},{3,1},{4,2},{5,3},{6,4},{7,5},{8,6},{9,7},{10,8},{11,9},{12,... | collective-permute-start | bytes 3080 | tf_op jit(solution)/shard_map/ppermute | solution.py:316
  116.7 38.3 %collective-permute-start.8 = (f32[256,256]{1,0:T(8,128)S(1)}, f32[256,256]{1,0:T(8,128)S(1)}, u32[]{:S(2)}, u32[]{:S(2)}) collective-permute-start(f32[256,256]{1,0:T(8,128)S(1)} %convolution_add_fusion.3), channel_id=1, source_target_pairs={{2,0},{3,1},{4,2},{5,3},{6,4},{7,5},{8,6},{9,7},{10,8},{11,9},{12,... | collective-permute-start | bytes 786440 | tf_op jit(solution)/shard_map/ppermute | solution.py:316
  118.6 39.2 %collective-permute-start.1 = (f32[256,256]{1,0:T(8,128)S(1)}, f32[256,256]{1,0:T(8,128)S(1)}, u32[]{:S(2)}, u32[]{:S(2)}) collective-permute-start(f32[256,256]{1,0:T(8,128)S(1)} %fusion.18), channel_id=1, source_target_pairs={{2,0},{3,1},{4,2},{5,3},{6,4},{7,5},{8,6},{9,7},{10,8},{11,9},{12,... | collective-permute-start | bytes 786440 | tf_op jit(solution)/shard_map/ppermute | solution.py:316
  149.7 61.1 %collective-permute-start.5 = (f32[256]{0:T(256)S(1)}, f32[256]{0:T(256)S(1)}, u32[]{:S(2)}, u32[]{:S(2)}) collective-permute-start(f32[256]{0:T(256)S(1)} %add.99), channel_id=1, source_target_pairs={{4,0},{5,1},{6,2},{7,3},{8,4},{9,5},{10,6},{11,7},{12,8},{13,9},{1... | collective-permute-start | bytes 3080 | tf_op jit(solution)/shard_map/ppermute | solution.py:316
  155.8 63.9 %collective-permute-start.9 = (f32[256,256]{1,0:T(8,128)S(1)}, f32[256,256]{1,0:T(8,128)S(1)}, u32[]{:S(2)}, u32[]{:S(2)}) collective-permute-start(f32[256,256]{1,0:T(8,128)S(1)} %convolution_add_fusion.2), channel_id=1, source_target_pairs={{4,0},{5,1},{6,2},{7,3},{8,4},{9,5},{10,6},{11,7},{12,8},{13,9},{1... | collective-permute-start | bytes 786440 | tf_op jit(solution)/shard_map/ppermute | solution.py:316
  158.2 64.3 %collective-permute-start.2 = (f32[256,256]{1,0:T(8,128)S(1)}, f32[256,256]{1,0:T(8,128)S(1)}, u32[]{:S(2)}, u32[]{:S(2)}) collective-permute-start(f32[256,256]{1,0:T(8,128)S(1)} %fusion.19), channel_id=1, source_target_pairs={{4,0},{5,1},{6,2},{7,3},{8,4},{9,5},{10,6},{11,7},{12,8},{13,9},{1... | collective-permute-start | bytes 786440 | tf_op jit(solution)/shard_map/ppermute | solution.py:316
  211.1 98.6 %collective-permute-start.6 = (f32[256]{0:T(256)S(1)}, f32[256]{0:T(256)S(1)}, u32[]{:S(2)}, u32[]{:S(2)}) collective-permute-start(f32[256]{0:T(256)S(1)} %add.100), channel_id=1, source_target_pairs={{8,0},{9,1},{10,2},{11,3},{12,4},{13,5},{14,6},{15,7},{24,16},{25,... | collective-permute-start | bytes 3080 | tf_op jit(solution)/shard_map/ppermute | solution.py:316
  220.5 107.1 %collective-permute-start.10 = (f32[256,256]{1,0:T(8,128)S(1)}, f32[256,256]{1,0:T(8,128)S(1)}, u32[]{:S(2)}, u32[]{:S(2)}) collective-permute-start(f32[256,256]{1,0:T(8,128)S(1)} %convolution_add_fusion.1), channel_id=1, source_target_pairs={{8,0},{9,1},{10,2},{11,3},{12,4},{13,5},{14,6},{15,7},{24,16},{25,... | collective-permute-start | bytes 786440 | tf_op jit(solution)/shard_map/ppermute | solution.py:316

commit v4 on v3

--- a/solution.py
+++ b/solution.py
@@ -25,19 +25,31 @@
         base = blk * PANEL
         orig = o_ref[base:base + PANEL, :]
         panel = orig
-        for t in range(PANEL):
-            is_row = sub == t
-            is_col = lane == base + t
-            colv = jnp.sum(jnp.where(is_col, panel, 0.0), axis=1, keepdims=True)
-            rowv = jnp.sum(jnp.where(is_row, panel, 0.0), axis=0, keepdims=True)
-            pivot = jnp.sum(jnp.where(sub_col == t, colv, 0.0), axis=0, keepdims=True)
-            inv = 1.0 / pivot
-            scaled_row = rowv * inv
-            panel = jnp.where(
-                is_row,
-                jnp.where(is_col, -inv, scaled_row),
-                jnp.where(is_col, colv * inv, panel - colv * scaled_row),
-            )
+        for t in range(0, PANEL, 2):
+            row_a = sub == t
+            row_b = sub == t + 1
+            col_a = lane == base + t
+            col_b = lane == base + t + 1
+            cv_a = jnp.sum(jnp.where(col_a, panel, 0.0), axis=1, keepdims=True)
+            cv_b = jnp.sum(jnp.where(col_b, panel, 0.0), axis=1, keepdims=True)
+            rv_a = jnp.sum(jnp.where(row_a, panel, 0.0), axis=0, keepdims=True)
+            rv_b = jnp.sum(jnp.where(row_b, panel, 0.0), axis=0, keepdims=True)
+            p = jnp.sum(jnp.where(sub_col == t, cv_a, 0.0), axis=0, keepdims=True)
+            q = jnp.sum(jnp.where(sub_col == t + 1, cv_a, 0.0), axis=0, keepdims=True)
+            s = jnp.sum(jnp.where(sub_col == t + 1, cv_b, 0.0), axis=0, keepdims=True)
+            idet = 1.0 / (p * s - q * q)
+            i_pp = s * idet
+            i_pq = -q * idet
+            i_ss = p * idet
+            nr_a = i_pp * rv_a + i_pq * rv_b
+            nr_b = i_pq * rv_a + i_ss * rv_b
+            nc_a = cv_a * i_pp + cv_b * i_pq
+            nc_b = cv_a * i_pq + cv_b * i_ss
+            rest = panel - cv_a * nr_a - cv_b * nr_b
+            rest = jnp.where(col_a, nc_a, jnp.where(col_b, nc_b, rest))
+            top = jnp.where(col_a, -i_pp, jnp.where(col_b, -i_pq, nr_a))
+            bot = jnp.where(col_a, -i_pq, jnp.where(col_b, -i_ss, nr_b))
+            panel = jnp.where(row_a, top, jnp.where(row_b, bot, rest))
         full = o_ref[...]
         update = lax.dot_general(
             orig, panel, (((0,), (0,)), ((), ())), precision=HIGHEST,

time: 330 us -> 228 us (0.69)
  waiting for transfers between devices: 210 us -> 132 us
  Pallas kernels: 62.7 us -> 39 us
    ppermute x11, waiting for transfers between devices: 210 us -> 132 us  [shards(): received = lax.ppermute(running, 'tm', pairs)]
    pallas_call x1, Pallas kernels: 31.3 us -> 19.2 us  [run_filter(): pl.pallas_call(_filter_kernel, out_shape=(jax.ShapeDtypeStruct((1, width)...]
    pallas_call x1, Pallas kernels: 31.4 us -> 19.8 us  [neg_inverse(): pl.pallas_call(_sweep_kernel, out_shape=jax.ShapeDtypeStruct((size, size)...]
  transfers between devices with their start and end apart: 11 -> 11, of which waited for: 9 -> 10; matrix products, arithmetic and copies ran while one was open for 2% -> 2% of each run, Pallas kernels for 0% -> 0%
where the time goes in v4:
time: 228 us; the launch traced here: 227 us
  waiting for transfers between devices  132 us (58%)
  Pallas kernels  39 us (17%)
  blocking collectives  23 us (10%)
  starting transfers between devices  16.5 us (7%)
  matrix products  8.89 us (4%)
  local copies, waits for them, and re-layouts  4.36 us (2%)
  other arithmetic  2.55 us (1%)
    ppermute x11, waiting for transfers between devices, shards(): received = lax.ppermute(running, 'tm', pairs)  132 us
    all_gather x1, blocking collectives, shards(): gathered = lax.all_gather(packed, 'tm', tiled=True)  23 us
    pallas_call x1, Pallas kernels, neg_inverse(): pl.pallas_call(_sweep_kernel, out_shape=jax.ShapeDtypeStruct((size, size)...  19.8 us
    pallas_call x1, Pallas kernels, run_filter(): pl.pallas_call(_filter_kernel, out_shape=(jax.ShapeDtypeStruct((1, width)...  19.2 us
    ppermute x11, starting transfers between devices, shards(): received = lax.ppermute(running, 'tm', pairs)  16.5 us
    dot_general x18, matrix products, matmul_hi(): return jnp.matmul(left, right, precision=HIGHEST)  8.89 us
  transfers between devices with their start and end apart: 11, of which 10 were waited for; matrix products, arithmetic and copies ran while one was open for 2% of the time, Pallas kernels for 0%

profile of v4, /device:TPU:1, one launch (start us, length us, event | category | flops | bytes accessed | tf_op | source)
XLA Modules:
  0.0 227.1 jit_solution(7867953168792788877)
XLA Ops:
  0.6 0.6 copy-done.2
  1.3 0.6 fusion.15
  1.9 0.9 copy.22.trans_col_ref
  2.8 0.7 copy-done.3
  3.5 23.0 %all_gather.3 = f32[16,2,128]{2,1,0:T(2,128)S(1)} all-gather(f32[1,2,128]{2,1,0:T(2,128)S(1)} %pad_maximum_fusion.4), channel_id=1, replica_groups=mesh['groups'=2,'tm'=16] {'tm'}, dimensions={0}, use_global_device_ids=true | all-gather | bytes 17408 | tf_op jit(solution)/shard_map/all_gather | solution.py:257
  26.4 0.6 fusion.17
  27.0 1.4 copy.21.root_col_ref
  28.5 0.7 select_maximum_fusion
  29.3 19.2 %shard_map.68 = (f32[1,256]{1,0:T(1,128)S(1)}, f32[256,256]{1,0:T(8,128)S(1)}) custom-call(s32[1]{0:T(128)} %bitcast.14.count_ref, f32[16,128]{1,0:T(8,128)} %bitcast.115, f32[16,128]{1,0:T(8,128)} %bitcast.114, f32[16,128,1]{2,1,0:T(8,128)} %copy.21.root_col_ref, f32[4,128]{1,0:T(4,128)} %get-tuple-element.92.trans_row_ref, ...), custom_call_target="tpu_custom_call" | custom-call | tf_op jit(solution)/shard_map/pallas_call | solution.py:126
  48.5 23.5 %conditional.1 = (f32[1,256]{1,0:T(1,128)S(1)}, f32[256,256]{1,0:T(8,128)S(1)}, f32[1,256,256]{2,1,0:T(8,128)S(1)}) conditional(s32[]{:T(128)} %convert_element_type.12, (f32[128]{0:T(128)S(1)}, f32[1,256,256]{2,1,0:T(8,128)S(1)}, f32[128]{0:T(128)S(1)}, f32[128]{0:T(128)S(1)}, f32[128]{0:T(128)S(1)}, /*index=5*/f32[256,256]{1,0:T(8,128)S(1)}, ...), branch_computations={%region_0.1_spmd, %region_1.2_spmd} | conditional | flops 404358400 | bytes 5516342 | solution.py:302
  49.3 0.7 maximum_add_fusion.a_ref
  50.0 19.8 %vmap__.2 = f32[256,256]{1,0:T(8,128)} custom-call(f32[256,256]{1,0:T(8,128)} %maximum_add_fusion.a_ref), custom_call_target="tpu_custom_call" | custom-call | tf_op jit(solution)/shard_map/cond/branch_0_fun/vmap()/pallas_call | solution.py:65
  69.8 1.5 fusion
  71.3 0.4 fusion.1
  71.8 0.3 convolution_subtract_fusion
  72.0 2.0 collective-permute-start.7
  74.0 1.9 collective-permute-start.3
  75.9 1.9 collective-permute-start
  77.9 6.7 %collective-permute-done.3 = f32[256]{0:T(256)S(1)} collective-permute-done((f32[256]{0:T(256)S(1)}, f32[256]{0:T(256)S(1)}, u32[]{:S(2)}, u32[]{:S(2)}) %collective-permute-start.3) | collective-permute-done | bytes 1056 | tf_op jit(solution)/shard_map/ppermute | solution.py:328
  84.9 1.3 collective-permute-start.4
  86.2 0.4 fusion.24
  86.6 0.4 convolution_add_fusion.3
  87.0 1.3 collective-permute-start.8
  88.4 0.4 fusion.18
  88.8 1.3 collective-permute-start.1
  90.1 17.6 %collective-permute-done.4 = f32[256]{0:T(256)S(1)} collective-permute-done((f32[256]{0:T(256)S(1)}, f32[256]{0:T(256)S(1)}, u32[]{:S(2)}, u32[]{:S(2)}) %collective-permute-start.4) | collective-permute-done | bytes 1056 | tf_op jit(solution)/shard_map/ppermute | solution.py:328
  108.0 1.3 collective-permute-start.5
  109.3 3.9 %collective-permute-done.8 = f32[256,256]{1,0:T(8,128)S(1)} collective-permute-done((f32[256,256]{1,0:T(8,128)S(1)}, f32[256,256]{1,0:T(8,128)S(1)}, u32[]{:S(2)}, u32[]{:S(2)}) %collective-permute-start.8) | collective-permute-done | bytes 262176 | tf_op jit(solution)/shard_map/ppermute | solution.py:328
  113.3 0.4 fusion.25
  113.7 0.4 convolution_add_fusion.2
  114.1 1.5 collective-permute-start.9
  115.6 0.5 collective-permute-done.1
  116.1 0.4 fusion.19
  116.5 1.3 collective-permute-start.2
  117.8 27.6 %collective-permute-done.5 = f32[256]{0:T(256)S(1)} collective-permute-done((f32[256]{0:T(256)S(1)}, f32[256]{0:T(256)S(1)}, u32[]{:S(2)}, u32[]{:S(2)}) %collective-permute-start.5) | collective-permute-done | bytes 1056 | tf_op jit(solution)/shard_map/ppermute | solution.py:328
  145.4 0.3 fusion.23
  145.7 1.3 collective-permute-start.6
  147.0 6.8 %collective-permute-done.9 = f32[256,256]{1,0:T(8,128)S(1)} collective-permute-done((f32[256,256]{1,0:T(8,128)S(1)}, f32[256,256]{1,0:T(8,128)S(1)}, u32[]{:S(2)}, u32[]{:S(2)}) %collective-permute-start.9) | collective-permute-done | bytes 262176 | tf_op jit(solution)/shard_map/ppermute | solution.py:328
  153.8 0.4 fusion.26
  154.2 0.4 convolution_add_fusion.1
  154.7 1.3 collective-permute-start.10
  156.0 0.7 collective-permute-done.2
  156.7 0.4 fusion.20
  157.0 50.7 %collective-permute-done.6 = f32[256]{0:T(256)S(1)} collective-permute-done((f32[256]{0:T(256)S(1)}, f32[256]{0:T(256)S(1)}, u32[]{:S(2)}, u32[]{:S(2)}) %collective-permute-start.6) | collective-permute-done | bytes 1056 | tf_op jit(solution)/shard_map/ppermute | solution.py:328
  207.7 0.9 convolution_add_fusion.4
  208.6 17.0 %collective-permute-done.10 = f32[256,256]{1,0:T(8,128)S(1)} collective-permute-done((f32[256,256]{1,0:T(8,128)S(1)}, f32[256,256]{1,0:T(8,128)S(1)}, u32[]{:S(2)}, u32[]{:S(2)}) %collective-permute-start.10) | collective-permute-done | bytes 262176 | tf_op jit(solution)/shard_map/ppermute | solution.py:328
  225.6 0.4 fusion.27
  226.0 1.1 fusion.12
  (28 shorter events, 1.3 us)
Async XLA Ops:
  0.6 0.7 copy-start.2
  1.9 0.9 copy-start.4
  1.9 0.9 copy-start.5
  2.8 0.7 copy-start.3
  27.0 1.4 copy-start.1
  27.0 1.4 copy-start
  72.0 14.2 %collective-permute-start.7 = (f32[256,256]{1,0:T(8,128)S(1)}, f32[256,256]{1,0:T(8,128)S(1)}, u32[]{:S(2)}, u32[]{:S(2)}) collective-permute-start(f32[256,256]{1,0:T(8,128)S(1)} %bitcast.112), channel_id=1, source_target_pairs={{1,0},{2,1},{3,2},{4,3},{5,4},{6,5},{7,6},{8,7},{9,8},{10,9},{11,1... | collective-permute-start | bytes 786440 | tf_op jit(solution)/shard_map/ppermute | solution.py:328
  74.0 10.6 %collective-permute-start.3 = (f32[256]{0:T(256)S(1)}, f32[256]{0:T(256)S(1)}, u32[]{:S(2)}, u32[]{:S(2)}) collective-permute-start(f32[256]{0:T(256)S(1)} %bitcast.122), channel_id=1, source_target_pairs={{1,0},{2,1},{3,2},{4,3},{5,4},{6,5},{7,6},{8,7},{9,8},{10,9},{11,1... | collective-permute-start | bytes 3080 | tf_op jit(solution)/shard_map/ppermute | solution.py:328
  75.9 12.5 %collective-permute-start = (f32[256,256]{1,0:T(8,128)S(1)}, f32[256,256]{1,0:T(8,128)S(1)}, u32[]{:S(2)}, u32[]{:S(2)}) collective-permute-start(f32[256,256]{1,0:T(8,128)S(1)} %get-tuple-element.72), channel_id=1, source_target_pairs={{1,0},{2,1},{3,2},{4,3},{5,4},{6,5},{7,6},{8,7},{9,8},{10,9},{11,1... | collective-permute-start | bytes 786440 | tf_op jit(solution)/shard_map/ppermute | solution.py:328
  84.9 22.9 %collective-permute-start.4 = (f32[256]{0:T(256)S(1)}, f32[256]{0:T(256)S(1)}, u32[]{:S(2)}, u32[]{:S(2)}) collective-permute-start(f32[256]{0:T(256)S(1)} %add.98), channel_id=1, source_target_pairs={{2,0},{3,1},{4,2},{5,3},{6,4},{7,5},{8,6},{9,7},{10,8},{11,9},{12,... | collective-permute-start | bytes 3080 | tf_op jit(solution)/shard_map/ppermute | solution.py:328
  87.0 26.2 %collective-permute-start.8 = (f32[256,256]{1,0:T(8,128)S(1)}, f32[256,256]{1,0:T(8,128)S(1)}, u32[]{:S(2)}, u32[]{:S(2)}) collective-permute-start(f32[256,256]{1,0:T(8,128)S(1)} %convolution_add_fusion.3), channel_id=1, source_target_pairs={{2,0},{3,1},{4,2},{5,3},{6,4},{7,5},{8,6},{9,7},{10,8},{11,9},{12,... | collective-permute-start | bytes 786440 | tf_op jit(solution)/shard_map/ppermute | solution.py:328
  88.8 27.3 %collective-permute-start.1 = (f32[256,256]{1,0:T(8,128)S(1)}, f32[256,256]{1,0:T(8,128)S(1)}, u32[]{:S(2)}, u32[]{:S(2)}) collective-permute-start(f32[256,256]{1,0:T(8,128)S(1)} %fusion.18), channel_id=1, source_target_pairs={{2,0},{3,1},{4,2},{5,3},{6,4},{7,5},{8,6},{9,7},{10,8},{11,9},{12,... | collective-permute-start | bytes 786440 | tf_op jit(solution)/shard_map/ppermute | solution.py:328
  108.0 37.4 %collective-permute-start.5 = (f32[256]{0:T(256)S(1)}, f32[256]{0:T(256)S(1)}, u32[]{:S(2)}, u32[]{:S(2)}) collective-permute-start(f32[256]{0:T(256)S(1)} %add.99), channel_id=1, source_target_pairs={{4,0},{5,1},{6,2},{7,3},{8,4},{9,5},{10,6},{11,7},{12,8},{13,9},{1... | collective-permute-start | bytes 3080 | tf_op jit(solution)/shard_map/ppermute | solution.py:328
  114.1 39.8 %collective-permute-start.9 = (f32[256,256]{1,0:T(8,128)S(1)}, f32[256,256]{1,0:T(8,128)S(1)}, u32[]{:S(2)}, u32[]{:S(2)}) collective-permute-start(f32[256,256]{1,0:T(8,128)S(1)} %convolution_add_fusion.2), channel_id=1, source_target_pairs={{4,0},{5,1},{6,2},{7,3},{8,4},{9,5},{10,6},{11,7},{12,8},{13,9},{1... | collective-permute-start | bytes 786440 | tf_op jit(solution)/shard_map/ppermute | solution.py:328
  116.5 40.2 %collective-permute-start.2 = (f32[256,256]{1,0:T(8,128)S(1)}, f32[256,256]{1,0:T(8,128)S(1)}, u32[]{:S(2)}, u32[]{:S(2)}) collective-permute-start(f32[256,256]{1,0:T(8,128)S(1)} %fusion.19), channel_id=1, source_target_pairs={{4,0},{5,1},{6,2},{7,3},{8,4},{9,5},{10,6},{11,7},{12,8},{13,9},{1... | collective-permute-start | bytes 786440 | tf_op jit(solution)/shard_map/ppermute | solution.py:328
  145.7 62.1 %collective-permute-start.6 = (f32[256]{0:T(256)S(1)}, f32[256]{0:T(256)S(1)}, u32[]{:S(2)}, u32[]{:S(2)}) collective-permute-start(f32[256]{0:T(256)S(1)} %add.100), channel_id=1, source_target_pairs={{8,0},{9,1},{10,2},{11,3},{12,4},{13,5},{14,6},{15,7},{24,16},{25,... | collective-permute-start | bytes 3080 | tf_op jit(solution)/shard_map/ppermute | solution.py:328
  154.7 70.9 %collective-permute-start.10 = (f32[256,256]{1,0:T(8,128)S(1)}, f32[256,256]{1,0:T(8,128)S(1)}, u32[]{:S(2)}, u32[]{:S(2)}) collective-permute-start(f32[256,256]{1,0:T(8,128)S(1)} %convolution_add_fusion.1), channel_id=1, source_target_pairs={{8,0},{9,1},{10,2},{11,3},{12,4},{13,5},{14,6},{15,7},{24,16},{25,... | collective-permute-start | bytes 786440 | tf_op jit(solution)/shard_map/ppermute | solution.py:328

commit v5 on v3

--- a/solution.py
+++ b/solution.py
@@ -10,10 +10,33 @@
 PANEL = 32
 
 
+def _inv2(a, b, d):
+    idet = 1.0 / (a * d - b * b)
+    return d * idet, -b * idet, a * idet
+
+def _inv4(m):
+    a00, a01, a11 = _inv2(m[0][0], m[0][1], m[1][1])
+    b = ((m[0][2], m[0][3]), (m[1][2], m[1][3]))
+    x = [[a00 * b[0][j] + a01 * b[1][j] for j in range(2)], [a01 * b[0][j] + a11 * b[1][j] for j in range(2)]]
+    s00 = m[2][2] - (b[0][0] * x[0][0] + b[1][0] * x[1][0])
+    s01 = m[2][3] - (b[0][0] * x[0][1] + b[1][0] * x[1][1])
+    s11 = m[3][3] - (b[0][1] * x[0][1] + b[1][1] * x[1][1])
+    c00, c01, c11 = _inv2(s00, s01, s11)
+    cm = ((c00, c01), (c01, c11))
+    y = [[x[i][0] * cm[0][j] + x[i][1] * cm[1][j] for j in range(2)] for i in range(2)]
+    am = ((a00, a01), (a01, a11))
+    out = [[None] * 4 for _ in range(4)]
+    for i in range(2):
+        for j in range(2):
+            out[i][j] = am[i][j] + y[i][0] * x[j][0] + y[i][1] * x[j][1]
+            out[i][2 + j] = -y[i][j]
+            out[2 + j][i] = -y[i][j]
+            out[2 + i][2 + j] = cm[i][j]
+    return out
+
 def _sweep_kernel(a_ref, o_ref):
     o_ref[...] = a_ref[...]
     _sweep_in_place(o_ref)
-
 
 def _sweep_in_place(o_ref):
     n = o_ref.shape[0]
@@ -25,28 +48,34 @@
         base = blk * PANEL
         orig = o_ref[base:base + PANEL, :]
         panel = orig
-        for t in range(PANEL):
-            is_row = sub == t
-            is_col = lane == base + t
-            colv = jnp.sum(jnp.where(is_col, panel, 0.0), axis=1, keepdims=True)
-            rowv = jnp.sum(jnp.where(is_row, panel, 0.0), axis=0, keepdims=True)
-            pivot = jnp.sum(jnp.where(sub_col == t, colv, 0.0), axis=0, keepdims=True)
-            inv = 1.0 / pivot
-            scaled_row = rowv * inv
-            panel = jnp.where(
-                is_row,
-                jnp.where(is_col, -inv, scaled_row),
-                jnp.where(is_col, colv * inv, panel - colv * scaled_row),
-            )
+        for t in range(0, PANEL, 4):
+            rows = [sub == t + i for i in range(4)]
+            cols = [lane == base + t + i for i in range(4)]
+            cv = [jnp.sum(jnp.where(cols[i], panel, 0.0), axis=1, keepdims=True) for i in range(4)]
+            rv = [jnp.sum(jnp.where(rows[i], panel, 0.0), axis=0, keepdims=True) for i in range(4)]
+            m = [[None] * 4 for _ in range(4)]
+            for i in range(4):
+                for j in range(i, 4):
+                    m[i][j] = jnp.sum(jnp.where(sub_col == t + i, cv[j], 0.0), axis=0, keepdims=True)
+                    m[j][i] = m[i][j]
+            mi = _inv4(m)
+            nr = [mi[i][0] * rv[0] + mi[i][1] * rv[1] + mi[i][2] * rv[2] + mi[i][3] * rv[3] for i in range(4)]
+            nc = [cv[0] * mi[0][j] + cv[1] * mi[1][j] + cv[2] * mi[2][j] + cv[3] * mi[3][j] for j in range(4)]
+            rest = panel - cv[0] * nr[0] - cv[1] * nr[1] - cv[2] * nr[2] - cv[3] * nr[3]
+            for j in range(4):
+                rest = jnp.where(cols[j], nc[j], rest)
+            for i in range(4):
+                row_val = nr[i]
+                for j in range(4):
+                    row_val = jnp.where(cols[j], -mi[i][j], row_val)
+                rest = jnp.where(rows[i], row_val, rest)
+            panel = rest
         full = o_ref[...]
-        update = lax.dot_general(
-            orig, panel, (((0,), (0,)), ((), ())), precision=HIGHEST,
-            preferred_element_type=jnp.float32,
-        )
-        in_block = (lane_full >= base) & (lane_full < base + PANEL)
-        o_ref[...] = jnp.where(in_block, 0.0, full) - update
+        update = lax.dot_general(orig, panel, (((0,), (0,)), ((), ())), precision=HIGHEST,
+                                 preferred_element_type=jnp.float32)
+        in_blk = (lane_full >= base) & (lane_full < base + PANEL)
+        o_ref[...] = jnp.where(in_blk, 0.0, full) - update
         o_ref[base:base + PANEL, :] = panel
-
 
 def neg_inverse(matrix):
     size = matrix.shape[-1]

time: 330 us -> 187 us (0.57)
  waiting for transfers between devices: 210 us -> 101 us
  Pallas kernels: 62.7 us -> 29.1 us
    ppermute x11, waiting for transfers between devices: 210 us -> 101 us  [shards(): received = lax.ppermute(running, 'tm', pairs)]
    pallas_call x1, Pallas kernels: 31.4 us -> 14.6 us  [neg_inverse(): pl.pallas_call(_sweep_kernel, out_shape=jax.ShapeDtypeStruct((size, size)...]
    pallas_call x1, Pallas kernels: 31.3 us -> 14.5 us  [run_filter(): pl.pallas_call(_filter_kernel, out_shape=(jax.ShapeDtypeStruct((1, width)...]
  transfers between devices with their start and end apart: 11 -> 11, of which waited for: 9 -> 10; matrix products, arithmetic and copies ran while one was open for 2% -> 3% of each run, Pallas kernels for 0% -> 0%
where the time goes in v5:
time: 187 us; the launch traced here: 186 us
  waiting for transfers between devices  101 us (54%)
  Pallas kernels  29.1 us (16%)
  blocking collectives  23 us (12%)
  starting transfers between devices  16.5 us (9%)
  matrix products  8.89 us (5%)
  local copies, waits for them, and re-layouts  4.36 us (2%)
  other arithmetic  2.55 us (1%)
    ppermute x11, waiting for transfers between devices, shards(): received = lax.ppermute(running, 'tm', pairs)  101 us
    all_gather x1, blocking collectives, shards(): gathered = lax.all_gather(packed, 'tm', tiled=True)  23 us
    ppermute x11, starting transfers between devices, shards(): received = lax.ppermute(running, 'tm', pairs)  16.5 us
    pallas_call x1, Pallas kernels, neg_inverse(): pl.pallas_call(_sweep_kernel, out_shape=jax.ShapeDtypeStruct((size, size)...  14.6 us
    pallas_call x1, Pallas kernels, run_filter(): pl.pallas_call(_filter_kernel, out_shape=(jax.ShapeDtypeStruct((1, width)...  14.5 us
    dot_general x18, matrix products, matmul_hi(): return jnp.matmul(left, right, precision=HIGHEST)  8.89 us
  transfers between devices with their start and end apart: 11, of which 10 were waited for; matrix products, arithmetic and copies ran while one was open for 3% of the time, Pallas kernels for 0%

profile of v5, /device:TPU:1, one launch (start us, length us, event | category | flops | bytes accessed | tf_op | source)
XLA Modules:
  0.0 186.3 jit_solution(11220826074269779860)
XLA Ops:
  0.6 0.6 copy-done.2
  1.3 0.6 fusion.15
  1.9 0.9 copy.22.trans_col_ref
  2.8 0.7 copy-done.3
  3.5 23.0 %all_gather.3 = f32[16,2,128]{2,1,0:T(2,128)S(1)} all-gather(f32[1,2,128]{2,1,0:T(2,128)S(1)} %pad_maximum_fusion.4), channel_id=1, replica_groups=mesh['groups'=2,'tm'=16] {'tm'}, dimensions={0}, use_global_device_ids=true | all-gather | bytes 17408 | tf_op jit(solution)/shard_map/all_gather | solution.py:274
  26.4 0.6 fusion.17
  27.0 1.4 copy.21.root_col_ref
  28.5 0.7 select_maximum_fusion
  29.3 14.5 %shard_map.68 = (f32[1,256]{1,0:T(1,128)S(1)}, f32[256,256]{1,0:T(8,128)S(1)}) custom-call(s32[1]{0:T(128)} %bitcast.14.count_ref, f32[16,128]{1,0:T(8,128)} %bitcast.115, f32[16,128]{1,0:T(8,128)} %bitcast.114, f32[16,128,1]{2,1,0:T(8,128)} %copy.21.root_col_ref, f32[4,128]{1,0:T(4,128)} %get-tuple-element.92.trans_row_ref, ...), custom_call_target="tpu_custom_call" | custom-call | tf_op jit(solution)/shard_map/pallas_call | solution.py:143
  43.8 18.3 %conditional.1 = (f32[1,256]{1,0:T(1,128)S(1)}, f32[256,256]{1,0:T(8,128)S(1)}, f32[1,256,256]{2,1,0:T(8,128)S(1)}) conditional(s32[]{:T(128)} %convert_element_type.12, (f32[128]{0:T(128)S(1)}, f32[1,256,256]{2,1,0:T(8,128)S(1)}, f32[128]{0:T(128)S(1)}, f32[128]{0:T(128)S(1)}, f32[128]{0:T(128)S(1)}, /*index=5*/f32[256,256]{1,0:T(8,128)S(1)}, ...), branch_computations={%region_0.1_spmd, %region_1.2_spmd} | conditional | flops 404358400 | bytes 5516342 | solution.py:319
  44.5 0.7 maximum_add_fusion.a_ref
  45.3 14.6 %vmap__.2 = f32[256,256]{1,0:T(8,128)} custom-call(f32[256,256]{1,0:T(8,128)} %maximum_add_fusion.a_ref), custom_call_target="tpu_custom_call" | custom-call | tf_op jit(solution)/shard_map/cond/branch_0_fun/vmap()/pallas_call | solution.py:82
  59.8 1.5 fusion
  61.4 0.4 fusion.1
  61.8 0.3 convolution_subtract_fusion
  62.1 2.0 %collective-permute-start.7 = (f32[256,256]{1,0:T(8,128)S(1)}, f32[256,256]{1,0:T(8,128)S(1)}, u32[]{:S(2)}, u32[]{:S(2)}) collective-permute-start(f32[256,256]{1,0:T(8,128)S(1)} %bitcast.112), channel_id=1, source_target_pairs={{1,0},{2,1},{3,2},{4,3},{5,4},{6,5},{7,6},{8,7},{9,8},{10,9},{11,1... | collective-permute-start | bytes 786440 | tf_op jit(solution)/shard_map/ppermute | solution.py:345
  64.0 1.9 %collective-permute-start.3 = (f32[256]{0:T(256)S(1)}, f32[256]{0:T(256)S(1)}, u32[]{:S(2)}, u32[]{:S(2)}) collective-permute-start(f32[256]{0:T(256)S(1)} %bitcast.122), channel_id=1, source_target_pairs={{1,0},{2,1},{3,2},{4,3},{5,4},{6,5},{7,6},{8,7},{9,8},{10,9},{11,1... | collective-permute-start | bytes 3080 | tf_op jit(solution)/shard_map/ppermute | solution.py:345
  66.0 1.9 %collective-permute-start = (f32[256,256]{1,0:T(8,128)S(1)}, f32[256,256]{1,0:T(8,128)S(1)}, u32[]{:S(2)}, u32[]{:S(2)}) collective-permute-start(f32[256,256]{1,0:T(8,128)S(1)} %get-tuple-element.72), channel_id=1, source_target_pairs={{1,0},{2,1},{3,2},{4,3},{5,4},{6,5},{7,6},{8,7},{9,8},{10,9},{11,1... | collective-permute-start | bytes 786440 | tf_op jit(solution)/shard_map/ppermute | solution.py:345
  67.9 4.4 %collective-permute-done.3 = f32[256]{0:T(256)S(1)} collective-permute-done((f32[256]{0:T(256)S(1)}, f32[256]{0:T(256)S(1)}, u32[]{:S(2)}, u32[]{:S(2)}) %collective-permute-start.3) | collective-permute-done | bytes 1056 | tf_op jit(solution)/shard_map/ppermute | solution.py:345
  72.5 1.3 collective-permute-start.4
  73.9 0.4 fusion.24
  74.3 0.4 convolution_add_fusion.3
  74.7 1.3 collective-permute-start.8
  76.1 0.4 fusion.18
  76.5 1.3 collective-permute-start.1
  77.8 12.9 %collective-permute-done.4 = f32[256]{0:T(256)S(1)} collective-permute-done((f32[256]{0:T(256)S(1)}, f32[256]{0:T(256)S(1)}, u32[]{:S(2)}, u32[]{:S(2)}) %collective-permute-start.4) | collective-permute-done | bytes 1056 | tf_op jit(solution)/shard_map/ppermute | solution.py:345
  90.9 1.6 collective-permute-start.5
  92.5 3.7 %collective-permute-done.8 = f32[256,256]{1,0:T(8,128)S(1)} collective-permute-done((f32[256,256]{1,0:T(8,128)S(1)}, f32[256,256]{1,0:T(8,128)S(1)}, u32[]{:S(2)}, u32[]{:S(2)}) %collective-permute-start.8) | collective-permute-done | bytes 262176 | tf_op jit(solution)/shard_map/ppermute | solution.py:345
  96.2 0.4 fusion.25
  96.6 0.4 convolution_add_fusion.2
  97.0 1.3 collective-permute-start.9
  98.3 0.7 collective-permute-done.1
  99.0 0.4 fusion.19
  99.4 1.3 collective-permute-start.2
  100.7 18.1 %collective-permute-done.5 = f32[256]{0:T(256)S(1)} collective-permute-done((f32[256]{0:T(256)S(1)}, f32[256]{0:T(256)S(1)}, u32[]{:S(2)}, u32[]{:S(2)}) %collective-permute-start.5) | collective-permute-done | bytes 1056 | tf_op jit(solution)/shard_map/ppermute | solution.py:345
  118.8 0.3 fusion.23
  119.1 1.3 collective-permute-start.6
  120.4 6.8 %collective-permute-done.9 = f32[256,256]{1,0:T(8,128)S(1)} collective-permute-done((f32[256,256]{1,0:T(8,128)S(1)}, f32[256,256]{1,0:T(8,128)S(1)}, u32[]{:S(2)}, u32[]{:S(2)}) %collective-permute-start.9) | collective-permute-done | bytes 262176 | tf_op jit(solution)/shard_map/ppermute | solution.py:345
  127.3 0.4 fusion.26
  127.7 0.4 convolution_add_fusion.1
  128.1 1.3 collective-permute-start.10
  129.4 0.7 collective-permute-done.2
  130.1 0.4 fusion.20
  130.5 36.5 %collective-permute-done.6 = f32[256]{0:T(256)S(1)} collective-permute-done((f32[256]{0:T(256)S(1)}, f32[256]{0:T(256)S(1)}, u32[]{:S(2)}, u32[]{:S(2)}) %collective-permute-start.6) | collective-permute-done | bytes 1056 | tf_op jit(solution)/shard_map/ppermute | solution.py:345
  167.0 0.9 convolution_add_fusion.4
  167.8 17.0 %collective-permute-done.10 = f32[256,256]{1,0:T(8,128)S(1)} collective-permute-done((f32[256,256]{1,0:T(8,128)S(1)}, f32[256,256]{1,0:T(8,128)S(1)}, u32[]{:S(2)}, u32[]{:S(2)}) %collective-permute-start.10) | collective-permute-done | bytes 262176 | tf_op jit(solution)/shard_map/ppermute | solution.py:345
  184.8 0.4 fusion.27
  185.2 1.1 fusion.12
  (28 shorter events, 1.3 us)
Async XLA Ops:
  0.6 0.7 copy-start.2
  1.9 0.9 copy-start.4
  1.9 0.9 copy-start.5
  2.8 0.7 copy-start.3
  27.0 1.4 copy-start.1
  27.0 1.4 copy-start
  62.1 11.8 %collective-permute-start.7 = (f32[256,256]{1,0:T(8,128)S(1)}, f32[256,256]{1,0:T(8,128)S(1)}, u32[]{:S(2)}, u32[]{:S(2)}) collective-permute-start(f32[256,256]{1,0:T(8,128)S(1)} %bitcast.112), channel_id=1, source_target_pairs={{1,0},{2,1},{3,2},{4,3},{5,4},{6,5},{7,6},{8,7},{9,8},{10,9},{11,1... | collective-permute-start | bytes 786440 | tf_op jit(solution)/shard_map/ppermute | solution.py:345
  64.0 8.2 %collective-permute-start.3 = (f32[256]{0:T(256)S(1)}, f32[256]{0:T(256)S(1)}, u32[]{:S(2)}, u32[]{:S(2)}) collective-permute-start(f32[256]{0:T(256)S(1)} %bitcast.122), channel_id=1, source_target_pairs={{1,0},{2,1},{3,2},{4,3},{5,4},{6,5},{7,6},{8,7},{9,8},{10,9},{11,1... | collective-permute-start | bytes 3080 | tf_op jit(solution)/shard_map/ppermute | solution.py:345
  66.0 10.1 %collective-permute-start = (f32[256,256]{1,0:T(8,128)S(1)}, f32[256,256]{1,0:T(8,128)S(1)}, u32[]{:S(2)}, u32[]{:S(2)}) collective-permute-start(f32[256,256]{1,0:T(8,128)S(1)} %get-tuple-element.72), channel_id=1, source_target_pairs={{1,0},{2,1},{3,2},{4,3},{5,4},{6,5},{7,6},{8,7},{9,8},{10,9},{11,1... | collective-permute-start | bytes 786440 | tf_op jit(solution)/shard_map/ppermute | solution.py:345
  72.5 18.1 %collective-permute-start.4 = (f32[256]{0:T(256)S(1)}, f32[256]{0:T(256)S(1)}, u32[]{:S(2)}, u32[]{:S(2)}) collective-permute-start(f32[256]{0:T(256)S(1)} %add.98), channel_id=1, source_target_pairs={{2,0},{3,1},{4,2},{5,3},{6,4},{7,5},{8,6},{9,7},{10,8},{11,9},{12,... | collective-permute-start | bytes 3080 | tf_op jit(solution)/shard_map/ppermute | solution.py:345
  74.7 21.5 %collective-permute-start.8 = (f32[256,256]{1,0:T(8,128)S(1)}, f32[256,256]{1,0:T(8,128)S(1)}, u32[]{:S(2)}, u32[]{:S(2)}) collective-permute-start(f32[256,256]{1,0:T(8,128)S(1)} %convolution_add_fusion.3), channel_id=1, source_target_pairs={{2,0},{3,1},{4,2},{5,3},{6,4},{7,5},{8,6},{9,7},{10,8},{11,9},{12,... | collective-permute-start | bytes 786440 | tf_op jit(solution)/shard_map/ppermute | solution.py:345
  76.5 22.6 %collective-permute-start.1 = (f32[256,256]{1,0:T(8,128)S(1)}, f32[256,256]{1,0:T(8,128)S(1)}, u32[]{:S(2)}, u32[]{:S(2)}) collective-permute-start(f32[256,256]{1,0:T(8,128)S(1)} %fusion.18), channel_id=1, source_target_pairs={{2,0},{3,1},{4,2},{5,3},{6,4},{7,5},{8,6},{9,7},{10,8},{11,9},{12,... | collective-permute-start | bytes 786440 | tf_op jit(solution)/shard_map/ppermute | solution.py:345
  90.9 27.9 %collective-permute-start.5 = (f32[256]{0:T(256)S(1)}, f32[256]{0:T(256)S(1)}, u32[]{:S(2)}, u32[]{:S(2)}) collective-permute-start(f32[256]{0:T(256)S(1)} %add.99), channel_id=1, source_target_pairs={{4,0},{5,1},{6,2},{7,3},{8,4},{9,5},{10,6},{11,7},{12,8},{13,9},{1... | collective-permute-start | bytes 3080 | tf_op jit(solution)/shard_map/ppermute | solution.py:345
  97.0 30.3 %collective-permute-start.9 = (f32[256,256]{1,0:T(8,128)S(1)}, f32[256,256]{1,0:T(8,128)S(1)}, u32[]{:S(2)}, u32[]{:S(2)}) collective-permute-start(f32[256,256]{1,0:T(8,128)S(1)} %convolution_add_fusion.2), channel_id=1, source_target_pairs={{4,0},{5,1},{6,2},{7,3},{8,4},{9,5},{10,6},{11,7},{12,8},{13,9},{1... | collective-permute-start | bytes 786440 | tf_op jit(solution)/shard_map/ppermute | solution.py:345
  99.4 30.7 %collective-permute-start.2 = (f32[256,256]{1,0:T(8,128)S(1)}, f32[256,256]{1,0:T(8,128)S(1)}, u32[]{:S(2)}, u32[]{:S(2)}) collective-permute-start(f32[256,256]{1,0:T(8,128)S(1)} %fusion.19), channel_id=1, source_target_pairs={{4,0},{5,1},{6,2},{7,3},{8,4},{9,5},{10,6},{11,7},{12,8},{13,9},{1... | collective-permute-start | bytes 786440 | tf_op jit(solution)/shard_map/ppermute | solution.py:345
  119.1 47.9 %collective-permute-start.6 = (f32[256]{0:T(256)S(1)}, f32[256]{0:T(256)S(1)}, u32[]{:S(2)}, u32[]{:S(2)}) collective-permute-start(f32[256]{0:T(256)S(1)} %add.100), channel_id=1, source_target_pairs={{8,0},{9,1},{10,2},{11,3},{12,4},{13,5},{14,6},{15,7},{24,16},{25,... | collective-permute-start | bytes 3080 | tf_op jit(solution)/shard_map/ppermute | solution.py:345
  128.1 56.7 %collective-permute-start.10 = (f32[256,256]{1,0:T(8,128)S(1)}, f32[256,256]{1,0:T(8,128)S(1)}, u32[]{:S(2)}, u32[]{:S(2)}) collective-permute-start(f32[256,256]{1,0:T(8,128)S(1)} %convolution_add_fusion.1), channel_id=1, source_target_pairs={{8,0},{9,1},{10,2},{11,3},{12,4},{13,5},{14,6},{15,7},{24,16},{25,... | collective-permute-start | bytes 786440 | tf_op jit(solution)/shard_map/ppermute | solution.py:345

commit v6 on v5

--- a/solution.py
+++ b/solution.py
@@ -261,6 +261,16 @@
     )
 
 
+def send_packed(element, pairs, with_gain):
+    gain, mean, cov = element
+    width = mean.shape[-1]
+    pieces = ([gain] if with_gain else []) + [cov, jnp.broadcast_to(mean[None], (8, width))]
+    received = lax.ppermute(jnp.concatenate(pieces, axis=0), "tm", pairs)
+    offset = width if with_gain else 0
+    recv_gain = received[:width] if with_gain else jnp.zeros_like(gain)
+    return (recv_gain, received[offset + width], received[offset:offset + width])
+
+
 def shards(observed, obs_masks, decay_rates, noise_var, spatial_cov):
     transit, process, prior = build_model(decay_rates, spatial_cov)
     local_steps, points = observed.shape
@@ -342,7 +352,8 @@
     shift = 1
     while shift < tm_count:
         pairs = [(source, source - shift) for source in range(shift, tm_count)]
-        received = lax.ppermute(running, "tm", pairs)
+        final_round = 2 * shift >= tm_count
+        received = send_packed(running, pairs, not final_round)
         running = smooth_join(running, received)
         shift *= 2
 

time: 187 us -> 202 us (1.080)
  waiting for transfers between devices: 101 us -> 126 us
  starting transfers between devices: 16.5 us -> 6.02 us
    ppermute x11 -> x4, waiting for transfers between devices: 101 us -> 126 us  [send_packed(): received = lax.ppermute(jnp.concatenate(pieces, axis=0), 'tm', pairs)]
    ppermute x11 -> x4, starting transfers between devices: 16.5 us -> 6.02 us  [send_packed(): received = lax.ppermute(jnp.concatenate(pieces, axis=0), 'tm', pairs)]
  transfers between devices with their start and end apart: 11 -> 4, of which waited for: 10 -> 4; matrix products, arithmetic and copies ran while one was open for 3% -> 0% of each run, Pallas kernels for 0% -> 0%
where the time goes in v6:
time: 202 us
  waiting for transfers between devices  126 us (62%)
  Pallas kernels  29.1 us (14%)
  blocking collectives  23 us (11%)
  matrix products  8.99 us (4%)
  starting transfers between devices  6.02 us (3%)
  local copies, waits for them, and re-layouts  4.43 us (2%)
  other arithmetic  2.82 us (1%)
    ppermute x4, waiting for transfers between devices, send_packed(): received = lax.ppermute(jnp.concatenate(pieces, axis=0), 'tm', pairs)  126 us
    all_gather x1, blocking collectives, shards(): gathered = lax.all_gather(packed, 'tm', tiled=True)  23 us
    pallas_call x1, Pallas kernels, neg_inverse(): pl.pallas_call(_sweep_kernel, out_shape=jax.ShapeDtypeStruct((size, size)...  14.6 us
    pallas_call x1, Pallas kernels, run_filter(): pl.pallas_call(_filter_kernel, out_shape=(jax.ShapeDtypeStruct((1, width)...  14.5 us
    dot_general x18, matrix products, matmul_hi(): return jnp.matmul(left, right, precision=HIGHEST)  8.99 us
    ppermute x4, starting transfers between devices, send_packed(): received = lax.ppermute(jnp.concatenate(pieces, axis=0), 'tm', pairs)  6.02 us
  transfers between devices with their start and end apart: 4, of which 4 were waited for; matrix products, arithmetic and copies ran while one was open for 0% of the time, Pallas kernels for 0%

profile of v6, /device:TPU:1, one launch (start us, length us, event | category | flops | bytes accessed | tf_op | source)
XLA Modules:
  0.0 201.6 jit_solution(3806629080556215492)
XLA Ops:
  0.6 0.6 copy-done.2
  1.3 0.6 fusion.30
  1.9 0.9 copy.22.trans_col_ref
  2.8 0.0 copy-start.3
  2.8 0.7 copy-done.3
  3.5 23.0 %all_gather.3 = f32[16,2,128]{2,1,0:T(2,128)S(1)} all-gather(f32[1,2,128]{2,1,0:T(2,128)S(1)} %pad_maximum_fusion.8), channel_id=1, replica_groups=mesh['groups'=2,'tm'=16] {'tm'}, dimensions={0}, use_global_device_ids=true | all-gather | bytes 17408 | tf_op jit(solution)/shard_map/all_gather | solution.py:284
  26.4 0.6 fusion.32
  27.0 1.4 copy.21.root_col_ref
  28.4 0.1 multiply_multiply_fusion.1
  28.5 0.7 select_maximum_fusion
  29.3 14.5 %shard_map.68 = (f32[1,256]{1,0:T(1,128)S(1)}, f32[256,256]{1,0:T(8,128)S(1)}) custom-call(s32[1]{0:T(128)} %bitcast.16.count_ref, f32[16,128]{1,0:T(8,128)} %bitcast.122, f32[16,128]{1,0:T(8,128)} %bitcast.121, f32[16,128,1]{2,1,0:T(8,128)} %copy.21.root_col_ref, f32[4,128]{1,0:T(4,128)} %get-tuple-element.81.trans_row_ref, ...), custom_call_target="tpu_custom_call" | custom-call | tf_op jit(solution)/shard_map/pallas_call | solution.py:143
  43.8 18.4 %conditional.1 = (f32[1,256]{1,0:T(1,128)S(1)}, f32[256,256]{1,0:T(8,128)S(1)}, f32[256,256]{1,0:T(8,128)S(1)}) conditional(s32[]{:T(128)} %convert_element_type.12, (f32[128]{0:T(128)S(1)}, f32[1,256,256]{2,1,0:T(8,128)S(1)}, f32[128]{0:T(128)S(1)}, f32[128]{0:T(128)S(1)}, f32[128]{0:T(128)S(1)}, /*index=5*/f32[256,256]{1,0:T(8,128)S(1)}, s32[]{:T(128)}, ...), branch_computations={%region_0.1_spmd, %region_1.2_spmd} | conditional | flops 404358400 | bytes 5516342 | solution.py:329
  44.0 0.1 multiply_add_fusion.1
  44.1 0.1 copy.23
  44.3 0.1 copy.24
  44.4 0.1 add_bitcast_fusion.1
  44.5 0.7 maximum_add_fusion.a_ref
  45.2 14.6 %vmap__.2 = f32[256,256]{1,0:T(8,128)} custom-call(f32[256,256]{1,0:T(8,128)} %maximum_add_fusion.a_ref), custom_call_target="tpu_custom_call" | custom-call | tf_op jit(solution)/shard_map/cond/branch_0_fun/vmap()/pallas_call | solution.py:82
  59.8 1.5 fusion
  61.4 0.5 fusion.2
  61.8 0.3 convolution_subtract_fusion
  62.1 0.1 broadcast_in_dim.74
  62.2 1.9 collective-permute-start
  64.2 11.1 %collective-permute-done = f32[520,256]{1,0:T(8,128)S(1)} collective-permute-done((f32[520,256]{1,0:T(8,128)S(1)}, f32[520,256]{1,0:T(8,128)S(1)}, u32[]{:S(2)}, u32[]{:S(2)}) %collective-permute-start) | collective-permute-done | bytes 532512 | tf_op jit(solution)/shard_map/ppermute | solution.py:268
  75.2 0.4 fusion.24
  75.6 0.4 convolution_add_fusion.3
  76.0 0.4 fusion.26
  76.4 0.3 convolution_add_fusion.7
  76.7 0.1 pad_maximum_fusion.4
  76.8 1.5 collective-permute-start.1
  78.3 22.2 %collective-permute-done.1 = f32[520,256]{1,0:T(8,128)S(1)} collective-permute-done((f32[520,256]{1,0:T(8,128)S(1)}, f32[520,256]{1,0:T(8,128)S(1)}, u32[]{:S(2)}, u32[]{:S(2)}) %collective-permute-start.1) | collective-permute-done | bytes 532512 | tf_op jit(solution)/shard_map/ppermute | solution.py:268
  100.6 0.4 fusion.20
  101.0 0.4 convolution_add_fusion.2
  101.4 0.4 fusion.22
  101.8 0.3 convolution_add_fusion.6
  102.0 0.1 pad_maximum_fusion.5
  102.1 1.3 collective-permute-start.2
  103.4 31.9 %collective-permute-done.2 = f32[520,256]{1,0:T(8,128)S(1)} collective-permute-done((f32[520,256]{1,0:T(8,128)S(1)}, f32[520,256]{1,0:T(8,128)S(1)}, u32[]{:S(2)}, u32[]{:S(2)}) %collective-permute-start.2) | collective-permute-done | bytes 532512 | tf_op jit(solution)/shard_map/ppermute | solution.py:268
  135.3 0.4 fusion.16
  135.7 0.4 convolution_add_fusion.1
  136.1 0.3 convolution_add_fusion.5
  136.4 0.1 pad_maximum_fusion.6
  136.5 1.3 collective-permute-start.3
  137.8 0.4 fusion.18
  138.2 61.0 %collective-permute-done.3 = f32[264,256]{1,0:T(8,128)S(1)} collective-permute-done((f32[264,256]{1,0:T(8,128)S(1)}, f32[264,256]{1,0:T(8,128)S(1)}, u32[]{:S(2)}, u32[]{:S(2)}) %collective-permute-start.3) | collective-permute-done | bytes 270368 | tf_op jit(solution)/shard_map/ppermute | solution.py:268
  199.2 0.4 fusion.14
  199.5 1.1 fusion.13
  200.7 0.9 convolution_add_fusion.4
  (19 shorter events, 0.2 us)
Async XLA Ops:
  0.6 0.7 copy-start.2
  1.9 0.9 copy-start.4
  1.9 0.9 copy-start.5
  2.8 0.7 copy-start.3
  27.0 1.4 copy-start.1
  27.0 1.4 copy-start
  62.2 13.0 %collective-permute-start = (f32[520,256]{1,0:T(8,128)S(1)}, f32[520,256]{1,0:T(8,128)S(1)}, u32[]{:S(2)}, u32[]{:S(2)}) collective-permute-start(f32[520,256]{1,0:T(8,128)S(1)} %pad_maximum_fusion.3), channel_id=1, source_target_pairs={{1,0},{2,1},{3,2},{4,3},{5,4},{6,5},{7,6},{8,7},{9,8},{10,9},{11,1... | collective-permute-start | bytes 1597448 | tf_op jit(solution)/shard_map/ppermute | solution.py:268
  76.8 23.8 %collective-permute-start.1 = (f32[520,256]{1,0:T(8,128)S(1)}, f32[520,256]{1,0:T(8,128)S(1)}, u32[]{:S(2)}, u32[]{:S(2)}) collective-permute-start(f32[520,256]{1,0:T(8,128)S(1)} %pad_maximum_fusion.4), channel_id=1, source_target_pairs={{2,0},{3,1},{4,2},{5,3},{6,4},{7,5},{8,6},{9,7},{10,8},{11,9},{12,... | collective-permute-start | bytes 1597448 | tf_op jit(solution)/shard_map/ppermute | solution.py:268
  102.1 33.2 %collective-permute-start.2 = (f32[520,256]{1,0:T(8,128)S(1)}, f32[520,256]{1,0:T(8,128)S(1)}, u32[]{:S(2)}, u32[]{:S(2)}) collective-permute-start(f32[520,256]{1,0:T(8,128)S(1)} %pad_maximum_fusion.5), channel_id=1, source_target_pairs={{4,0},{5,1},{6,2},{7,3},{8,4},{9,5},{10,6},{11,7},{12,8},{13,9},{1... | collective-permute-start | bytes 1597448 | tf_op jit(solution)/shard_map/ppermute | solution.py:268
  136.5 62.7 %collective-permute-start.3 = (f32[264,256]{1,0:T(8,128)S(1)}, f32[264,256]{1,0:T(8,128)S(1)}, u32[]{:S(2)}, u32[]{:S(2)}) collective-permute-start(f32[264,256]{1,0:T(8,128)S(1)} %pad_maximum_fusion.6), channel_id=1, source_target_pairs={{8,0},{9,1},{10,2},{11,3},{12,4},{13,5},{14,6},{15,7},{24,16},{25,... | collective-permute-start | bytes 811016 | tf_op jit(solution)/shard_map/ppermute | solution.py:268

commit v7 on v5

--- a/solution.py
+++ b/solution.py
@@ -40,6 +40,7 @@
 
 def _sweep_in_place(o_ref):
     n = o_ref.shape[0]
+    PANEL = 64 if n >= 256 else 32
     sub = lax.broadcasted_iota(jnp.int32, (PANEL, n), 0)
     lane = lax.broadcasted_iota(jnp.int32, (PANEL, n), 1)
     sub_col = lax.broadcasted_iota(jnp.int32, (PANEL, 1), 0)
@@ -261,6 +262,14 @@
     )
 
 
+def send_element(element, pairs):
+    gain, mean, cov = element
+    width = mean.shape[-1]
+    packed = jnp.concatenate([cov, jnp.broadcast_to(mean[None], (8, width))], axis=0)
+    recv_gain, recv_packed = lax.ppermute((gain, packed), "tm", pairs)
+    return (recv_gain, recv_packed[width], recv_packed[:width])
+
+
 def shards(observed, obs_masks, decay_rates, noise_var, spatial_cov):
     transit, process, prior = build_model(decay_rates, spatial_cov)
     local_steps, points = observed.shape
@@ -342,7 +351,7 @@
     shift = 1
     while shift < tm_count:
         pairs = [(source, source - shift) for source in range(shift, tm_count)]
-        received = lax.ppermute(running, "tm", pairs)
+        received = send_element(running, pairs)
         running = smooth_join(running, received)
         shift *= 2
 

time: 187 us -> 186 us (level)
  starting transfers between devices: 16.5 us -> 10.5 us
  waiting for transfers between devices: 101 us -> 107 us
    ppermute x11 -> x7, starting transfers between devices: 16.5 us -> 10.5 us  [send_element(): recv_gain, recv_packed = lax.ppermute((gain, packed), 'tm', pairs)]
    ppermute x11 -> x7, waiting for transfers between devices: 101 us -> 107 us  [send_element(): recv_gain, recv_packed = lax.ppermute((gain, packed), 'tm', pairs)]
  transfers between devices with their start and end apart: 11 -> 7, of which waited for: 10 -> 7; matrix products, arithmetic and copies ran while one was open for 3% -> 2% of each run, Pallas kernels for 0% -> 0%
where the time goes in v7:
time: 186 us
  waiting for transfers between devices  107 us (58%)
  Pallas kernels  28.5 us (15%)
  blocking collectives  23 us (12%)
  starting transfers between devices  10.5 us (6%)
  matrix products  8.98 us (5%)
  local copies, waits for them, and re-layouts  4.43 us (2%)
  other arithmetic  2.76 us (1%)
    ppermute x7, waiting for transfers between devices, send_element(): recv_gain, recv_packed = lax.ppermute((gain, packed), 'tm', pairs)  107 us
    all_gather x1, blocking collectives, shards(): gathered = lax.all_gather(packed, 'tm', tiled=True)  23 us
    pallas_call x1, Pallas kernels, run_filter(): pl.pallas_call(_filter_kernel, out_shape=(jax.ShapeDtypeStruct((1, width)...  14.5 us
    pallas_call x1, Pallas kernels, neg_inverse(): pl.pallas_call(_sweep_kernel, out_shape=jax.ShapeDtypeStruct((size, size)...  14 us
    ppermute x7, starting transfers between devices, send_element(): recv_gain, recv_packed = lax.ppermute((gain, packed), 'tm', pairs)  10.5 us
    dot_general x18, matrix products, matmul_hi(): return jnp.matmul(left, right, precision=HIGHEST)  8.98 us
  transfers between devices with their start and end apart: 7, of which 7 were waited for; matrix products, arithmetic and copies ran while one was open for 2% of the time, Pallas kernels for 0%

profile of v7, /device:TPU:1, one launch (start us, length us, event | category | flops | bytes accessed | tf_op | source)
XLA Modules:
  0.0 185.9 jit_solution(15265104139105726561)
XLA Ops:
  0.6 0.6 copy-done.2
  1.3 0.6 fusion.24
  1.9 0.9 copy.22.trans_col_ref
  2.8 0.7 copy-done.3
  3.5 23.0 %all_gather.3 = f32[16,2,128]{2,1,0:T(2,128)S(1)} all-gather(f32[1,2,128]{2,1,0:T(2,128)S(1)} %pad_maximum_fusion.8), channel_id=1, replica_groups=mesh['groups'=2,'tm'=16] {'tm'}, dimensions={0}, use_global_device_ids=true | all-gather | bytes 17408 | tf_op jit(solution)/shard_map/all_gather | solution.py:283
  26.4 0.6 fusion.26
  27.0 1.4 copy.21.root_col_ref
  28.4 0.1 multiply_multiply_fusion.1
  28.5 0.7 select_maximum_fusion
  29.3 14.5 %shard_map.68 = (f32[1,256]{1,0:T(1,128)S(1)}, f32[256,256]{1,0:T(8,128)S(1)}) custom-call(s32[1]{0:T(128)} %bitcast.16.count_ref, f32[16,128]{1,0:T(8,128)} %bitcast.125, f32[16,128]{1,0:T(8,128)} %bitcast.124, f32[16,128,1]{2,1,0:T(8,128)} %copy.21.root_col_ref, f32[4,128]{1,0:T(4,128)} %get-tuple-element.81.trans_row_ref, ...), custom_call_target="tpu_custom_call" | custom-call | tf_op jit(solution)/shard_map/pallas_call | solution.py:144
  43.8 17.7 %conditional.1 = (f32[1,256]{1,0:T(1,128)S(1)}, f32[256,256]{1,0:T(8,128)S(1)}, f32[256,256]{1,0:T(8,128)S(1)}) conditional(s32[]{:T(128)} %convert_element_type.12, (f32[128]{0:T(128)S(1)}, f32[1,256,256]{2,1,0:T(8,128)S(1)}, f32[128]{0:T(128)S(1)}, f32[128]{0:T(128)S(1)}, f32[128]{0:T(128)S(1)}, /*index=5*/f32[256,256]{1,0:T(8,128)S(1)}, s32[]{:T(128)}, ...), branch_computations={%region_0.1_spmd, %region_1.2_spmd} | conditional | flops 404358400 | bytes 5516342 | solution.py:328
  44.0 0.1 multiply_add_fusion.1
  44.1 0.1 copy.23
  44.4 0.1 add_bitcast_fusion.1
  44.5 0.7 maximum_add_fusion.a_ref
  45.2 14.0 %vmap__.2 = f32[256,256]{1,0:T(8,128)} custom-call(f32[256,256]{1,0:T(8,128)} %maximum_add_fusion.a_ref), custom_call_target="tpu_custom_call" | custom-call | tf_op jit(solution)/shard_map/cond/branch_0_fun/vmap()/pallas_call | solution.py:83
  59.2 1.5 fusion
  60.7 0.5 fusion.2
  61.2 0.3 convolution_subtract_fusion
  61.6 1.9 %collective-permute-start.3 = (f32[264,256]{1,0:T(8,128)S(1)}, f32[264,256]{1,0:T(8,128)S(1)}, u32[]{:S(2)}, u32[]{:S(2)}) collective-permute-start(f32[264,256]{1,0:T(8,128)S(1)} %pad_maximum_fusion.3), channel_id=1, source_target_pairs={{1,0},{2,1},{3,2},{4,3},{5,4},{6,5},{7,6},{8,7},{9,8},{10,9},{11,1... | collective-permute-start | bytes 811016 | tf_op jit(solution)/shard_map/ppermute | solution.py:269
  63.5 1.9 %collective-permute-start = (f32[256,256]{1,0:T(8,128)S(1)}, f32[256,256]{1,0:T(8,128)S(1)}, u32[]{:S(2)}, u32[]{:S(2)}) collective-permute-start(f32[256,256]{1,0:T(8,128)S(1)} %get-tuple-element.60), channel_id=1, source_target_pairs={{1,0},{2,1},{3,2},{4,3},{5,4},{6,5},{7,6},{8,7},{9,8},{10,9},{11,1... | collective-permute-start | bytes 786440 | tf_op jit(solution)/shard_map/ppermute | solution.py:269
  65.5 6.3 %collective-permute-done.3 = f32[264,256]{1,0:T(8,128)S(1)} collective-permute-done((f32[264,256]{1,0:T(8,128)S(1)}, f32[264,256]{1,0:T(8,128)S(1)}, u32[]{:S(2)}, u32[]{:S(2)}) %collective-permute-start.3) | collective-permute-done | bytes 270368 | tf_op jit(solution)/shard_map/ppermute | solution.py:269
  71.8 0.4 fusion.20
  72.2 0.4 convolution_add_fusion.3
  72.6 0.3 convolution_add_fusion.7
  73.0 1.5 collective-permute-start.4
  74.5 0.1 collective-permute-done
  74.6 0.4 fusion.27
  75.0 1.3 collective-permute-start.1
  76.3 17.6 %collective-permute-done.4 = f32[264,256]{1,0:T(8,128)S(1)} collective-permute-done((f32[264,256]{1,0:T(8,128)S(1)}, f32[264,256]{1,0:T(8,128)S(1)}, u32[]{:S(2)}, u32[]{:S(2)}) %collective-permute-start.4) | collective-permute-done | bytes 270368 | tf_op jit(solution)/shard_map/ppermute | solution.py:269
  93.9 0.4 fusion.18
  94.3 0.4 convolution_add_fusion.2
  94.7 0.3 convolution_add_fusion.6
  95.1 1.3 collective-permute-start.5
  96.4 0.3 collective-permute-done.1
  96.7 0.4 fusion.28
  97.1 1.3 collective-permute-start.2
  98.4 27.0 %collective-permute-done.5 = f32[264,256]{1,0:T(8,128)S(1)} collective-permute-done((f32[264,256]{1,0:T(8,128)S(1)}, f32[264,256]{1,0:T(8,128)S(1)}, u32[]{:S(2)}, u32[]{:S(2)}) %collective-permute-start.5) | collective-permute-done | bytes 270368 | tf_op jit(solution)/shard_map/ppermute | solution.py:269
  125.5 0.4 fusion.16
  125.8 0.4 convolution_add_fusion.1
  126.3 0.3 convolution_add_fusion.5
  126.6 1.3 collective-permute-start.6
  127.9 0.3 collective-permute-done.2
  128.3 0.4 fusion.29
  128.6 54.8 %collective-permute-done.6 = f32[264,256]{1,0:T(8,128)S(1)} collective-permute-done((f32[264,256]{1,0:T(8,128)S(1)}, f32[264,256]{1,0:T(8,128)S(1)}, u32[]{:S(2)}, u32[]{:S(2)}) %collective-permute-start.6) | collective-permute-done | bytes 270368 | tf_op jit(solution)/shard_map/ppermute | solution.py:269
  183.5 0.4 fusion.14
  183.9 1.1 fusion.13
  185.0 0.9 convolution_add_fusion.4
  (25 shorter events, 0.5 us)
Async XLA Ops:
  0.6 0.7 copy-start.2
  1.9 0.9 copy-start.4
  1.9 0.9 copy-start.5
  2.8 0.7 copy-start.3
  27.0 1.4 copy-start.1
  27.0 1.4 copy-start
  61.6 10.2 %collective-permute-start.3 = (f32[264,256]{1,0:T(8,128)S(1)}, f32[264,256]{1,0:T(8,128)S(1)}, u32[]{:S(2)}, u32[]{:S(2)}) collective-permute-start(f32[264,256]{1,0:T(8,128)S(1)} %pad_maximum_fusion.3), channel_id=1, source_target_pairs={{1,0},{2,1},{3,2},{4,3},{5,4},{6,5},{7,6},{8,7},{9,8},{10,9},{11,1... | collective-permute-start | bytes 811016 | tf_op jit(solution)/shard_map/ppermute | solution.py:269
  63.5 11.1 %collective-permute-start = (f32[256,256]{1,0:T(8,128)S(1)}, f32[256,256]{1,0:T(8,128)S(1)}, u32[]{:S(2)}, u32[]{:S(2)}) collective-permute-start(f32[256,256]{1,0:T(8,128)S(1)} %get-tuple-element.60), channel_id=1, source_target_pairs={{1,0},{2,1},{3,2},{4,3},{5,4},{6,5},{7,6},{8,7},{9,8},{10,9},{11,1... | collective-permute-start | bytes 786440 | tf_op jit(solution)/shard_map/ppermute | solution.py:269
  73.0 21.0 %collective-permute-start.4 = (f32[264,256]{1,0:T(8,128)S(1)}, f32[264,256]{1,0:T(8,128)S(1)}, u32[]{:S(2)}, u32[]{:S(2)}) collective-permute-start(f32[264,256]{1,0:T(8,128)S(1)} %pad_maximum_fusion.4), channel_id=1, source_target_pairs={{2,0},{3,1},{4,2},{5,3},{6,4},{7,5},{8,6},{9,7},{10,8},{11,9},{12,... | collective-permute-start | bytes 811016 | tf_op jit(solution)/shard_map/ppermute | solution.py:269
  75.0 21.7 %collective-permute-start.1 = (f32[256,256]{1,0:T(8,128)S(1)}, f32[256,256]{1,0:T(8,128)S(1)}, u32[]{:S(2)}, u32[]{:S(2)}) collective-permute-start(f32[256,256]{1,0:T(8,128)S(1)} %fusion.27), channel_id=1, source_target_pairs={{2,0},{3,1},{4,2},{5,3},{6,4},{7,5},{8,6},{9,7},{10,8},{11,9},{12,... | collective-permute-start | bytes 786440 | tf_op jit(solution)/shard_map/ppermute | solution.py:269
  95.1 30.4 %collective-permute-start.5 = (f32[264,256]{1,0:T(8,128)S(1)}, f32[264,256]{1,0:T(8,128)S(1)}, u32[]{:S(2)}, u32[]{:S(2)}) collective-permute-start(f32[264,256]{1,0:T(8,128)S(1)} %pad_maximum_fusion.5), channel_id=1, source_target_pairs={{4,0},{5,1},{6,2},{7,3},{8,4},{9,5},{10,6},{11,7},{12,8},{13,9},{1... | collective-permute-start | bytes 811016 | tf_op jit(solution)/shard_map/ppermute | solution.py:269
  97.1 31.2 %collective-permute-start.2 = (f32[256,256]{1,0:T(8,128)S(1)}, f32[256,256]{1,0:T(8,128)S(1)}, u32[]{:S(2)}, u32[]{:S(2)}) collective-permute-start(f32[256,256]{1,0:T(8,128)S(1)} %fusion.28), channel_id=1, source_target_pairs={{4,0},{5,1},{6,2},{7,3},{8,4},{9,5},{10,6},{11,7},{12,8},{13,9},{1... | collective-permute-start | bytes 786440 | tf_op jit(solution)/shard_map/ppermute | solution.py:269
  126.6 56.9 %collective-permute-start.6 = (f32[264,256]{1,0:T(8,128)S(1)}, f32[264,256]{1,0:T(8,128)S(1)}, u32[]{:S(2)}, u32[]{:S(2)}) collective-permute-start(f32[264,256]{1,0:T(8,128)S(1)} %pad_maximum_fusion.6), channel_id=1, source_target_pairs={{8,0},{9,1},{10,2},{11,3},{12,4},{13,5},{14,6},{15,7},{24,16},{25,... | collective-permute-start | bytes 811016 | tf_op jit(solution)/shard_map/ppermute | solution.py:269

commit v8 on v7

--- a/solution.py
+++ b/solution.py
@@ -6,6 +6,7 @@
 from jax.sharding import PartitionSpec as P
 
 HIGHEST = lax.Precision.HIGHEST
+KERNEL_PRECISION = lax.Precision.HIGH
 JITTER = 0.001
 PANEL = 32
 
@@ -41,6 +42,7 @@
 def _sweep_in_place(o_ref):
     n = o_ref.shape[0]
     PANEL = 64 if n >= 256 else 32
+    precision = HIGHEST if n >= 256 else KERNEL_PRECISION
     sub = lax.broadcasted_iota(jnp.int32, (PANEL, n), 0)
     lane = lax.broadcasted_iota(jnp.int32, (PANEL, n), 1)
     sub_col = lax.broadcasted_iota(jnp.int32, (PANEL, 1), 0)
@@ -72,7 +74,7 @@
                 rest = jnp.where(rows[i], row_val, rest)
             panel = rest
         full = o_ref[...]
-        update = lax.dot_general(orig, panel, (((0,), (0,)), ((), ())), precision=HIGHEST,
+        update = lax.dot_general(orig, panel, (((0,), (0,)), ((), ())), precision=precision,
                                  preferred_element_type=jnp.float32)
         in_blk = (lane_full >= base) & (lane_full < base + PANEL)
         o_ref[...] = jnp.where(in_blk, 0.0, full) - update
@@ -124,14 +126,14 @@
         normal_ref[...] = eye + r_col * cov_pred[:points, :points] * r_row
         _sweep_in_place(normal_ref)
         scaled = r_col * cov_pred[:points, :]
-        solved = jnp.dot(normal_ref[...], scaled, precision=HIGHEST, preferred_element_type=jnp.float32)
+        solved = jnp.dot(normal_ref[...], scaled, precision=KERNEL_PRECISION, preferred_element_type=jnp.float32)
         correction = lax.dot_general(
-            scaled, solved, (((0,), (0,)), ((), ())), precision=HIGHEST,
+            scaled, solved, (((0,), (0,)), ((), ())), precision=KERNEL_PRECISION,
             preferred_element_type=jnp.float32,
         )
         cov_ref[...] = cov_pred + correction
         innovation = jnp.broadcast_to(r_row * (obs_row - mean_pred[:, :points]), (8, points))
-        mean_shift = jnp.dot(innovation, solved, precision=HIGHEST, preferred_element_type=jnp.float32)
+        mean_shift = jnp.dot(innovation, solved, precision=KERNEL_PRECISION, preferred_element_type=jnp.float32)
         return mean_pred - mean_shift[0:1, :]
 
     mean_ref[...] = lax.fori_loop(0, count_ref[0], step, jnp.zeros((1, 2 * points), jnp.float32))

time: 186 us -> 179 us (0.962)
  waiting for transfers between devices: 107 us -> 100 us
    ppermute x7, waiting for transfers between devices: 107 us -> 100 us  [send_element(): recv_gain, recv_packed = lax.ppermute((gain, packed), 'tm', pairs)]
  transfers between devices with their start and end apart: 7 -> 7, of which waited for: 7 -> 7; matrix products, arithmetic and copies ran while one was open for 2% -> 3% of each run, Pallas kernels for 0% -> 0%
where the time goes in v8:
time: 179 us; the launch traced here: 178 us
  waiting for transfers between devices  100 us (56%)
  Pallas kernels  27.5 us (15%)
  blocking collectives  23 us (13%)
  starting transfers between devices  10.5 us (6%)
  matrix products  8.99 us (5%)
  local copies, waits for them, and re-layouts  4.43 us (2%)
  other arithmetic  2.76 us (2%)
    ppermute x7, waiting for transfers between devices, send_element(): recv_gain, recv_packed = lax.ppermute((gain, packed), 'tm', pairs)  100 us
    all_gather x1, blocking collectives, shards(): gathered = lax.all_gather(packed, 'tm', tiled=True)  23 us
    pallas_call x1, Pallas kernels, neg_inverse(): pl.pallas_call(_sweep_kernel, out_shape=jax.ShapeDtypeStruct((size, size)...  14 us
    pallas_call x1, Pallas kernels, run_filter(): pl.pallas_call(_filter_kernel, out_shape=(jax.ShapeDtypeStruct((1, width)...  13.5 us
    ppermute x7, starting transfers between devices, send_element(): recv_gain, recv_packed = lax.ppermute((gain, packed), 'tm', pairs)  10.5 us
    dot_general x18, matrix products, matmul_hi(): return jnp.matmul(left, right, precision=HIGHEST)  8.99 us
  transfers between devices with their start and end apart: 7, of which 7 were waited for; matrix products, arithmetic and copies ran while one was open for 3% of the time, Pallas kernels for 0%

profile of v8, /device:TPU:1, one launch (start us, length us, event | category | flops | bytes accessed | tf_op | source)
XLA Modules:
  0.0 178.4 jit_solution(17768584847324388100)
XLA Ops:
  0.6 0.6 copy-done.2
  1.3 0.6 fusion.24
  1.9 0.9 copy.22.trans_col_ref
  2.8 0.7 copy-done.3
  3.5 23.0 %all_gather.3 = f32[16,2,128]{2,1,0:T(2,128)S(1)} all-gather(f32[1,2,128]{2,1,0:T(2,128)S(1)} %pad_maximum_fusion.8), channel_id=1, replica_groups=mesh['groups'=2,'tm'=16] {'tm'}, dimensions={0}, use_global_device_ids=true | all-gather | bytes 17408 | tf_op jit(solution)/shard_map/all_gather | solution.py:285
  26.4 0.6 fusion.26
  27.0 1.4 copy.21.root_col_ref
  28.4 0.1 multiply_multiply_fusion.1
  28.5 0.7 select_maximum_fusion
  29.3 13.5 %shard_map.68 = (f32[1,256]{1,0:T(1,128)S(1)}, f32[256,256]{1,0:T(8,128)S(1)}) custom-call(s32[1]{0:T(128)} %bitcast.16.count_ref, f32[16,128]{1,0:T(8,128)} %bitcast.125, f32[16,128]{1,0:T(8,128)} %bitcast.124, f32[16,128,1]{2,1,0:T(8,128)} %copy.21.root_col_ref, f32[4,128]{1,0:T(4,128)} %get-tuple-element.81.trans_row_ref, ...), custom_call_target="tpu_custom_call" | custom-call | tf_op jit(solution)/shard_map/pallas_call | solution.py:146
  42.8 17.7 %conditional.1 = (f32[1,256]{1,0:T(1,128)S(1)}, f32[256,256]{1,0:T(8,128)S(1)}, f32[256,256]{1,0:T(8,128)S(1)}) conditional(s32[]{:T(128)} %convert_element_type.12, (f32[128]{0:T(128)S(1)}, f32[1,256,256]{2,1,0:T(8,128)S(1)}, f32[128]{0:T(128)S(1)}, f32[128]{0:T(128)S(1)}, f32[128]{0:T(128)S(1)}, /*index=5*/f32[256,256]{1,0:T(8,128)S(1)}, s32[]{:T(128)}, ...), branch_computations={%region_0.1_spmd, %region_1.2_spmd} | conditional | flops 404358400 | bytes 5516342 | solution.py:330
  43.0 0.1 multiply_add_fusion.1
  43.1 0.1 copy.23
  43.4 0.1 add_bitcast_fusion.1
  43.5 0.7 maximum_add_fusion.a_ref
  44.2 14.0 %vmap__.2 = f32[256,256]{1,0:T(8,128)} custom-call(f32[256,256]{1,0:T(8,128)} %maximum_add_fusion.a_ref), custom_call_target="tpu_custom_call" | custom-call | tf_op jit(solution)/shard_map/cond/branch_0_fun/vmap()/pallas_call | solution.py:85
  58.2 1.5 fusion
  59.7 0.5 fusion.2
  60.2 0.3 convolution_subtract_fusion
  60.6 1.9 %collective-permute-start.3 = (f32[264,256]{1,0:T(8,128)S(1)}, f32[264,256]{1,0:T(8,128)S(1)}, u32[]{:S(2)}, u32[]{:S(2)}) collective-permute-start(f32[264,256]{1,0:T(8,128)S(1)} %pad_maximum_fusion.3), channel_id=1, source_target_pairs={{1,0},{2,1},{3,2},{4,3},{5,4},{6,5},{7,6},{8,7},{9,8},{10,9},{11,1... | collective-permute-start | bytes 811016 | tf_op jit(solution)/shard_map/ppermute | solution.py:271
  62.5 1.9 %collective-permute-start = (f32[256,256]{1,0:T(8,128)S(1)}, f32[256,256]{1,0:T(8,128)S(1)}, u32[]{:S(2)}, u32[]{:S(2)}) collective-permute-start(f32[256,256]{1,0:T(8,128)S(1)} %get-tuple-element.60), channel_id=1, source_target_pairs={{1,0},{2,1},{3,2},{4,3},{5,4},{6,5},{7,6},{8,7},{9,8},{10,9},{11,1... | collective-permute-start | bytes 786440 | tf_op jit(solution)/shard_map/ppermute | solution.py:271
  64.5 5.8 %collective-permute-done.3 = f32[264,256]{1,0:T(8,128)S(1)} collective-permute-done((f32[264,256]{1,0:T(8,128)S(1)}, f32[264,256]{1,0:T(8,128)S(1)}, u32[]{:S(2)}, u32[]{:S(2)}) %collective-permute-start.3) | collective-permute-done | bytes 270368 | tf_op jit(solution)/shard_map/ppermute | solution.py:271
  70.3 0.4 fusion.20
  70.7 0.4 convolution_add_fusion.3
  71.1 0.3 convolution_add_fusion.7
  71.5 1.5 collective-permute-start.4
  73.0 0.1 collective-permute-done
  73.1 0.4 fusion.27
  73.5 1.3 collective-permute-start.1
  74.8 16.6 %collective-permute-done.4 = f32[264,256]{1,0:T(8,128)S(1)} collective-permute-done((f32[264,256]{1,0:T(8,128)S(1)}, f32[264,256]{1,0:T(8,128)S(1)}, u32[]{:S(2)}, u32[]{:S(2)}) %collective-permute-start.4) | collective-permute-done | bytes 270368 | tf_op jit(solution)/shard_map/ppermute | solution.py:271
  91.4 0.4 fusion.18
  91.8 0.4 convolution_add_fusion.2
  92.2 0.3 convolution_add_fusion.6
  92.6 1.3 collective-permute-start.5
  93.9 0.3 collective-permute-done.1
  94.2 0.4 fusion.28
  94.6 1.3 collective-permute-start.2
  95.9 25.1 %collective-permute-done.5 = f32[264,256]{1,0:T(8,128)S(1)} collective-permute-done((f32[264,256]{1,0:T(8,128)S(1)}, f32[264,256]{1,0:T(8,128)S(1)}, u32[]{:S(2)}, u32[]{:S(2)}) %collective-permute-start.5) | collective-permute-done | bytes 270368 | tf_op jit(solution)/shard_map/ppermute | solution.py:271
  121.0 0.4 fusion.16
  121.3 0.4 convolution_add_fusion.1
  121.8 0.3 convolution_add_fusion.5
  122.1 1.3 collective-permute-start.6
  123.4 0.3 collective-permute-done.2
  123.8 0.4 fusion.29
  124.2 51.8 %collective-permute-done.6 = f32[264,256]{1,0:T(8,128)S(1)} collective-permute-done((f32[264,256]{1,0:T(8,128)S(1)}, f32[264,256]{1,0:T(8,128)S(1)}, u32[]{:S(2)}, u32[]{:S(2)}) %collective-permute-start.6) | collective-permute-done | bytes 270368 | tf_op jit(solution)/shard_map/ppermute | solution.py:271
  176.0 0.4 fusion.14
  176.4 1.1 fusion.13
  177.5 0.9 convolution_add_fusion.4
  (25 shorter events, 0.5 us)
Async XLA Ops:
  0.6 0.7 copy-start.2
  1.9 0.9 copy-start.4
  1.9 0.9 copy-start.5
  2.8 0.7 copy-start.3
  27.0 1.4 copy-start.1
  27.0 1.4 copy-start
  60.6 9.7 %collective-permute-start.3 = (f32[264,256]{1,0:T(8,128)S(1)}, f32[264,256]{1,0:T(8,128)S(1)}, u32[]{:S(2)}, u32[]{:S(2)}) collective-permute-start(f32[264,256]{1,0:T(8,128)S(1)} %pad_maximum_fusion.3), channel_id=1, source_target_pairs={{1,0},{2,1},{3,2},{4,3},{5,4},{6,5},{7,6},{8,7},{9,8},{10,9},{11,1... | collective-permute-start | bytes 811016 | tf_op jit(solution)/shard_map/ppermute | solution.py:271
  62.5 10.6 %collective-permute-start = (f32[256,256]{1,0:T(8,128)S(1)}, f32[256,256]{1,0:T(8,128)S(1)}, u32[]{:S(2)}, u32[]{:S(2)}) collective-permute-start(f32[256,256]{1,0:T(8,128)S(1)} %get-tuple-element.60), channel_id=1, source_target_pairs={{1,0},{2,1},{3,2},{4,3},{5,4},{6,5},{7,6},{8,7},{9,8},{10,9},{11,1... | collective-permute-start | bytes 786440 | tf_op jit(solution)/shard_map/ppermute | solution.py:271
  71.5 20.0 %collective-permute-start.4 = (f32[264,256]{1,0:T(8,128)S(1)}, f32[264,256]{1,0:T(8,128)S(1)}, u32[]{:S(2)}, u32[]{:S(2)}) collective-permute-start(f32[264,256]{1,0:T(8,128)S(1)} %pad_maximum_fusion.4), channel_id=1, source_target_pairs={{2,0},{3,1},{4,2},{5,3},{6,4},{7,5},{8,6},{9,7},{10,8},{11,9},{12,... | collective-permute-start | bytes 811016 | tf_op jit(solution)/shard_map/ppermute | solution.py:271
  73.5 20.7 %collective-permute-start.1 = (f32[256,256]{1,0:T(8,128)S(1)}, f32[256,256]{1,0:T(8,128)S(1)}, u32[]{:S(2)}, u32[]{:S(2)}) collective-permute-start(f32[256,256]{1,0:T(8,128)S(1)} %fusion.27), channel_id=1, source_target_pairs={{2,0},{3,1},{4,2},{5,3},{6,4},{7,5},{8,6},{9,7},{10,8},{11,9},{12,... | collective-permute-start | bytes 786440 | tf_op jit(solution)/shard_map/ppermute | solution.py:271
  92.6 28.4 %collective-permute-start.5 = (f32[264,256]{1,0:T(8,128)S(1)}, f32[264,256]{1,0:T(8,128)S(1)}, u32[]{:S(2)}, u32[]{:S(2)}) collective-permute-start(f32[264,256]{1,0:T(8,128)S(1)} %pad_maximum_fusion.5), channel_id=1, source_target_pairs={{4,0},{5,1},{6,2},{7,3},{8,4},{9,5},{10,6},{11,7},{12,8},{13,9},{1... | collective-permute-start | bytes 811016 | tf_op jit(solution)/shard_map/ppermute | solution.py:271
  94.6 29.2 %collective-permute-start.2 = (f32[256,256]{1,0:T(8,128)S(1)}, f32[256,256]{1,0:T(8,128)S(1)}, u32[]{:S(2)}, u32[]{:S(2)}) collective-permute-start(f32[256,256]{1,0:T(8,128)S(1)} %fusion.28), channel_id=1, source_target_pairs={{4,0},{5,1},{6,2},{7,3},{8,4},{9,5},{10,6},{11,7},{12,8},{13,9},{1... | collective-permute-start | bytes 786440 | tf_op jit(solution)/shard_map/ppermute | solution.py:271
  122.1 53.9 %collective-permute-start.6 = (f32[264,256]{1,0:T(8,128)S(1)}, f32[264,256]{1,0:T(8,128)S(1)}, u32[]{:S(2)}, u32[]{:S(2)}) collective-permute-start(f32[264,256]{1,0:T(8,128)S(1)} %pad_maximum_fusion.6), channel_id=1, source_target_pairs={{8,0},{9,1},{10,2},{11,3},{12,4},{13,5},{14,6},{15,7},{24,16},{25,... | collective-permute-start | bytes 811016 | tf_op jit(solution)/shard_map/ppermute | solution.py:271

commit v9 on v8

--- a/solution.py
+++ b/solution.py
@@ -128,12 +128,12 @@
         scaled = r_col * cov_pred[:points, :]
         solved = jnp.dot(normal_ref[...], scaled, precision=KERNEL_PRECISION, preferred_element_type=jnp.float32)
         correction = lax.dot_general(
-            scaled, solved, (((0,), (0,)), ((), ())), precision=KERNEL_PRECISION,
+            scaled, solved, (((0,), (0,)), ((), ())), precision=HIGHEST,
             preferred_element_type=jnp.float32,
         )
         cov_ref[...] = cov_pred + correction
         innovation = jnp.broadcast_to(r_row * (obs_row - mean_pred[:, :points]), (8, points))
-        mean_shift = jnp.dot(innovation, solved, precision=KERNEL_PRECISION, preferred_element_type=jnp.float32)
+        mean_shift = jnp.dot(innovation, solved, precision=HIGHEST, preferred_element_type=jnp.float32)
         return mean_pred - mean_shift[0:1, :]
 
     mean_ref[...] = lax.fori_loop(0, count_ref[0], step, jnp.zeros((1, 2 * points), jnp.float32))

time: 179 us -> 181 us (1.011)
  waiting for transfers between devices: 100 us -> 102 us
where the time goes in v9:
time: 181 us; the launch traced here: 180 us
  waiting for transfers between devices  102 us (56%)
  Pallas kernels  27.7 us (15%)
  blocking collectives  23 us (13%)
  starting transfers between devices  10.5 us (6%)
  matrix products  8.98 us (5%)
  local copies, waits for them, and re-layouts  4.43 us (2%)
  other arithmetic  2.76 us (2%)
    ppermute x7, waiting for transfers between devices, send_element(): recv_gain, recv_packed = lax.ppermute((gain, packed), 'tm', pairs)  102 us
    all_gather x1, blocking collectives, shards(): gathered = lax.all_gather(packed, 'tm', tiled=True)  23 us
    pallas_call x1, Pallas kernels, neg_inverse(): pl.pallas_call(_sweep_kernel, out_shape=jax.ShapeDtypeStruct((size, size)...  14 us
    pallas_call x1, Pallas kernels, run_filter(): pl.pallas_call(_filter_kernel, out_shape=(jax.ShapeDtypeStruct((1, width)...  13.8 us
    ppermute x7, starting transfers between devices, send_element(): recv_gain, recv_packed = lax.ppermute((gain, packed), 'tm', pairs)  10.5 us
    dot_general x18, matrix products, matmul_hi(): return jnp.matmul(left, right, precision=HIGHEST)  8.98 us
  transfers between devices with their start and end apart: 7, of which 7 were waited for; matrix products, arithmetic and copies ran while one was open for 3% of the time, Pallas kernels for 0%

profile of v9, /device:TPU:1, one launch (start us, length us, event | category | flops | bytes accessed | tf_op | source)
XLA Modules:
  0.0 180.4 jit_solution(11601181660114284263)
XLA Ops:
  0.6 0.6 copy-done.2
  1.3 0.6 fusion.24
  1.9 0.9 copy.22.trans_col_ref
  2.8 0.7 copy-done.3
  3.5 23.0 %all_gather.3 = f32[16,2,128]{2,1,0:T(2,128)S(1)} all-gather(f32[1,2,128]{2,1,0:T(2,128)S(1)} %pad_maximum_fusion.8), channel_id=1, replica_groups=mesh['groups'=2,'tm'=16] {'tm'}, dimensions={0}, use_global_device_ids=true | all-gather | bytes 17408 | tf_op jit(solution)/shard_map/all_gather | solution.py:285
  26.4 0.6 fusion.26
  27.0 1.4 copy.21.root_col_ref
  28.4 0.1 multiply_multiply_fusion.1
  28.5 0.7 select_maximum_fusion
  29.3 13.8 %shard_map.68 = (f32[1,256]{1,0:T(1,128)S(1)}, f32[256,256]{1,0:T(8,128)S(1)}) custom-call(s32[1]{0:T(128)} %bitcast.16.count_ref, f32[16,128]{1,0:T(8,128)} %bitcast.125, f32[16,128]{1,0:T(8,128)} %bitcast.124, f32[16,128,1]{2,1,0:T(8,128)} %copy.21.root_col_ref, f32[4,128]{1,0:T(4,128)} %get-tuple-element.81.trans_row_ref, ...), custom_call_target="tpu_custom_call" | custom-call | tf_op jit(solution)/shard_map/pallas_call | solution.py:146
  43.0 17.7 %conditional.1 = (f32[1,256]{1,0:T(1,128)S(1)}, f32[256,256]{1,0:T(8,128)S(1)}, f32[256,256]{1,0:T(8,128)S(1)}) conditional(s32[]{:T(128)} %convert_element_type.12, (f32[128]{0:T(128)S(1)}, f32[1,256,256]{2,1,0:T(8,128)S(1)}, f32[128]{0:T(128)S(1)}, f32[128]{0:T(128)S(1)}, f32[128]{0:T(128)S(1)}, /*index=5*/f32[256,256]{1,0:T(8,128)S(1)}, s32[]{:T(128)}, ...), branch_computations={%region_0.1_spmd, %region_1.2_spmd} | conditional | flops 404358400 | bytes 5516342 | solution.py:330
  43.2 0.1 multiply_add_fusion.1
  43.4 0.1 copy.23
  43.6 0.1 add_bitcast_fusion.1
  43.8 0.7 maximum_add_fusion.a_ref
  44.5 14.0 %vmap__.2 = f32[256,256]{1,0:T(8,128)} custom-call(f32[256,256]{1,0:T(8,128)} %maximum_add_fusion.a_ref), custom_call_target="tpu_custom_call" | custom-call | tf_op jit(solution)/shard_map/cond/branch_0_fun/vmap()/pallas_call | solution.py:85
  58.5 1.5 fusion
  60.0 0.5 fusion.2
  60.5 0.3 convolution_subtract_fusion
  60.9 1.9 %collective-permute-start.3 = (f32[264,256]{1,0:T(8,128)S(1)}, f32[264,256]{1,0:T(8,128)S(1)}, u32[]{:S(2)}, u32[]{:S(2)}) collective-permute-start(f32[264,256]{1,0:T(8,128)S(1)} %pad_maximum_fusion.3), channel_id=1, source_target_pairs={{1,0},{2,1},{3,2},{4,3},{5,4},{6,5},{7,6},{8,7},{9,8},{10,9},{11,1... | collective-permute-start | bytes 811016 | tf_op jit(solution)/shard_map/ppermute | solution.py:271
  62.8 1.9 %collective-permute-start = (f32[256,256]{1,0:T(8,128)S(1)}, f32[256,256]{1,0:T(8,128)S(1)}, u32[]{:S(2)}, u32[]{:S(2)}) collective-permute-start(f32[256,256]{1,0:T(8,128)S(1)} %get-tuple-element.60), channel_id=1, source_target_pairs={{1,0},{2,1},{3,2},{4,3},{5,4},{6,5},{7,6},{8,7},{9,8},{10,9},{11,1... | collective-permute-start | bytes 786440 | tf_op jit(solution)/shard_map/ppermute | solution.py:271
  64.7 6.0 %collective-permute-done.3 = f32[264,256]{1,0:T(8,128)S(1)} collective-permute-done((f32[264,256]{1,0:T(8,128)S(1)}, f32[264,256]{1,0:T(8,128)S(1)}, u32[]{:S(2)}, u32[]{:S(2)}) %collective-permute-start.3) | collective-permute-done | bytes 270368 | tf_op jit(solution)/shard_map/ppermute | solution.py:271
  70.7 0.4 fusion.20
  71.1 0.4 convolution_add_fusion.3
  71.5 0.3 convolution_add_fusion.7
  71.9 1.5 collective-permute-start.4
  73.4 0.1 collective-permute-done
  73.5 0.4 fusion.27
  73.9 1.3 collective-permute-start.1
  75.2 16.9 %collective-permute-done.4 = f32[264,256]{1,0:T(8,128)S(1)} collective-permute-done((f32[264,256]{1,0:T(8,128)S(1)}, f32[264,256]{1,0:T(8,128)S(1)}, u32[]{:S(2)}, u32[]{:S(2)}) %collective-permute-start.4) | collective-permute-done | bytes 270368 | tf_op jit(solution)/shard_map/ppermute | solution.py:271
  92.1 0.4 fusion.18
  92.5 0.4 convolution_add_fusion.2
  92.9 0.3 convolution_add_fusion.6
  93.3 1.3 collective-permute-start.5
  94.6 0.3 collective-permute-done.1
  94.9 0.4 fusion.28
  95.3 1.3 collective-permute-start.2
  96.6 25.6 %collective-permute-done.5 = f32[264,256]{1,0:T(8,128)S(1)} collective-permute-done((f32[264,256]{1,0:T(8,128)S(1)}, f32[264,256]{1,0:T(8,128)S(1)}, u32[]{:S(2)}, u32[]{:S(2)}) %collective-permute-start.5) | collective-permute-done | bytes 270368 | tf_op jit(solution)/shard_map/ppermute | solution.py:271
  122.2 0.4 fusion.16
  122.6 0.4 convolution_add_fusion.1
  123.0 0.3 convolution_add_fusion.5
  123.4 1.3 collective-permute-start.6
  124.7 0.3 collective-permute-done.2
  125.0 0.4 fusion.29
  125.4 52.7 %collective-permute-done.6 = f32[264,256]{1,0:T(8,128)S(1)} collective-permute-done((f32[264,256]{1,0:T(8,128)S(1)}, f32[264,256]{1,0:T(8,128)S(1)}, u32[]{:S(2)}, u32[]{:S(2)}) %collective-permute-start.6) | collective-permute-done | bytes 270368 | tf_op jit(solution)/shard_map/ppermute | solution.py:271
  178.1 0.4 fusion.14
  178.4 1.1 fusion.13
  179.6 0.9 convolution_add_fusion.4
  (25 shorter events, 0.5 us)
Async XLA Ops:
  0.6 0.7 copy-start.2
  1.9 0.9 copy-start.4
  1.9 0.9 copy-start.5
  2.8 0.7 copy-start.3
  27.0 1.4 copy-start.1
  27.0 1.4 copy-start
  60.9 9.9 %collective-permute-start.3 = (f32[264,256]{1,0:T(8,128)S(1)}, f32[264,256]{1,0:T(8,128)S(1)}, u32[]{:S(2)}, u32[]{:S(2)}) collective-permute-start(f32[264,256]{1,0:T(8,128)S(1)} %pad_maximum_fusion.3), channel_id=1, source_target_pairs={{1,0},{2,1},{3,2},{4,3},{5,4},{6,5},{7,6},{8,7},{9,8},{10,9},{11,1... | collective-permute-start | bytes 811016 | tf_op jit(solution)/shard_map/ppermute | solution.py:271
  62.8 10.7 %collective-permute-start = (f32[256,256]{1,0:T(8,128)S(1)}, f32[256,256]{1,0:T(8,128)S(1)}, u32[]{:S(2)}, u32[]{:S(2)}) collective-permute-start(f32[256,256]{1,0:T(8,128)S(1)} %get-tuple-element.60), channel_id=1, source_target_pairs={{1,0},{2,1},{3,2},{4,3},{5,4},{6,5},{7,6},{8,7},{9,8},{10,9},{11,1... | collective-permute-start | bytes 786440 | tf_op jit(solution)/shard_map/ppermute | solution.py:271
  71.9 20.2 %collective-permute-start.4 = (f32[264,256]{1,0:T(8,128)S(1)}, f32[264,256]{1,0:T(8,128)S(1)}, u32[]{:S(2)}, u32[]{:S(2)}) collective-permute-start(f32[264,256]{1,0:T(8,128)S(1)} %pad_maximum_fusion.4), channel_id=1, source_target_pairs={{2,0},{3,1},{4,2},{5,3},{6,4},{7,5},{8,6},{9,7},{10,8},{11,9},{12,... | collective-permute-start | bytes 811016 | tf_op jit(solution)/shard_map/ppermute | solution.py:271
  73.9 21.0 %collective-permute-start.1 = (f32[256,256]{1,0:T(8,128)S(1)}, f32[256,256]{1,0:T(8,128)S(1)}, u32[]{:S(2)}, u32[]{:S(2)}) collective-permute-start(f32[256,256]{1,0:T(8,128)S(1)} %fusion.27), channel_id=1, source_target_pairs={{2,0},{3,1},{4,2},{5,3},{6,4},{7,5},{8,6},{9,7},{10,8},{11,9},{12,... | collective-permute-start | bytes 786440 | tf_op jit(solution)/shard_map/ppermute | solution.py:271
  93.3 28.9 %collective-permute-start.5 = (f32[264,256]{1,0:T(8,128)S(1)}, f32[264,256]{1,0:T(8,128)S(1)}, u32[]{:S(2)}, u32[]{:S(2)}) collective-permute-start(f32[264,256]{1,0:T(8,128)S(1)} %pad_maximum_fusion.5), channel_id=1, source_target_pairs={{4,0},{5,1},{6,2},{7,3},{8,4},{9,5},{10,6},{11,7},{12,8},{13,9},{1... | collective-permute-start | bytes 811016 | tf_op jit(solution)/shard_map/ppermute | solution.py:271
  95.3 29.7 %collective-permute-start.2 = (f32[256,256]{1,0:T(8,128)S(1)}, f32[256,256]{1,0:T(8,128)S(1)}, u32[]{:S(2)}, u32[]{:S(2)}) collective-permute-start(f32[256,256]{1,0:T(8,128)S(1)} %fusion.28), channel_id=1, source_target_pairs={{4,0},{5,1},{6,2},{7,3},{8,4},{9,5},{10,6},{11,7},{12,8},{13,9},{1... | collective-permute-start | bytes 786440 | tf_op jit(solution)/shard_map/ppermute | solution.py:271
  123.4 54.7 %collective-permute-start.6 = (f32[264,256]{1,0:T(8,128)S(1)}, f32[264,256]{1,0:T(8,128)S(1)}, u32[]{:S(2)}, u32[]{:S(2)}) collective-permute-start(f32[264,256]{1,0:T(8,128)S(1)} %pad_maximum_fusion.6), channel_id=1, source_target_pairs={{8,0},{9,1},{10,2},{11,3},{12,4},{13,5},{14,6},{15,7},{24,16},{25,... | collective-permute-start | bytes 811016 | tf_op jit(solution)/shard_map/ppermute | solution.py:271

commit v10 on v7

--- a/solution.py
+++ b/solution.py
@@ -90,7 +90,8 @@
 
 def _filter_kernel(
     count_ref, obs_ref, root_row_ref, root_col_ref, trans_row_ref, trans_col_ref, process_ref,
-    prior_ref, mean_ref, cov_ref, pred_ref, normal_ref,
+    prior_ref, mean_ref, cov_ref, gain_ref, shift_mean_ref, shift_cov_ref, pred_ref, normal_ref,
+    forward_ref, wide_ref,
 ):
     points = obs_ref.shape[1]
     eye = (
@@ -134,27 +135,68 @@
         mean_shift = jnp.dot(innovation, solved, precision=HIGHEST, preferred_element_type=jnp.float32)
         return mean_pred - mean_shift[0:1, :]
 
-    mean_ref[...] = lax.fori_loop(0, count_ref[0], step, jnp.zeros((1, 2 * points), jnp.float32))
-
-
-def run_filter(count, obs_all, root_all, transit, process, prior):
+    mean_last = lax.fori_loop(0, count_ref[0], step, jnp.zeros((1, 2 * points), jnp.float32))
+    mean_ref[...] = mean_last
+
+    @pl.when(count_ref[1] == 0)
+    def _final_step():
+        gain_ref[...] = jnp.zeros_like(gain_ref)
+        shift_mean_ref[...] = mean_last
+        shift_cov_ref[...] = cov_ref[...]
+
+    @pl.when(count_ref[1] != 0)
+    def _smoother_element():
+        top = cov_ref[:points, :]
+        bottom = cov_ref[points:, :]
+        forward_ref[:points, :] = a_col * top + b_col * bottom
+        forward_ref[points:, :] = c_col * top + d_col * bottom
+        forward = forward_ref[...]
+        f_left = forward[:, :points]
+        f_right = forward[:, points:]
+        wide_ref[:, :points] = f_left * a_row + f_right * b_row
+        wide_ref[:, points:] = f_left * c_row + f_right * d_row
+        wide_ref[...] = wide_ref[...] + process_ref[...]
+        _sweep_in_place(wide_ref)
+        gain = -lax.dot_general(
+            forward, wide_ref[...], (((0,), (0,)), ((), ())), precision=HIGHEST,
+            preferred_element_type=jnp.float32,
+        )
+        gain_ref[...] = gain
+        m_top = mean_last[:, :points]
+        m_bottom = mean_last[:, points:]
+        mean_fwd = jnp.broadcast_to(
+            jnp.concatenate([a_row * m_top + b_row * m_bottom, c_row * m_top + d_row * m_bottom], axis=1),
+            (8, 2 * points),
+        )
+        mean_shift = lax.dot_general(
+            mean_fwd, gain, (((1,), (1,)), ((), ())), precision=HIGHEST,
+            preferred_element_type=jnp.float32,
+        )
+        shift_mean_ref[...] = mean_last - mean_shift[0:1, :]
+        shift_cov_ref[...] = cov_ref[...] - jnp.dot(
+            gain, forward, precision=HIGHEST, preferred_element_type=jnp.float32
+        )
+
+
+def run_filter(count, not_last, obs_all, root_all, transit, process, prior):
     total, points = obs_all.shape
     width = 2 * points
     vmem = pl.BlockSpec(memory_space=pltpu.VMEM)
+    square = jax.ShapeDtypeStruct((width, width), jnp.float32)
+    row = jax.ShapeDtypeStruct((1, width), jnp.float32)
     return pl.pallas_call(
         _filter_kernel,
-        out_shape=(
-            jax.ShapeDtypeStruct((1, width), jnp.float32),
-            jax.ShapeDtypeStruct((width, width), jnp.float32),
-        ),
+        out_shape=(row, square, square, row, square),
         in_specs=[pl.BlockSpec(memory_space=pltpu.SMEM)] + [vmem] * 7,
-        out_specs=(vmem, vmem),
+        out_specs=(vmem,) * 5,
         scratch_shapes=[
             pltpu.VMEM((width, width), jnp.float32),
             pltpu.VMEM((points, points), jnp.float32),
+            pltpu.VMEM((width, width), jnp.float32),
+            pltpu.VMEM((width, width), jnp.float32),
         ],
     )(
-        jnp.reshape(count, (1,)).astype(jnp.int32),
+        jnp.stack([count, not_last]).astype(jnp.int32),
         obs_all,
         root_all,
         root_all[:, :, None],
@@ -293,9 +335,10 @@
         return kalman_update(mean_pred, cov_pred, obs_now, root_now)
 
     if local_steps == 1:
-        mean_last, cov_last = run_filter(position + 1, obs_all, root_all, transit, process, prior)
-        means = mean_last
-        covs = cov_last[None]
+        not_last = (position != tm_count - 1).astype(jnp.int32)
+        _, _, gain_k, shift_mean_k, shift_cov_k = run_filter(
+            position + 1, not_last, obs_all, root_all, transit, process, prior
+        )
     else:
         mean_first, cov_first = kalman_update(
             jnp.zeros((width,), jnp.float32), prior, obs_all[0], root_all[0]
@@ -318,14 +361,7 @@
     global_step = position * local_steps + jnp.arange(local_steps)
     last_flag = global_step == total_steps - 1
     if local_steps == 1:
-
-        def compute_elements(operand):
-            return smoother_elements(operand[0], operand[1], last_flag, transit, process)
-
-        def final_elements(operand):
-            return (jnp.zeros_like(operand[1]), operand[0], operand[1])
-
-        smooth = lax.cond(position == tm_count - 1, final_elements, compute_elements, (means, covs))
+        smooth = (gain_k[None], shift_mean_k, shift_cov_k[None])
     else:
         smooth = smoother_elements(means, covs, last_flag, transit, process)
 

time: 186 us -> 187 us (level)
  matrix products: 8.98 us -> 6.7 us
    dot_general x18 -> x15, matrix products: 8.98 us -> 6.7 us  [matmul_hi(): return jnp.matmul(left, right, precision=HIGHEST)]
    pallas_call x2 -> x1, Pallas kernels: 28.5 us -> 29.6 us  [run_filter(): pl.pallas_call(_filter_kernel, out_shape=(row, square, square, row, squar...]
where the time goes in v10:
time: 187 us; the launch traced here: 186 us
  waiting for transfers between devices  107 us (57%)
  Pallas kernels  29.6 us (16%)
  blocking collectives  23 us (12%)
  starting transfers between devices  10.7 us (6%)
  matrix products  6.7 us (4%)
  local copies, waits for them, and re-layouts  5.5 us (3%)
  other arithmetic  3.48 us (2%)
    ppermute x7, waiting for transfers between devices, send_element(): recv_gain, recv_packed = lax.ppermute((gain, packed), 'tm', pairs)  107 us
    pallas_call x1, Pallas kernels, run_filter(): pl.pallas_call(_filter_kernel, out_shape=(row, square, square, row, squar...  29.6 us
    all_gather x1, blocking collectives, shards(): gathered = lax.all_gather(packed, 'tm', tiled=True)  23 us
    ppermute x7, starting transfers between devices, send_element(): recv_gain, recv_packed = lax.ppermute((gain, packed), 'tm', pairs)  10.7 us
    dot_general x15, matrix products, matmul_hi(): return jnp.matmul(left, right, precision=HIGHEST)  6.7 us
  transfers between devices with their start and end apart: 7, of which 7 were waited for; matrix products, arithmetic and copies ran while one was open for 2% of the time, Pallas kernels for 0%

profile of v10, /device:TPU:1, one launch (start us, length us, event | category | flops | bytes accessed | tf_op | source)
XLA Modules:
  0.0 186.3 jit_solution(16259631940442527560)
XLA Ops:
  0.6 0.6 copy-done.6
  1.3 0.6 copy-done.7
  1.9 0.0 copy-done.8
  2.0 0.7 copy-done.5
  2.6 23.0 %all_gather.3 = f32[16,2,128]{2,1,0:T(2,128)S(1)} all-gather(f32[1,2,128]{2,1,0:T(2,128)S(1)} %pad_maximum_fusion.5), channel_id=1, replica_groups=mesh['groups'=2,'tm'=16] {'tm'}, dimensions={0}, use_global_device_ids=true | all-gather | bytes 17408 | tf_op jit(solution)/shard_map/all_gather | solution.py:325
  25.6 0.6 fusion.10
  26.2 0.6 fusion.9
  26.8 0.9 copy.16.trans_col_ref
  27.7 1.4 copy.15.root_col_ref
  29.0 0.7 pad_add_fusion.count_ref
  29.7 0.1 multiply_multiply_fusion.1
  29.8 0.8 select_maximum_fusion
  30.7 29.6 %shard_map.68 = (f32[1,256]{1,0:T(1,128)}, f32[256,256]{1,0:T(8,128)}, f32[256,256]{1,0:T(8,128)}, f32[1,256]{1,0:T(1,128)}, f32[256,256]{1,0:T(8,128)}) custom-call(s32[2]{0:T(128)} %pad_add_fusion.count_ref, f32[16,128]{1,0:T(8,128)} %bitcast.77, f32[16,128]{1,0:T(8,128)} %bitcast.76, f32[16,128,1]{2,1,0:T(8,128)} %copy.15.root_col_ref, ...), custom_call_target="tpu_custom_call" | custom-call | tf_op jit(solution)/shard_map/pallas_call | solution.py:187
  60.3 0.7 copy-done.4
  60.9 1.0 pad_maximum_fusion
  62.0 1.9 %collective-permute-start.3 = (f32[264,256]{1,0:T(8,128)S(1)}, f32[264,256]{1,0:T(8,128)S(1)}, u32[]{:S(2)}, u32[]{:S(2)}) collective-permute-start(f32[264,256]{1,0:T(8,128)S(1)} %pad_maximum_fusion), channel_id=1, source_target_pairs={{1,0},{2,1},{3,2},{4,3},{5,4},{6,5},{7,6},{8,7},{9,8},{10,9},{11,1... | collective-permute-start | bytes 811016 | tf_op jit(solution)/shard_map/ppermute | solution.py:311
  63.9 2.1 %collective-permute-start = (f32[256,256]{1,0:T(8,128)S(1)}, f32[256,256]{1,0:T(8,128)S(1)}, u32[]{:S(2)}, u32[]{:S(2)}) collective-permute-start(f32[256,256]{1,0:T(8,128)S(1)} %copy-done), channel_id=1, source_target_pairs={{1,0},{2,1},{3,2},{4,3},{5,4},{6,5},{7,6},{8,7},{9,8},{10,9},{11,1... | collective-permute-start | bytes 786440 | tf_op jit(solution)/shard_map/ppermute | solution.py:311
  66.0 6.2 %collective-permute-done.3 = f32[264,256]{1,0:T(8,128)S(1)} collective-permute-done((f32[264,256]{1,0:T(8,128)S(1)}, f32[264,256]{1,0:T(8,128)S(1)}, u32[]{:S(2)}, u32[]{:S(2)}) %collective-permute-start.3) | collective-permute-done | bytes 270368 | tf_op jit(solution)/shard_map/ppermute | solution.py:311
  72.1 0.4 fusion.7
  72.5 0.0 copy-done.1
  72.5 0.4 convolution_add_fusion.3
  73.0 0.3 convolution_add_fusion.7
  73.2 0.1 pad_maximum_fusion.1
  73.3 1.3 collective-permute-start.4
  74.6 0.3 collective-permute-done
  75.0 0.4 fusion.11
  75.3 1.5 collective-permute-start.1
  76.9 17.4 %collective-permute-done.4 = f32[264,256]{1,0:T(8,128)S(1)} collective-permute-done((f32[264,256]{1,0:T(8,128)S(1)}, f32[264,256]{1,0:T(8,128)S(1)}, u32[]{:S(2)}, u32[]{:S(2)}) %collective-permute-start.4) | collective-permute-done | bytes 270368 | tf_op jit(solution)/shard_map/ppermute | solution.py:311
  94.3 0.4 fusion.5
  94.7 0.4 convolution_add_fusion.2
  95.1 0.3 convolution_add_fusion.6
  95.4 0.1 pad_maximum_fusion.2
  95.5 1.3 collective-permute-start.5
  96.8 0.3 collective-permute-done.1
  97.1 0.4 fusion.12
  97.5 1.3 collective-permute-start.2
  98.8 27.0 %collective-permute-done.5 = f32[264,256]{1,0:T(8,128)S(1)} collective-permute-done((f32[264,256]{1,0:T(8,128)S(1)}, f32[264,256]{1,0:T(8,128)S(1)}, u32[]{:S(2)}, u32[]{:S(2)}) %collective-permute-start.5) | collective-permute-done | bytes 270368 | tf_op jit(solution)/shard_map/ppermute | solution.py:311
  125.8 0.4 fusion.3
  126.2 0.4 convolution_add_fusion.1
  126.6 0.3 convolution_add_fusion.5
  126.9 0.1 pad_maximum_fusion.3
  127.0 1.3 collective-permute-start.6
  128.3 0.3 collective-permute-done.2
  128.6 0.4 fusion.13
  129.0 54.8 %collective-permute-done.6 = f32[264,256]{1,0:T(8,128)S(1)} collective-permute-done((f32[264,256]{1,0:T(8,128)S(1)}, f32[264,256]{1,0:T(8,128)S(1)}, u32[]{:S(2)}, u32[]{:S(2)}) %collective-permute-start.6) | collective-permute-done | bytes 270368 | tf_op jit(solution)/shard_map/ppermute | solution.py:311
  183.9 0.4 fusion.1
  184.2 1.1 fusion
  185.4 0.9 convolution_add_fusion.4
  (19 shorter events, 0.1 us)
Async XLA Ops:
  0.6 0.7 copy-start.6
  1.3 0.7 copy-start.7
  1.3 0.7 copy-start.8
  2.0 0.7 copy-start.5
  26.2 1.4 copy-start.3
  27.7 2.0 %copy-start.2 = (f32[128,128]{1,0:T(8,128)S(1)}, f32[128,128]{1,0:T(8,128)}, u32[]{:S(2)}) copy-start(f32[128,128]{1,0:T(8,128)} %param.9) | copy-start | bytes 196612
  60.3 0.7 copy-start.4
  60.9 2.9 %copy-start = (f32[256,256]{1,0:T(8,128)S(1)}, f32[256,256]{1,0:T(8,128)}, u32[]{:S(2)}) copy-start(f32[256,256]{1,0:T(8,128)} %get-tuple-element.5) | copy-start | bytes 786436
  62.0 10.2 %collective-permute-start.3 = (f32[264,256]{1,0:T(8,128)S(1)}, f32[264,256]{1,0:T(8,128)S(1)}, u32[]{:S(2)}, u32[]{:S(2)}) collective-permute-start(f32[264,256]{1,0:T(8,128)S(1)} %pad_maximum_fusion), channel_id=1, source_target_pairs={{1,0},{2,1},{3,2},{4,3},{5,4},{6,5},{7,6},{8,7},{9,8},{10,9},{11,1... | collective-permute-start | bytes 811016 | tf_op jit(solution)/shard_map/ppermute | solution.py:311
  63.9 8.6 %copy-start.1 = (f32[256,256]{1,0:T(8,128)S(1)}, f32[256,256]{1,0:T(8,128)}, u32[]{:S(2)}) copy-start(f32[256,256]{1,0:T(8,128)} %get-tuple-element.6) | copy-start | bytes 786436
  63.9 11.0 %collective-permute-start = (f32[256,256]{1,0:T(8,128)S(1)}, f32[256,256]{1,0:T(8,128)S(1)}, u32[]{:S(2)}, u32[]{:S(2)}) collective-permute-start(f32[256,256]{1,0:T(8,128)S(1)} %copy-done), channel_id=1, source_target_pairs={{1,0},{2,1},{3,2},{4,3},{5,4},{6,5},{7,6},{8,7},{9,8},{10,9},{11,1... | collective-permute-start | bytes 786440 | tf_op jit(solution)/shard_map/ppermute | solution.py:311
  73.3 21.0 %collective-permute-start.4 = (f32[264,256]{1,0:T(8,128)S(1)}, f32[264,256]{1,0:T(8,128)S(1)}, u32[]{:S(2)}, u32[]{:S(2)}) collective-permute-start(f32[264,256]{1,0:T(8,128)S(1)} %pad_maximum_fusion.1), channel_id=1, source_target_pairs={{2,0},{3,1},{4,2},{5,3},{6,4},{7,5},{8,6},{9,7},{10,8},{11,9},{12,... | collective-permute-start | bytes 811016 | tf_op jit(solution)/shard_map/ppermute | solution.py:311
  75.3 21.8 %collective-permute-start.1 = (f32[256,256]{1,0:T(8,128)S(1)}, f32[256,256]{1,0:T(8,128)S(1)}, u32[]{:S(2)}, u32[]{:S(2)}) collective-permute-start(f32[256,256]{1,0:T(8,128)S(1)} %fusion.11), channel_id=1, source_target_pairs={{2,0},{3,1},{4,2},{5,3},{6,4},{7,5},{8,6},{9,7},{10,8},{11,9},{12,... | collective-permute-start | bytes 786440 | tf_op jit(solution)/shard_map/ppermute | solution.py:311
  95.5 30.4 %collective-permute-start.5 = (f32[264,256]{1,0:T(8,128)S(1)}, f32[264,256]{1,0:T(8,128)S(1)}, u32[]{:S(2)}, u32[]{:S(2)}) collective-permute-start(f32[264,256]{1,0:T(8,128)S(1)} %pad_maximum_fusion.2), channel_id=1, source_target_pairs={{4,0},{5,1},{6,2},{7,3},{8,4},{9,5},{10,6},{11,7},{12,8},{13,9},{1... | collective-permute-start | bytes 811016 | tf_op jit(solution)/shard_map/ppermute | solution.py:311
  97.5 31.2 %collective-permute-start.2 = (f32[256,256]{1,0:T(8,128)S(1)}, f32[256,256]{1,0:T(8,128)S(1)}, u32[]{:S(2)}, u32[]{:S(2)}) collective-permute-start(f32[256,256]{1,0:T(8,128)S(1)} %fusion.12), channel_id=1, source_target_pairs={{4,0},{5,1},{6,2},{7,3},{8,4},{9,5},{10,6},{11,7},{12,8},{13,9},{1... | collective-permute-start | bytes 786440 | tf_op jit(solution)/shard_map/ppermute | solution.py:311
  127.0 56.9 %collective-permute-start.6 = (f32[264,256]{1,0:T(8,128)S(1)}, f32[264,256]{1,0:T(8,128)S(1)}, u32[]{:S(2)}, u32[]{:S(2)}) collective-permute-start(f32[264,256]{1,0:T(8,128)S(1)} %pad_maximum_fusion.3), channel_id=1, source_target_pairs={{8,0},{9,1},{10,2},{11,3},{12,4},{13,5},{14,6},{15,7},{24,16},{25,... | collective-permute-start | bytes 811016 | tf_op jit(solution)/shard_map/ppermute | solution.py:311

commit v11 on v7

--- a/solution.py
+++ b/solution.py
@@ -280,7 +280,10 @@
 
     root_local = jnp.sqrt(obs_masks.astype(jnp.float32) / noise_var)
     packed = jnp.stack([observed, root_local], axis=1)
-    gathered = lax.all_gather(packed, "tm", tiled=True)
+    placed = lax.dynamic_update_slice_in_dim(
+        jnp.zeros((total_steps,) + packed.shape[1:], jnp.float32), packed, position * local_steps, 0
+    )
+    gathered = lax.psum(placed, "tm")
     obs_all = gathered[:, 0]
     root_all = gathered[:, 1]
 

time: 186 us -> 224 us (1.20)
  blocking collectives: 23 us -> 58 us
    psum x0 -> x1, blocking collectives: none -> 58 us  [shards(): gathered = lax.psum(placed, 'tm')]
    all_gather x1 -> x0, blocking collectives: 23 us -> none  [shards(): gathered = lax.all_gather(packed, 'tm', tiled=True)]
    ppermute x7, waiting for transfers between devices: 107 us -> 109 us  [send_element(): recv_gain, recv_packed = lax.ppermute((gain, packed), 'tm', pairs)]
where the time goes in v11:
time: 224 us
  waiting for transfers between devices  109 us (49%)
  blocking collectives  58 us (26%)
  Pallas kernels  28.4 us (13%)
  starting transfers between devices  10.5 us (5%)
  matrix products  8.99 us (4%)
  local copies, waits for them, and re-layouts  5.13 us (2%)
  other arithmetic  2.76 us (1%)
    ppermute x7, waiting for transfers between devices, send_element(): recv_gain, recv_packed = lax.ppermute((gain, packed), 'tm', pairs)  109 us
    psum x1, blocking collectives, shards(): gathered = lax.psum(placed, 'tm')  58 us
    pallas_call x1, Pallas kernels, run_filter(): pl.pallas_call(_filter_kernel, out_shape=(jax.ShapeDtypeStruct((1, width)...  14.5 us
    pallas_call x1, Pallas kernels, neg_inverse(): pl.pallas_call(_sweep_kernel, out_shape=jax.ShapeDtypeStruct((size, size)...  14 us
    ppermute x7, starting transfers between devices, send_element(): recv_gain, recv_packed = lax.ppermute((gain, packed), 'tm', pairs)  10.5 us
    dot_general x18, matrix products, matmul_hi(): return jnp.matmul(left, right, precision=HIGHEST)  8.99 us
  transfers between devices with their start and end apart: 7, of which 7 were waited for; matrix products, arithmetic and copies ran while one was open for 2% of the time, Pallas kernels for 0%

profile of v11, /device:TPU:1, one launch (start us, length us, event | category | flops | bytes accessed | tf_op | source)
XLA Modules:
  0.0 224.1 jit_solution(17873245199336766099)
XLA Ops:
  0.6 0.6 copy-done.1
  1.3 0.6 fusion.24
  1.9 0.9 copy.16.trans_col_ref
  2.8 0.7 copy-done.3
  3.5 0.7 copy-done.2
  4.1 58.0 %psum.7 = f32[16,2,128]{2,0,1:T(8,128)S(1)} all-reduce(f32[16,2,128]{2,0,1:T(8,128)S(1)} %dynamic_update_slice.3), channel_id=1, replica_groups=mesh['groups'=2,'tm'=16] {'tm'}, use_global_device_ids=true, to_apply=%region_0.1 | all-reduce | flops 4096 | bytes 32768 | tf_op jit(solution)/shard_map/psum | solution.py:286
  62.1 0.6 slice_bitcast_fusion.1
  62.7 1.4 copy.15.root_col_ref
  64.1 0.1 multiply_multiply_fusion.1
  64.2 0.7 select_maximum_fusion
  65.0 14.5 %shard_map.68 = (f32[1,256]{1,0:T(1,128)S(1)}, f32[256,256]{1,0:T(8,128)S(1)}) custom-call(s32[1]{0:T(128)} %bitcast.16.count_ref, f32[16,128]{1,0:T(8,128)} %get-tuple-element.80.obs_ref, f32[16,128]{1,0:T(8,128)} %get-tuple-element.79.root_row_ref, f32[16,128,1]{2,1,0:T(8,128)} %copy.15.root_col_ref, f32[4,128]{1,0:T(4,128)} %get-tuple-element.82.trans_row_ref, ...), custom_call_target="tpu_custom_call" | custom-call | tf_op jit(solution)/shard_map/pallas_call | solution.py:144
  79.5 17.7 %conditional.1 = (f32[1,256]{1,0:T(1,128)S(1)}, f32[256,256]{1,0:T(8,128)S(1)}, f32[256,256]{1,0:T(8,128)S(1)}) conditional(s32[]{:T(128)} %convert_element_type.12, (f32[128]{0:T(128)S(1)}, f32[1,256,256]{2,1,0:T(8,128)S(1)}, f32[128]{0:T(128)S(1)}, f32[128]{0:T(128)S(1)}, f32[128]{0:T(128)S(1)}, /*index=5*/f32[256,256]{1,0:T(8,128)S(1)}, s32[]{:T(128)}, ...), branch_computations={%region_1.2_spmd, %region_2.3_spmd} | conditional | flops 404358400 | bytes 5516342 | solution.py:331
  79.7 0.1 multiply_add_fusion.1
  80.1 0.1 add_bitcast_fusion.1
  80.2 0.7 maximum_add_fusion.a_ref
  81.0 14.0 %vmap__.2 = f32[256,256]{1,0:T(8,128)} custom-call(f32[256,256]{1,0:T(8,128)} %maximum_add_fusion.a_ref), custom_call_target="tpu_custom_call" | custom-call | tf_op jit(solution)/shard_map/cond/branch_0_fun/vmap()/pallas_call | solution.py:83
  94.9 1.5 fusion
  96.5 0.5 fusion.2
  96.9 0.3 convolution_subtract_fusion
  97.3 1.9 collective-permute-start.3
  99.2 1.9 collective-permute-start
  101.2 10.4 %collective-permute-done.3 = f32[264,256]{1,0:T(8,128)S(1)} collective-permute-done((f32[264,256]{1,0:T(8,128)S(1)}, f32[264,256]{1,0:T(8,128)S(1)}, u32[]{:S(2)}, u32[]{:S(2)}) %collective-permute-start.3) | collective-permute-done | bytes 270368 | tf_op jit(solution)/shard_map/ppermute | solution.py:269
  111.6 0.4 fusion.20
  112.0 0.4 convolution_add_fusion.3
  112.4 0.3 convolution_add_fusion.7
  112.8 1.5 collective-permute-start.4
  114.3 0.1 collective-permute-done
  114.4 0.4 fusion.26
  114.8 1.3 collective-permute-start.1
  116.1 13.2 %collective-permute-done.4 = f32[264,256]{1,0:T(8,128)S(1)} collective-permute-done((f32[264,256]{1,0:T(8,128)S(1)}, f32[264,256]{1,0:T(8,128)S(1)}, u32[]{:S(2)}, u32[]{:S(2)}) %collective-permute-start.4) | collective-permute-done | bytes 270368 | tf_op jit(solution)/shard_map/ppermute | solution.py:269
  129.3 0.4 fusion.18
  129.7 0.4 convolution_add_fusion.2
  130.1 0.3 convolution_add_fusion.6
  130.4 1.3 collective-permute-start.5
  131.7 0.3 collective-permute-done.1
  132.1 0.4 fusion.27
  132.5 1.3 collective-permute-start.2
  133.8 21.8 %collective-permute-done.5 = f32[264,256]{1,0:T(8,128)S(1)} collective-permute-done((f32[264,256]{1,0:T(8,128)S(1)}, f32[264,256]{1,0:T(8,128)S(1)}, u32[]{:S(2)}, u32[]{:S(2)}) %collective-permute-start.5) | collective-permute-done | bytes 270368 | tf_op jit(solution)/shard_map/ppermute | solution.py:269
  155.6 0.4 fusion.16
  156.0 0.4 convolution_add_fusion.1
  156.4 0.3 convolution_add_fusion.5
  156.7 1.3 collective-permute-start.6
  158.0 0.3 collective-permute-done.2
  158.4 0.4 fusion.28
  158.8 62.9 %collective-permute-done.6 = f32[264,256]{1,0:T(8,128)S(1)} collective-permute-done((f32[264,256]{1,0:T(8,128)S(1)}, f32[264,256]{1,0:T(8,128)S(1)}, u32[]{:S(2)}, u32[]{:S(2)}) %collective-permute-start.6) | collective-permute-done | bytes 270368 | tf_op jit(solution)/shard_map/ppermute | solution.py:269
  221.7 0.4 fusion.14
  222.1 1.1 fusion.13
  223.2 0.9 convolution_add_fusion.4
  (25 shorter events, 0.6 us)
Async XLA Ops:
  0.6 0.7 copy-start.1
  2.8 0.7 copy-start.3
  2.8 0.7 copy-start.4
  3.4 0.7 copy-start.2
  62.7 1.4 copy-start
  97.3 14.3 %collective-permute-start.3 = (f32[264,256]{1,0:T(8,128)S(1)}, f32[264,256]{1,0:T(8,128)S(1)}, u32[]{:S(2)}, u32[]{:S(2)}) collective-permute-start(f32[264,256]{1,0:T(8,128)S(1)} %pad_maximum_fusion.3), channel_id=1, source_target_pairs={{1,0},{2,1},{3,2},{4,3},{5,4},{6,5},{7,6},{8,7},{9,8},{10,9},{11,1... | collective-permute-start | bytes 811016 | tf_op jit(solution)/shard_map/ppermute | solution.py:269
  99.2 15.2 %collective-permute-start = (f32[256,256]{1,0:T(8,128)S(1)}, f32[256,256]{1,0:T(8,128)S(1)}, u32[]{:S(2)}, u32[]{:S(2)}) collective-permute-start(f32[256,256]{1,0:T(8,128)S(1)} %get-tuple-element.60), channel_id=1, source_target_pairs={{1,0},{2,1},{3,2},{4,3},{5,4},{6,5},{7,6},{8,7},{9,8},{10,9},{11,1... | collective-permute-start | bytes 786440 | tf_op jit(solution)/shard_map/ppermute | solution.py:269
  112.8 16.5 %collective-permute-start.4 = (f32[264,256]{1,0:T(8,128)S(1)}, f32[264,256]{1,0:T(8,128)S(1)}, u32[]{:S(2)}, u32[]{:S(2)}) collective-permute-start(f32[264,256]{1,0:T(8,128)S(1)} %pad_maximum_fusion.4), channel_id=1, source_target_pairs={{2,0},{3,1},{4,2},{5,3},{6,4},{7,5},{8,6},{9,7},{10,8},{11,9},{12,... | collective-permute-start | bytes 811016 | tf_op jit(solution)/shard_map/ppermute | solution.py:269
  114.8 17.3 %collective-permute-start.1 = (f32[256,256]{1,0:T(8,128)S(1)}, f32[256,256]{1,0:T(8,128)S(1)}, u32[]{:S(2)}, u32[]{:S(2)}) collective-permute-start(f32[256,256]{1,0:T(8,128)S(1)} %fusion.26), channel_id=1, source_target_pairs={{2,0},{3,1},{4,2},{5,3},{6,4},{7,5},{8,6},{9,7},{10,8},{11,9},{12,... | collective-permute-start | bytes 786440 | tf_op jit(solution)/shard_map/ppermute | solution.py:269
  130.4 25.1 %collective-permute-start.5 = (f32[264,256]{1,0:T(8,128)S(1)}, f32[264,256]{1,0:T(8,128)S(1)}, u32[]{:S(2)}, u32[]{:S(2)}) collective-permute-start(f32[264,256]{1,0:T(8,128)S(1)} %pad_maximum_fusion.5), channel_id=1, source_target_pairs={{4,0},{5,1},{6,2},{7,3},{8,4},{9,5},{10,6},{11,7},{12,8},{13,9},{1... | collective-permute-start | bytes 811016 | tf_op jit(solution)/shard_map/ppermute | solution.py:269
  132.5 25.9 %collective-permute-start.2 = (f32[256,256]{1,0:T(8,128)S(1)}, f32[256,256]{1,0:T(8,128)S(1)}, u32[]{:S(2)}, u32[]{:S(2)}) collective-permute-start(f32[256,256]{1,0:T(8,128)S(1)} %fusion.27), channel_id=1, source_target_pairs={{4,0},{5,1},{6,2},{7,3},{8,4},{9,5},{10,6},{11,7},{12,8},{13,9},{1... | collective-permute-start | bytes 786440 | tf_op jit(solution)/shard_map/ppermute | solution.py:269
  156.7 65.0 %collective-permute-start.6 = (f32[264,256]{1,0:T(8,128)S(1)}, f32[264,256]{1,0:T(8,128)S(1)}, u32[]{:S(2)}, u32[]{:S(2)}) collective-permute-start(f32[264,256]{1,0:T(8,128)S(1)} %pad_maximum_fusion.6), channel_id=1, source_target_pairs={{8,0},{9,1},{10,2},{11,3},{12,4},{13,5},{14,6},{15,7},{24,16},{25,... | collective-permute-start | bytes 811016 | tf_op jit(solution)/shard_map/ppermute | solution.py:269

commit v12 on v11

--- a/solution.py
+++ b/solution.py
@@ -280,10 +280,14 @@
 
     root_local = jnp.sqrt(obs_masks.astype(jnp.float32) / noise_var)
     packed = jnp.stack([observed, root_local], axis=1)
-    placed = lax.dynamic_update_slice_in_dim(
+    gathered = lax.dynamic_update_slice_in_dim(
         jnp.zeros((total_steps,) + packed.shape[1:], jnp.float32), packed, position * local_steps, 0
     )
-    gathered = lax.psum(placed, "tm")
+    shift = 1
+    while shift < tm_count:
+        pairs = [(source, source + shift) for source in range(tm_count - shift)]
+        gathered = gathered + lax.ppermute(gathered, "tm", pairs)
+        shift *= 2
     obs_all = gathered[:, 0]
     root_all = gathered[:, 1]
 

time: 224 us -> 191 us (0.85)
  blocking collectives: 58 us -> 0 us
  starting transfers between devices: 10.5 us -> 27.2 us
  waiting for transfers between devices: 109 us -> 116 us
    psum x1 -> x0, blocking collectives: 58 us -> none  [shards(): gathered = lax.psum(placed, 'tm')]
    ppermute x0 -> x4, starting transfers between devices: none -> 16.7 us  [shards(): gathered = gathered + lax.ppermute(gathered, 'tm', pairs)]
    ppermute x7, waiting for transfers between devices: 109 us -> 115 us  [send_element(): recv_gain, recv_packed = lax.ppermute((gain, packed), 'tm', pairs)]
  transfers between devices with their start and end apart: 7 -> 11, of which waited for: 7 -> 9; matrix products, arithmetic and copies ran while one was open for 2% -> 4% of each run, Pallas kernels for 0% -> 0%
where the time goes in v12:
time: 191 us; the launch traced here: 190 us
  waiting for transfers between devices  116 us (61%)
  Pallas kernels  28.5 us (15%)
  starting transfers between devices  27.2 us (14%)
  matrix products  8.99 us (5%)
  local copies, waits for them, and re-layouts  4.52 us (2%)
  other arithmetic  3.7 us (2%)
    ppermute x7, waiting for transfers between devices, send_element(): recv_gain, recv_packed = lax.ppermute((gain, packed), 'tm', pairs)  115 us
    ppermute x4, starting transfers between devices, shards(): gathered = gathered + lax.ppermute(gathered, 'tm', pairs)  16.7 us
    pallas_call x1, Pallas kernels, run_filter(): pl.pallas_call(_filter_kernel, out_shape=(jax.ShapeDtypeStruct((1, width)...  14.5 us
    pallas_call x1, Pallas kernels, neg_inverse(): pl.pallas_call(_sweep_kernel, out_shape=jax.ShapeDtypeStruct((size, size)...  14 us
    ppermute x7, starting transfers between devices, send_element(): recv_gain, recv_packed = lax.ppermute((gain, packed), 'tm', pairs)  10.5 us
    dot_general x18, matrix products, matmul_hi(): return jnp.matmul(left, right, precision=HIGHEST)  8.99 us
  transfers between devices with their start and end apart: 11, of which 9 were waited for; matrix products, arithmetic and copies ran while one was open for 4% of the time, Pallas kernels for 0%

profile of v12, /device:TPU:1, one launch (start us, length us, event | category | flops | bytes accessed | tf_op | source)
XLA Modules:
  0.0 190.2 jit_solution(1795847224993723385)
XLA Ops:
  0.7 0.6 copy-done.3
  1.3 0.7 copy-done.1
  2.0 4.5 %collective-permute-start = (f32[16,2,128]{2,0,1:T(8,128)S(1)}, f32[16,2,128]{2,0,1:T(8,128)S(1)}, u32[]{:S(2)}, u32[]{:S(2)}) collective-permute-start(f32[16,2,128]{2,0,1:T(8,128)S(1)} %dynamic_update_slice.5), channel_id=1, source_target_pairs={{0,1},{1,2},{2,3},{3,4},{4,5},{5,6},{6,7},{7,8},{8,9},{9,10},{10,1... | collective-permute-start | bytes 49160 | tf_op jit(solution)/shard_map/ppermute | solution.py:289
  6.6 0.8 collective-permute-done
  7.5 3.1 %collective-permute-start.1 = (f32[16,2,128]{2,0,1:T(8,128)S(1)}, f32[16,2,128]{2,0,1:T(8,128)S(1)}, u32[]{:S(2)}, u32[]{:S(2)}) collective-permute-start(f32[16,2,128]{2,0,1:T(8,128)S(1)} %add.110), channel_id=1, source_target_pairs={{0,2},{1,3},{2,4},{3,5},{4,6},{5,7},{6,8},{7,9},{8,10},{9,11},{10,... | collective-permute-start | bytes 49160 | tf_op jit(solution)/shard_map/ppermute | solution.py:289
  10.6 1.0 multiply_multiply_fusion.1
  11.7 4.4 %collective-permute-start.2 = (f32[16,2,128]{2,0,1:T(8,128)S(1)}, f32[16,2,128]{2,0,1:T(8,128)S(1)}, u32[]{:S(2)}, u32[]{:S(2)}) collective-permute-start(f32[16,2,128]{2,0,1:T(8,128)S(1)} %add.111), channel_id=1, source_target_pairs={{0,4},{1,5},{2,6},{3,7},{4,8},{5,9},{6,10},{7,11},{8,12},{9,13},{1... | collective-permute-start | bytes 49160 | tf_op jit(solution)/shard_map/ppermute | solution.py:289
  16.0 0.7 select_maximum_fusion
  16.9 4.6 %collective-permute-start.3 = (f32[16,2,128]{2,0,1:T(8,128)S(1)}, f32[16,2,128]{2,0,1:T(8,128)S(1)}, u32[]{:S(2)}, u32[]{:S(2)}) collective-permute-start(f32[16,2,128]{2,0,1:T(8,128)S(1)} %add.112), channel_id=1, source_target_pairs={{0,8},{1,9},{2,10},{3,11},{4,12},{5,13},{6,14},{7,15},{16,24},{17,... | collective-permute-start | bytes 49160 | tf_op jit(solution)/shard_map/ppermute | solution.py:289
  21.5 0.6 fusion.24
  22.1 0.9 copy.16.trans_col_ref
  23.0 0.6 slice_bitcast_fusion.1
  23.6 1.4 copy.15.root_col_ref
  25.0 14.5 %shard_map.68 = (f32[1,256]{1,0:T(1,128)S(1)}, f32[256,256]{1,0:T(8,128)S(1)}) custom-call(s32[1]{0:T(128)} %bitcast.16.count_ref, f32[16,128]{1,0:T(8,128)} %get-tuple-element.80.obs_ref, f32[16,128]{1,0:T(8,128)} %get-tuple-element.79.root_row_ref, f32[16,128,1]{2,1,0:T(8,128)} %copy.15.root_col_ref, f32[4,128]{1,0:T(4,128)} %get-tuple-element.82.trans_row_ref, ...), custom_call_target="tpu_custom_call" | custom-call | tf_op jit(solution)/shard_map/pallas_call | solution.py:144
  39.5 17.8 %conditional.1 = (f32[1,256]{1,0:T(1,128)S(1)}, f32[256,256]{1,0:T(8,128)S(1)}, f32[256,256]{1,0:T(8,128)S(1)}) conditional(s32[]{:T(128)} %convert_element_type.12, (f32[128]{0:T(128)S(1)}, f32[1,256,256]{2,1,0:T(8,128)S(1)}, f32[128]{0:T(128)S(1)}, f32[128]{0:T(128)S(1)}, f32[128]{0:T(128)S(1)}, /*index=5*/f32[256,256]{1,0:T(8,128)S(1)}, s32[]{:T(128)}, ...), branch_computations={%region_0.1_spmd, %region_1.2_spmd} | conditional | flops 404358400 | bytes 5516342 | solution.py:335
  40.2 0.7 maximum_add_fusion.a_ref
  41.0 14.0 %vmap__.2 = f32[256,256]{1,0:T(8,128)} custom-call(f32[256,256]{1,0:T(8,128)} %maximum_add_fusion.a_ref), custom_call_target="tpu_custom_call" | custom-call | tf_op jit(solution)/shard_map/cond/branch_0_fun/vmap()/pallas_call | solution.py:83
  54.9 1.5 fusion
  56.5 0.5 fusion.2
  57.0 0.3 convolution_subtract_fusion
  57.3 1.9 %collective-permute-start.7 = (f32[264,256]{1,0:T(8,128)S(1)}, f32[264,256]{1,0:T(8,128)S(1)}, u32[]{:S(2)}, u32[]{:S(2)}) collective-permute-start(f32[264,256]{1,0:T(8,128)S(1)} %pad_maximum_fusion.3), channel_id=1, source_target_pairs={{1,0},{2,1},{3,2},{4,3},{5,4},{6,5},{7,6},{8,7},{9,8},{10,9},{11,1... | collective-permute-start | bytes 811016 | tf_op jit(solution)/shard_map/ppermute | solution.py:269
  59.3 1.9 %collective-permute-start.4 = (f32[256,256]{1,0:T(8,128)S(1)}, f32[256,256]{1,0:T(8,128)S(1)}, u32[]{:S(2)}, u32[]{:S(2)}) collective-permute-start(f32[256,256]{1,0:T(8,128)S(1)} %get-tuple-element.60), channel_id=1, source_target_pairs={{1,0},{2,1},{3,2},{4,3},{5,4},{6,5},{7,6},{8,7},{9,8},{10,9},{11,1... | collective-permute-start | bytes 786440 | tf_op jit(solution)/shard_map/ppermute | solution.py:269
  61.2 12.8 %collective-permute-done.7 = f32[264,256]{1,0:T(8,128)S(1)} collective-permute-done((f32[264,256]{1,0:T(8,128)S(1)}, f32[264,256]{1,0:T(8,128)S(1)}, u32[]{:S(2)}, u32[]{:S(2)}) %collective-permute-start.7) | collective-permute-done | bytes 270368 | tf_op jit(solution)/shard_map/ppermute | solution.py:269
  74.0 0.4 fusion.20
  74.4 0.4 convolution_add_fusion.3
  74.9 0.3 convolution_add_fusion.7
  75.2 1.5 collective-permute-start.8
  76.9 0.4 fusion.26
  77.2 1.3 collective-permute-start.5
  78.5 18.4 %collective-permute-done.8 = f32[264,256]{1,0:T(8,128)S(1)} collective-permute-done((f32[264,256]{1,0:T(8,128)S(1)}, f32[264,256]{1,0:T(8,128)S(1)}, u32[]{:S(2)}, u32[]{:S(2)}) %collective-permute-start.8) | collective-permute-done | bytes 270368 | tf_op jit(solution)/shard_map/ppermute | solution.py:269
  97.0 0.4 fusion.18
  97.3 0.4 convolution_add_fusion.2
  97.8 0.3 convolution_add_fusion.6
  98.1 1.3 collective-permute-start.9
  99.4 0.3 collective-permute-done.5
  99.8 0.4 fusion.27
  100.1 1.3 collective-permute-start.6
  101.4 30.4 %collective-permute-done.9 = f32[264,256]{1,0:T(8,128)S(1)} collective-permute-done((f32[264,256]{1,0:T(8,128)S(1)}, f32[264,256]{1,0:T(8,128)S(1)}, u32[]{:S(2)}, u32[]{:S(2)}) %collective-permute-start.9) | collective-permute-done | bytes 270368 | tf_op jit(solution)/shard_map/ppermute | solution.py:269
  131.9 0.4 fusion.16
  132.3 0.4 convolution_add_fusion.1
  132.7 0.3 convolution_add_fusion.5
  133.0 1.3 collective-permute-start.10
  134.3 0.3 collective-permute-done.6
  134.7 0.4 fusion.28
  135.1 52.7 %collective-permute-done.10 = f32[264,256]{1,0:T(8,128)S(1)} collective-permute-done((f32[264,256]{1,0:T(8,128)S(1)}, f32[264,256]{1,0:T(8,128)S(1)}, u32[]{:S(2)}, u32[]{:S(2)}) %collective-permute-start.10) | collective-permute-done | bytes 270368 | tf_op jit(solution)/shard_map/ppermute | solution.py:269
  187.8 0.4 fusion.14
  188.2 1.1 fusion.13
  189.3 0.9 convolution_add_fusion.4
  (37 shorter events, 1.2 us)
Async XLA Ops:
  0.6 0.7 copy-start.3
  0.6 0.7 copy-start.4
  1.3 0.7 copy-start.1
  2.0 4.6 %copy-start.2 = (f32[128]{0:T(128)S(1)}, f32[128]{0:T(128)}, u32[]{:S(2)}) copy-start(f32[128]{0:T(128)} %param.9) | copy-start | bytes 1540
  2.0 5.4 %collective-permute-start = (f32[16,2,128]{2,0,1:T(8,128)S(1)}, f32[16,2,128]{2,0,1:T(8,128)S(1)}, u32[]{:S(2)}, u32[]{:S(2)}) collective-permute-start(f32[16,2,128]{2,0,1:T(8,128)S(1)} %dynamic_update_slice.5), channel_id=1, source_target_pairs={{0,1},{1,2},{2,3},{3,4},{4,5},{5,6},{6,7},{7,8},{8,9},{9,10},{10,1... | collective-permute-start | bytes 49160 | tf_op jit(solution)/shard_map/ppermute | solution.py:289
  7.5 4.2 %collective-permute-start.1 = (f32[16,2,128]{2,0,1:T(8,128)S(1)}, f32[16,2,128]{2,0,1:T(8,128)S(1)}, u32[]{:S(2)}, u32[]{:S(2)}) collective-permute-start(f32[16,2,128]{2,0,1:T(8,128)S(1)} %add.110), channel_id=1, source_target_pairs={{0,2},{1,3},{2,4},{3,5},{4,6},{5,7},{6,8},{7,9},{8,10},{9,11},{10,... | collective-permute-start | bytes 49160 | tf_op jit(solution)/shard_map/ppermute | solution.py:289
  10.6 5.4 %copy-start = (f32[128,128]{1,0:T(8,128)S(1)}, f32[128,128]{1,0:T(8,128)}, u32[]{:S(2)}) copy-start(f32[128,128]{1,0:T(8,128)} %param.11) | copy-start | bytes 196612
  11.7 5.2 %collective-permute-start.2 = (f32[16,2,128]{2,0,1:T(8,128)S(1)}, f32[16,2,128]{2,0,1:T(8,128)S(1)}, u32[]{:S(2)}, u32[]{:S(2)}) collective-permute-start(f32[16,2,128]{2,0,1:T(8,128)S(1)} %add.111), channel_id=1, source_target_pairs={{0,4},{1,5},{2,6},{3,7},{4,8},{5,9},{6,10},{7,11},{8,12},{9,13},{1... | collective-permute-start | bytes 49160 | tf_op jit(solution)/shard_map/ppermute | solution.py:289
  16.9 6.1 %collective-permute-start.3 = (f32[16,2,128]{2,0,1:T(8,128)S(1)}, f32[16,2,128]{2,0,1:T(8,128)S(1)}, u32[]{:S(2)}, u32[]{:S(2)}) collective-permute-start(f32[16,2,128]{2,0,1:T(8,128)S(1)} %add.112), channel_id=1, source_target_pairs={{0,8},{1,9},{2,10},{3,11},{4,12},{5,13},{6,14},{7,15},{16,24},{17,... | collective-permute-start | bytes 49160 | tf_op jit(solution)/shard_map/ppermute | solution.py:289
  57.3 16.7 %collective-permute-start.7 = (f32[264,256]{1,0:T(8,128)S(1)}, f32[264,256]{1,0:T(8,128)S(1)}, u32[]{:S(2)}, u32[]{:S(2)}) collective-permute-start(f32[264,256]{1,0:T(8,128)S(1)} %pad_maximum_fusion.3), channel_id=1, source_target_pairs={{1,0},{2,1},{3,2},{4,3},{5,4},{6,5},{7,6},{8,7},{9,8},{10,9},{11,1... | collective-permute-start | bytes 811016 | tf_op jit(solution)/shard_map/ppermute | solution.py:269
  59.3 17.6 %collective-permute-start.4 = (f32[256,256]{1,0:T(8,128)S(1)}, f32[256,256]{1,0:T(8,128)S(1)}, u32[]{:S(2)}, u32[]{:S(2)}) collective-permute-start(f32[256,256]{1,0:T(8,128)S(1)} %get-tuple-element.60), channel_id=1, source_target_pairs={{1,0},{2,1},{3,2},{4,3},{5,4},{6,5},{7,6},{8,7},{9,8},{10,9},{11,1... | collective-permute-start | bytes 786440 | tf_op jit(solution)/shard_map/ppermute | solution.py:269
  75.2 21.7 %collective-permute-start.8 = (f32[264,256]{1,0:T(8,128)S(1)}, f32[264,256]{1,0:T(8,128)S(1)}, u32[]{:S(2)}, u32[]{:S(2)}) collective-permute-start(f32[264,256]{1,0:T(8,128)S(1)} %pad_maximum_fusion.4), channel_id=1, source_target_pairs={{2,0},{3,1},{4,2},{5,3},{6,4},{7,5},{8,6},{9,7},{10,8},{11,9},{12,... | collective-permute-start | bytes 811016 | tf_op jit(solution)/shard_map/ppermute | solution.py:269
  77.2 22.5 %collective-permute-start.5 = (f32[256,256]{1,0:T(8,128)S(1)}, f32[256,256]{1,0:T(8,128)S(1)}, u32[]{:S(2)}, u32[]{:S(2)}) collective-permute-start(f32[256,256]{1,0:T(8,128)S(1)} %fusion.26), channel_id=1, source_target_pairs={{2,0},{3,1},{4,2},{5,3},{6,4},{7,5},{8,6},{9,7},{10,8},{11,9},{12,... | collective-permute-start | bytes 786440 | tf_op jit(solution)/shard_map/ppermute | solution.py:269
  98.1 33.8 %collective-permute-start.9 = (f32[264,256]{1,0:T(8,128)S(1)}, f32[264,256]{1,0:T(8,128)S(1)}, u32[]{:S(2)}, u32[]{:S(2)}) collective-permute-start(f32[264,256]{1,0:T(8,128)S(1)} %pad_maximum_fusion.5), channel_id=1, source_target_pairs={{4,0},{5,1},{6,2},{7,3},{8,4},{9,5},{10,6},{11,7},{12,8},{13,9},{1... | collective-permute-start | bytes 811016 | tf_op jit(solution)/shard_map/ppermute | solution.py:269
  100.1 34.5 %collective-permute-start.6 = (f32[256,256]{1,0:T(8,128)S(1)}, f32[256,256]{1,0:T(8,128)S(1)}, u32[]{:S(2)}, u32[]{:S(2)}) collective-permute-start(f32[256,256]{1,0:T(8,128)S(1)} %fusion.27), channel_id=1, source_target_pairs={{4,0},{5,1},{6,2},{7,3},{8,4},{9,5},{10,6},{11,7},{12,8},{13,9},{1... | collective-permute-start | bytes 786440 | tf_op jit(solution)/shard_map/ppermute | solution.py:269
  133.0 54.8 %collective-permute-start.10 = (f32[264,256]{1,0:T(8,128)S(1)}, f32[264,256]{1,0:T(8,128)S(1)}, u32[]{:S(2)}, u32[]{:S(2)}) collective-permute-start(f32[264,256]{1,0:T(8,128)S(1)} %pad_maximum_fusion.6), channel_id=1, source_target_pairs={{8,0},{9,1},{10,2},{11,3},{12,4},{13,5},{14,6},{15,7},{24,16},{25,... | collective-permute-start | bytes 811016 | tf_op jit(solution)/shard_map/ppermute | solution.py:269

commit v13 on v7

--- a/solution.py
+++ b/solution.py
@@ -105,6 +105,13 @@
         first = t == 0
         top = cov_ref[:points, :]
         bottom = cov_ref[points:, :]
+        r_col = root_col_ref[t]
+        r_row = root_row_ref[pl.ds(t, 1), :]
+        forward_top = a_col * top + b_col * bottom
+        pred_vv = forward_top[:, :points] * a_row + forward_top[:, points:] * b_row
+        pred_vv = jnp.where(first, prior_ref[:points, :points], pred_vv + process_ref[:points, :points])
+        normal_ref[...] = eye + r_col * pred_vv * r_row
+        _sweep_in_place(normal_ref)
         for rows, left_w, right_w in ((slice(0, points), a_col, b_col), (slice(points, None), c_col, d_col)):
             forward = left_w * top + right_w * bottom
             f_left = forward[:, :points]
@@ -118,11 +125,7 @@
             [a_row * m_top + b_row * m_bottom, c_row * m_top + d_row * m_bottom], axis=1
         )
         mean_pred = jnp.where(first, 0.0, mean_fwd)
-        r_col = root_col_ref[t]
-        r_row = root_row_ref[pl.ds(t, 1), :]
         obs_row = obs_ref[pl.ds(t, 1), :]
-        normal_ref[...] = eye + r_col * cov_pred[:points, :points] * r_row
-        _sweep_in_place(normal_ref)
         scaled = r_col * cov_pred[:points, :]
         solved = jnp.dot(normal_ref[...], scaled, precision=HIGHEST, preferred_element_type=jnp.float32)
         correction = lax.dot_general(

time: 186 us -> 186 us (level)
  no operation moved by 1% of the time
where the time goes in v13:
time: 186 us
  waiting for transfers between devices  107 us (58%)
  Pallas kernels  28.5 us (15%)
  blocking collectives  23 us (12%)
  starting transfers between devices  10.5 us (6%)
  matrix products  8.99 us (5%)
  local copies, waits for them, and re-layouts  4.43 us (2%)
  other arithmetic  2.76 us (1%)
    ppermute x7, waiting for transfers between devices, send_element(): recv_gain, recv_packed = lax.ppermute((gain, packed), 'tm', pairs)  107 us
    all_gather x1, blocking collectives, shards(): gathered = lax.all_gather(packed, 'tm', tiled=True)  23 us
    pallas_call x1, Pallas kernels, run_filter(): pl.pallas_call(_filter_kernel, out_shape=(jax.ShapeDtypeStruct((1, width)...  14.5 us
    pallas_call x1, Pallas kernels, neg_inverse(): pl.pallas_call(_sweep_kernel, out_shape=jax.ShapeDtypeStruct((size, size)...  14 us
    ppermute x7, starting transfers between devices, send_element(): recv_gain, recv_packed = lax.ppermute((gain, packed), 'tm', pairs)  10.5 us
    dot_general x18, matrix products, matmul_hi(): return jnp.matmul(left, right, precision=HIGHEST)  8.99 us
  transfers between devices with their start and end apart: 7, of which 7 were waited for; matrix products, arithmetic and copies ran while one was open for 2% of the time, Pallas kernels for 0%

profile of v13, /device:TPU:1, one launch (start us, length us, event | category | flops | bytes accessed | tf_op | source)
XLA Modules:
  0.0 185.9 jit_solution(5650950630211868334)
XLA Ops:
  0.6 0.6 copy-done.2
  1.3 0.6 fusion.24
  1.9 0.9 copy.22.trans_col_ref
  2.8 0.7 copy-done.3
  3.5 23.0 %all_gather.3 = f32[16,2,128]{2,1,0:T(2,128)S(1)} all-gather(f32[1,2,128]{2,1,0:T(2,128)S(1)} %pad_maximum_fusion.8), channel_id=1, replica_groups=mesh['groups'=2,'tm'=16] {'tm'}, dimensions={0}, use_global_device_ids=true | all-gather | bytes 17408 | tf_op jit(solution)/shard_map/all_gather | solution.py:286
  26.4 0.6 fusion.26
  27.0 1.4 copy.21.root_col_ref
  28.4 0.1 multiply_multiply_fusion.1
  28.5 0.7 select_maximum_fusion
  29.3 14.5 %shard_map.68 = (f32[1,256]{1,0:T(1,128)S(1)}, f32[256,256]{1,0:T(8,128)S(1)}) custom-call(s32[1]{0:T(128)} %bitcast.16.count_ref, f32[16,128]{1,0:T(8,128)} %bitcast.125, f32[16,128]{1,0:T(8,128)} %bitcast.124, f32[16,128,1]{2,1,0:T(8,128)} %copy.21.root_col_ref, f32[4,128]{1,0:T(4,128)} %get-tuple-element.81.trans_row_ref, ...), custom_call_target="tpu_custom_call" | custom-call | tf_op jit(solution)/shard_map/pallas_call | solution.py:147
  43.8 17.7 %conditional.1 = (f32[1,256]{1,0:T(1,128)S(1)}, f32[256,256]{1,0:T(8,128)S(1)}, f32[256,256]{1,0:T(8,128)S(1)}) conditional(s32[]{:T(128)} %convert_element_type.12, (f32[128]{0:T(128)S(1)}, f32[1,256,256]{2,1,0:T(8,128)S(1)}, f32[128]{0:T(128)S(1)}, f32[128]{0:T(128)S(1)}, f32[128]{0:T(128)S(1)}, /*index=5*/f32[256,256]{1,0:T(8,128)S(1)}, s32[]{:T(128)}, ...), branch_computations={%region_0.1_spmd, %region_1.2_spmd} | conditional | flops 404358400 | bytes 5516342 | solution.py:331
  44.0 0.1 multiply_add_fusion.1
  44.2 0.1 copy.23
  44.4 0.1 add_bitcast_fusion.1
  44.5 0.7 maximum_add_fusion.a_ref
  45.2 14.0 %vmap__.2 = f32[256,256]{1,0:T(8,128)} custom-call(f32[256,256]{1,0:T(8,128)} %maximum_add_fusion.a_ref), custom_call_target="tpu_custom_call" | custom-call | tf_op jit(solution)/shard_map/cond/branch_0_fun/vmap()/pallas_call | solution.py:83
  59.2 1.5 fusion
  60.7 0.5 fusion.2
  61.2 0.3 convolution_subtract_fusion
  61.6 1.9 %collective-permute-start.3 = (f32[264,256]{1,0:T(8,128)S(1)}, f32[264,256]{1,0:T(8,128)S(1)}, u32[]{:S(2)}, u32[]{:S(2)}) collective-permute-start(f32[264,256]{1,0:T(8,128)S(1)} %pad_maximum_fusion.3), channel_id=1, source_target_pairs={{1,0},{2,1},{3,2},{4,3},{5,4},{6,5},{7,6},{8,7},{9,8},{10,9},{11,1... | collective-permute-start | bytes 811016 | tf_op jit(solution)/shard_map/ppermute | solution.py:272
  63.5 1.9 %collective-permute-start = (f32[256,256]{1,0:T(8,128)S(1)}, f32[256,256]{1,0:T(8,128)S(1)}, u32[]{:S(2)}, u32[]{:S(2)}) collective-permute-start(f32[256,256]{1,0:T(8,128)S(1)} %get-tuple-element.60), channel_id=1, source_target_pairs={{1,0},{2,1},{3,2},{4,3},{5,4},{6,5},{7,6},{8,7},{9,8},{10,9},{11,1... | collective-permute-start | bytes 786440 | tf_op jit(solution)/shard_map/ppermute | solution.py:272
  65.5 6.3 %collective-permute-done.3 = f32[264,256]{1,0:T(8,128)S(1)} collective-permute-done((f32[264,256]{1,0:T(8,128)S(1)}, f32[264,256]{1,0:T(8,128)S(1)}, u32[]{:S(2)}, u32[]{:S(2)}) %collective-permute-start.3) | collective-permute-done | bytes 270368 | tf_op jit(solution)/shard_map/ppermute | solution.py:272
  71.8 0.4 fusion.20
  72.2 0.4 convolution_add_fusion.3
  72.6 0.3 convolution_add_fusion.7
  73.0 1.5 collective-permute-start.4
  74.5 0.1 collective-permute-done
  74.6 0.4 fusion.27
  75.0 1.3 collective-permute-start.1
  76.3 17.6 %collective-permute-done.4 = f32[264,256]{1,0:T(8,128)S(1)} collective-permute-done((f32[264,256]{1,0:T(8,128)S(1)}, f32[264,256]{1,0:T(8,128)S(1)}, u32[]{:S(2)}, u32[]{:S(2)}) %collective-permute-start.4) | collective-permute-done | bytes 270368 | tf_op jit(solution)/shard_map/ppermute | solution.py:272
  93.9 0.4 fusion.18
  94.3 0.4 convolution_add_fusion.2
  94.7 0.3 convolution_add_fusion.6
  95.1 1.3 collective-permute-start.5
  96.4 0.3 collective-permute-done.1
  96.7 0.4 fusion.28
  97.1 1.3 collective-permute-start.2
  98.4 27.1 %collective-permute-done.5 = f32[264,256]{1,0:T(8,128)S(1)} collective-permute-done((f32[264,256]{1,0:T(8,128)S(1)}, f32[264,256]{1,0:T(8,128)S(1)}, u32[]{:S(2)}, u32[]{:S(2)}) %collective-permute-start.5) | collective-permute-done | bytes 270368 | tf_op jit(solution)/shard_map/ppermute | solution.py:272
  125.5 0.4 fusion.16
  125.9 0.4 convolution_add_fusion.1
  126.3 0.3 convolution_add_fusion.5
  126.7 1.3 collective-permute-start.6
  128.0 0.3 collective-permute-done.2
  128.3 0.4 fusion.29
  128.7 54.9 %collective-permute-done.6 = f32[264,256]{1,0:T(8,128)S(1)} collective-permute-done((f32[264,256]{1,0:T(8,128)S(1)}, f32[264,256]{1,0:T(8,128)S(1)}, u32[]{:S(2)}, u32[]{:S(2)}) %collective-permute-start.6) | collective-permute-done | bytes 270368 | tf_op jit(solution)/shard_map/ppermute | solution.py:272
  183.5 0.4 fusion.14
  183.9 1.1 fusion.13
  185.0 0.9 convolution_add_fusion.4
  (25 shorter events, 0.5 us)
Async XLA Ops:
  0.6 0.7 copy-start.2
  1.9 0.9 copy-start.4
  1.9 0.9 copy-start.5
  2.8 0.7 copy-start.3
  27.0 1.4 copy-start.1
  27.0 1.4 copy-start
  61.6 10.2 %collective-permute-start.3 = (f32[264,256]{1,0:T(8,128)S(1)}, f32[264,256]{1,0:T(8,128)S(1)}, u32[]{:S(2)}, u32[]{:S(2)}) collective-permute-start(f32[264,256]{1,0:T(8,128)S(1)} %pad_maximum_fusion.3), channel_id=1, source_target_pairs={{1,0},{2,1},{3,2},{4,3},{5,4},{6,5},{7,6},{8,7},{9,8},{10,9},{11,1... | collective-permute-start | bytes 811016 | tf_op jit(solution)/shard_map/ppermute | solution.py:272
  63.5 11.1 %collective-permute-start = (f32[256,256]{1,0:T(8,128)S(1)}, f32[256,256]{1,0:T(8,128)S(1)}, u32[]{:S(2)}, u32[]{:S(2)}) collective-permute-start(f32[256,256]{1,0:T(8,128)S(1)} %get-tuple-element.60), channel_id=1, source_target_pairs={{1,0},{2,1},{3,2},{4,3},{5,4},{6,5},{7,6},{8,7},{9,8},{10,9},{11,1... | collective-permute-start | bytes 786440 | tf_op jit(solution)/shard_map/ppermute | solution.py:272
  73.0 21.0 %collective-permute-start.4 = (f32[264,256]{1,0:T(8,128)S(1)}, f32[264,256]{1,0:T(8,128)S(1)}, u32[]{:S(2)}, u32[]{:S(2)}) collective-permute-start(f32[264,256]{1,0:T(8,128)S(1)} %pad_maximum_fusion.4), channel_id=1, source_target_pairs={{2,0},{3,1},{4,2},{5,3},{6,4},{7,5},{8,6},{9,7},{10,8},{11,9},{12,... | collective-permute-start | bytes 811016 | tf_op jit(solution)/shard_map/ppermute | solution.py:272
  75.0 21.8 %collective-permute-start.1 = (f32[256,256]{1,0:T(8,128)S(1)}, f32[256,256]{1,0:T(8,128)S(1)}, u32[]{:S(2)}, u32[]{:S(2)}) collective-permute-start(f32[256,256]{1,0:T(8,128)S(1)} %fusion.27), channel_id=1, source_target_pairs={{2,0},{3,1},{4,2},{5,3},{6,4},{7,5},{8,6},{9,7},{10,8},{11,9},{12,... | collective-permute-start | bytes 786440 | tf_op jit(solution)/shard_map/ppermute | solution.py:272
  95.1 30.4 %collective-permute-start.5 = (f32[264,256]{1,0:T(8,128)S(1)}, f32[264,256]{1,0:T(8,128)S(1)}, u32[]{:S(2)}, u32[]{:S(2)}) collective-permute-start(f32[264,256]{1,0:T(8,128)S(1)} %pad_maximum_fusion.5), channel_id=1, source_target_pairs={{4,0},{5,1},{6,2},{7,3},{8,4},{9,5},{10,6},{11,7},{12,8},{13,9},{1... | collective-permute-start | bytes 811016 | tf_op jit(solution)/shard_map/ppermute | solution.py:272
  97.1 31.2 %collective-permute-start.2 = (f32[256,256]{1,0:T(8,128)S(1)}, f32[256,256]{1,0:T(8,128)S(1)}, u32[]{:S(2)}, u32[]{:S(2)}) collective-permute-start(f32[256,256]{1,0:T(8,128)S(1)} %fusion.28), channel_id=1, source_target_pairs={{4,0},{5,1},{6,2},{7,3},{8,4},{9,5},{10,6},{11,7},{12,8},{13,9},{1... | collective-permute-start | bytes 786440 | tf_op jit(solution)/shard_map/ppermute | solution.py:272
  126.7 56.9 %collective-permute-start.6 = (f32[264,256]{1,0:T(8,128)S(1)}, f32[264,256]{1,0:T(8,128)S(1)}, u32[]{:S(2)}, u32[]{:S(2)}) collective-permute-start(f32[264,256]{1,0:T(8,128)S(1)} %pad_maximum_fusion.6), channel_id=1, source_target_pairs={{8,0},{9,1},{10,2},{11,3},{12,4},{13,5},{14,6},{15,7},{24,16},{25,... | collective-permute-start | bytes 811016 | tf_op jit(solution)/shard_map/ppermute | solution.py:272
